TPU v7x, 256 devices: a whole 4x4x8 slice. The times are simulated.
256 devices in a mesh: axial: 16 (over x_lo, y, core), azim: 16 (over z, x_hi).
Axes of the slice: x: 4 (x_hi: 2, x_lo: 2; x = x_hi * 2 + x_lo), y: 4, z: 8, core: 2. Of those that a mesh axis runs over, the one named last changes fastest.
Arguments:
- coil_density: float32 [512, 256, 128], P('azim', 'axial'), may hold values from -6 to 6
- coil_mask: int32 [512, 256, 128], P('azim', 'axial'), may hold values 0 or 1
- drive: float32 [2], replicated, may hold values from 0.5 to 2
- potential: float32 [512, 256, 128], P('azim', 'axial'), may hold values from -6 to 6
- tile_weight: float32 [512, 64, 64], P('azim'), may hold values from -0.75 to 0.75
- relay_owner: int32 [2, 512, 16], P(None, 'azim', 'axial'), may hold values from 0 to 2
- relay_slot: int32 [2, 512, 16], P(None, 'azim', 'axial'), may hold values from 0 to 31, as said below
- velocity: float32 [512, 256, 128], P('azim', 'axial'), may hold values from -3 to 3
- strain: float32 [512, 256, 128], P('azim', 'axial'), may hold values from -3 to 3
- plastic: float32 [512, 256, 128], P('azim', 'axial'), may hold values from -0.6 to 0.6
Outputs:
- field_out: float32 [512, 256, 128], P('azim', 'axial')
- velocity_out: float32 [512, 256, 128], P('azim', 'axial')
- strain_out: float32 [512, 256, 128], P('azim', 'axial')
- plastic_out: float32 [512, 256, 128], P('azim', 'axial')
Inputs may be any that keep to these rules, and one draw needn't show every extreme that they name: `relay_slot`: for each step and axial block, the values over the 32 azimuthal cells of one sector are a permutation of 0 to 31.
All inputs are finite; a program needn't handle non-finite values. No bound on the sum of `coil_mask` on one device may be relied on, other than what follows from the above.
Results may differ from a plain program's by a relative error of at most 0.00011.
Values sent between devices are 32-bit elements; how exact they have to be, the bound alone decides.
No kernel may reach another device: no remote copies, remote signals or barrier semaphores. Data moves between devices by JAX's collectives and lax.ppermute only.
A program may use at most 64 MiB of HBM per device.

v0:
```python
import math

import jax
import jax.numpy as jnp
from jax import lax
from jax.sharding import PartitionSpec as P

STEPS = 2
SWEEPS = 3


HIGH = lax.Precision.HIGHEST
KAPPA = 2.0
AIR_TERM = 0.05
R_CORE = 16.0
MU_COIL = 1.0
FORCE_K = 1.0
E_MOD = 1.0
YIELD_ZERO = 0.5
HARDEN = 0.3
TIME_STEP = 0.5
STIFFNESS = 0.5
DAMPING = 0.9


def with_halo(block, sides, width):
    for axis, dim in sides:
        count = lax.axis_size(axis)
        forward = [(i, i + 1) for i in range(count - 1)]
        backward = [(target, source) for source, target in forward]
        low = lax.ppermute(
            lax.slice_in_dim(block, block.shape[dim] - width, None, axis=dim), axis, forward
        )
        high = lax.ppermute(lax.slice_in_dim(block, 0, width, axis=dim), axis, backward)
        block = jnp.concatenate([low, block, high], axis=dim)
    return block


def shifted(array, axis, by):
    devices = lax.axis_size(axis)
    pairs = [(i, i + by) for i in range(devices) if 0 <= i + by < devices]
    return lax.ppermute(array, axis, pairs)


def harmonic_table(azimuth, harmonic, count_all):
    half_count = count_all // 2
    orders = jnp.where(harmonic <= half_count, harmonic, harmonic - half_count)
    phases = azimuth[:, None] * orders[None, :] % count_all
    angles = phases.astype(jnp.float32) * (2.0 * math.pi / count_all)
    return jnp.where(harmonic[None, :] <= half_count, jnp.cos(angles), jnp.sin(angles))


def harmonic_weight(harmonic, count_all):
    half_count = count_all // 2
    edge_mode = (harmonic == 0) | (harmonic == half_count)
    return jnp.where(edge_mode, 1.0 / count_all, 2.0 / count_all).astype(jnp.float32)


def harmonic_order(harmonic, count_all):
    half_count = count_all // 2
    return jnp.where(harmonic <= half_count, harmonic, harmonic - half_count).astype(jnp.float32)


def radial_profiles(radial_count, band_start, band_width):
    cell_index = jnp.arange(radial_count, dtype=jnp.int32)
    radius = R_CORE + cell_index.astype(jnp.float32)
    inside = (cell_index >= band_start) & (cell_index < band_start + band_width)
    conduct = jnp.where(inside, KAPPA, AIR_TERM).astype(jnp.float32)
    coil_zone = (cell_index < band_start).astype(jnp.float32)
    return (radius, conduct, coil_zone)


def radial_sum(iterate):
    radial_pad = jnp.pad(iterate, ((0, 0), (0, 0), (1, 1)))
    return radial_pad[:, :, 2:] + radial_pad[:, :, :-2]


def lorentz(padded, previous, conduct, radius, band_start, band_width):
    current_field = padded[:, 1:-1]
    axial_slope = (padded[:, 2:] - padded[:, :-2]) * 0.5
    radial_pad = jnp.pad(current_field, ((0, 0), (0, 0), (1, 1)))
    radial_slope = (radial_pad[:, :, 2:] - radial_pad[:, :, :-2]) * 0.5
    b_axial = radial_slope + current_field / radius
    eddy_current = -conduct * (current_field - previous)
    force_radial = FORCE_K * eddy_current * b_axial
    force_axial = FORCE_K * eddy_current * axial_slope
    return jnp.concatenate(
        [
            force_radial[..., band_start : band_start + band_width],
            force_axial[..., band_start : band_start + band_width],
        ],
        axis=-1,
    )


def plastic_update(load, velocity, strain, plastic):
    trial_stress = E_MOD * (strain - plastic)
    excess = jnp.abs(trial_stress) - YIELD_ZERO
    increment = (
        trial_stress
        * jnp.maximum(excess, 0.0)
        / ((E_MOD + HARDEN) * jnp.maximum(jnp.abs(trial_stress), YIELD_ZERO))
    )
    plastic = plastic + increment
    stress = E_MOD * (strain - plastic)
    velocity = DAMPING * velocity + TIME_STEP * (load - STIFFNESS * stress)
    strain = strain + TIME_STEP * velocity
    return (velocity, strain, plastic)


def transform(parts, table_rows, all_index):
    flat_shape = parts.shape
    columns_all = parts.reshape(flat_shape[0], -1)
    spread = lax.all_to_all(columns_all, "azim", split_axis=1, concat_axis=0, tiled=True)
    full_table = table_rows(all_index, all_index)
    mixed = jnp.dot(full_table.T, spread, precision=HIGH, preferred_element_type=jnp.float32)
    joined = lax.all_to_all(mixed, "azim", split_axis=0, concat_axis=1, tiled=True)
    return joined.reshape(flat_shape)


def shards(
    coil_density,
    coil_mask,
    drive,
    potential,
    tile_weight,
    relay_owner,
    relay_slot,
    velocity,
    strain,
    plastic,
):
    local_count = potential.shape[0]
    axial_cells = potential.shape[1]
    radial_cells = potential.shape[2]
    band_width = tile_weight.shape[1]
    azim_total = local_count * lax.axis_size("azim")
    own_index = lax.axis_index("azim") * local_count + jnp.arange(local_count, dtype=jnp.int32)
    all_index = jnp.arange(azim_total, dtype=jnp.int32)
    band_start = radial_cells // 4
    radius, conduct, coil_zone = radial_profiles(radial_cells, band_start, band_width)
    orders = harmonic_order(own_index, azim_total)
    diagonal_term = (
        4.0 + conduct[None, None, :] + (orders[:, None, None] / radius[None, None, :]) ** 2
    )

    def forward_rows(rows_in, rows_out):
        return harmonic_table(rows_in, rows_out, azim_total)

    def inverse_rows(rows_in, rows_out):
        return (
            harmonic_table(rows_out, rows_in, azim_total).T
            * harmonic_weight(rows_in, azim_total)[:, None]
        )

    slot_range = jnp.arange(local_count, dtype=jnp.int32)
    field = potential
    for step_index in range(STEPS):
        source = drive[step_index] * coil_density * coil_mask.astype(jnp.float32) * coil_zone
        stacked = jnp.stack([source, field], axis=1)
        modes = transform(stacked, forward_rows, all_index)
        right_side = MU_COIL * modes[:, 0] + conduct * modes[:, 1]
        iterate = modes[:, 1]
        for sweep_index in range(SWEEPS):
            axial_pad = with_halo(iterate, (("axial", 1),), 1)
            nearby = axial_pad[:, 2:] + axial_pad[:, :-2] + radial_sum(iterate)
            iterate = (right_side + nearby) / diagonal_term
        new_field = transform(iterate[:, None], inverse_rows, all_index)[:, 0]
        padded = with_halo(new_field, (("axial", 1),), 1)
        tiles = lorentz(padded, field, conduct, radius, band_start, band_width)
        slot_table = (relay_slot[step_index, :, 0][:, None] == slot_range[None, :]).astype(
            jnp.float32
        )
        owner_now = relay_owner[step_index, :, 0]

        def place(target):
            chosen = (owner_now == target).astype(jnp.float32)
            return jnp.einsum(
                "jcw,jp->pcw", tiles * chosen[:, None, None], slot_table, precision=HIGH
            )

        from_below = shifted(place(2), "axial", 1)
        from_above = shifted(place(0), "axial", -1)
        received = (place(1) + from_below + from_above).reshape(
            local_count, axial_cells, 2, band_width
        )
        load = jnp.einsum("aqr,azcr->azcq", tile_weight, received, precision=HIGH).reshape(
            local_count, axial_cells, 2 * band_width
        )
        velocity, strain, plastic = plastic_update(load, velocity, strain, plastic)
        field = new_field
    return (field, velocity, strain, plastic)


def solution(mesh):
    placed = (
        P("azim", "axial", None),
        P("azim", "axial", None),
        P(),
        P("azim", "axial", None),
        P("azim", None, None),
        P(None, "azim", "axial"),
        P(None, "azim", "axial"),
        P("azim", "axial", None),
        P("azim", "axial", None),
        P("azim", "axial", None),
    )
    return jax.shard_map(
        shards,
        mesh=mesh,
        in_specs=placed,
        out_specs=(
            P("azim", "axial", None),
            P("azim", "axial", None),
            P("azim", "axial", None),
            P("azim", "axial", None),
        ),
        check_vma=False,
    )
```

profile of v0, /device:TPU:2, one launch (start us, length us, event | category | flops | bytes accessed | tf_op | source)
XLA Modules:
  0.0 289.7 jit_solution(16157686865284336224)
XLA Ops:
  0.7 0.7 copy-done.5
  1.4 0.6 fusion.134
  2.0 2.6 multiply_bitcast_fusion.1
  5.1 1.1 copy.68
  6.2 10.1 %all-to-all-start = ((f32[32,16,256]{2,0,1:T(8,128)}), f32[32,16,256]{2,0,1:T(8,128)S(1)}, u32[]{:S(2)}, u32[]{:S(2)}) async-start(f32[32,16,256]{2,0,1:T(8,128)} %copy.68), calls=%async_computation | async-start | bytes 1048576 | tf_op jit(solution)/shard_map/all_to_all | solution.py:114
  16.4 18.8 %all-to-all-done = f32[32,16,256]{2,0,1:T(8,128)S(1)} async-done(((f32[32,16,256]{2,0,1:T(8,128)}), f32[32,16,256]{2,0,1:T(8,128)S(1)}, u32[]{:S(2)}, u32[]{:S(2)}) %all-to-all-start) | async-done | bytes 524320 | tf_op jit(solution)/shard_map/all_to_all | solution.py:114
  35.2 8.6 %fusion.14 = f32[16,32,256]{2,1,0:T(8,128)} fusion(f32[512,256,1]{1,0,2:T(8,128)S(1)} %bitcast.139, s32[16,32]{1,0:T(8,128)S(1)} %add_select_fusion.2, pred[16,32]{1,0:T(8,128)(4,1)S(1)} %fusion.99), kind=kOutput, calls=%fused_computation.24 | convolution fusion | flops 809238528 | bytes 1051136 | tf_op jit(solution)/shard_map/dot_general | solution.py:116
  43.8 3.6 %all-to-all-start.1 = ((f32[16,32,256]{2,1,0:T(8,128)}), f32[16,32,256]{2,1,0:T(8,128)S(1)}, u32[]{:S(2)}, u32[]{:S(2)}) async-start(f32[16,32,256]{2,1,0:T(8,128)} %fusion.14), calls=%async_computation.1 | async-start | bytes 1048576 | tf_op jit(solution)/shard_map/all_to_all | solution.py:117
  47.5 18.2 %all-to-all-done.1 = f32[16,32,256]{2,1,0:T(8,128)S(1)} async-done(((f32[16,32,256]{2,1,0:T(8,128)}), f32[16,32,256]{2,1,0:T(8,128)S(1)}, u32[]{:S(2)}, u32[]{:S(2)}) %all-to-all-start.1) | async-done | bytes 524320 | tf_op jit(solution)/shard_map/all_to_all | solution.py:117
  66.1 3.6 %collective-permute-start = (f32[32,1,128]{2,1,0:T(1,128)S(1)}, f32[32,1,128]{2,1,0:T(1,128)S(1)}, u32[]{:S(2)}, u32[]{:S(2)}) collective-permute-start(f32[32,1,128]{2,1,0:T(1,128)S(1)} %get-tuple-element.45), channel_id=1, source_target_pairs={{16,0},{32,16},{48,32},{64,48},{80,64},{96,80},{112,96},{128,112},... | collective-permute-start | bytes 49160 | tf_op jit(solution)/shard_map/ppermute | solution.py:34
  69.6 1.9 collective-permute-start.1
  71.6 5.2 %collective-permute-done.1 = f32[32,1,128]{2,1,0:T(1,128)S(1)} collective-permute-done((f32[32,1,128]{2,1,0:T(1,128)S(1)}, f32[32,1,128]{2,1,0:T(1,128)S(1)}, u32[]{:S(2)}, u32[]{:S(2)}) %collective-permute-start.1) | collective-permute-done | bytes 16416 | tf_op jit(solution)/shard_map/ppermute | solution.py:31
  77.1 1.9 collective-permute-start.2
  79.0 2.4 collective-permute-start.3
  81.4 4.7 %collective-permute-done.3 = f32[32,1,128]{2,1,0:T(1,128)S(1)} collective-permute-done((f32[32,1,128]{2,1,0:T(1,128)S(1)}, f32[32,1,128]{2,1,0:T(1,128)S(1)}, u32[]{:S(2)}, u32[]{:S(2)}) %collective-permute-start.3) | collective-permute-done | bytes 16416 | tf_op jit(solution)/shard_map/ppermute | solution.py:31
  86.4 1.9 collective-permute-start.4
  88.3 2.4 collective-permute-start.5
  90.8 4.7 %collective-permute-done.5 = f32[32,1,128]{2,1,0:T(1,128)S(1)} collective-permute-done((f32[32,1,128]{2,1,0:T(1,128)S(1)}, f32[32,1,128]{2,1,0:T(1,128)S(1)}, u32[]{:S(2)}, u32[]{:S(2)}) %collective-permute-start.5) | collective-permute-done | bytes 16416 | tf_op jit(solution)/shard_map/ppermute | solution.py:31
  95.7 0.8 copy.71
  96.5 4.4 %all-to-all-start.2 = ((f32[32,16,128]{2,0,1:T(8,128)}), f32[32,16,128]{2,0,1:T(8,128)S(1)}, u32[]{:S(2)}, u32[]{:S(2)}) async-start(f32[32,16,128]{2,0,1:T(8,128)} %copy.71), calls=%async_computation.2 | async-start | bytes 524288 | tf_op jit(solution)/shard_map/all_to_all | solution.py:114
  101.0 12.2 %all-to-all-done.2 = f32[32,16,128]{2,0,1:T(8,128)S(1)} async-done(((f32[32,16,128]{2,0,1:T(8,128)}), f32[32,16,128]{2,0,1:T(8,128)S(1)}, u32[]{:S(2)}, u32[]{:S(2)}) %all-to-all-start.2) | async-done | bytes 262176 | tf_op jit(solution)/shard_map/all_to_all | solution.py:114
  113.2 5.1 %fusion.22 = f32[16,32,128]{2,1,0:T(8,128)S(1)} fusion(f32[512,128,1]{1,0,2:T(8,128)S(1)} %bitcast.142, f32[512]{0:T(512)S(1)} %fusion.101, s32[512]{0:T(512)S(1)} %add_select_fusion.3, s32[16,32]{1,0:T(8,128)S(1)} %multiply_add_fusion.3, pred[512]{0:T(512)(128)(4,1)S(1)} %iota_compare_fusion.4), kind=kOutput, calls=%fused_computation.52 | convolution fusion | flops 406847488 | bytes 530944 | tf_op jit(solution)/shard_map/dot_general | solution.py:116
  118.4 15.2 %all_to_all.122 = f32[16,32,128]{2,1,0:T(8,128)S(1)} all-to-all(f32[16,32,128]{2,1,0:T(8,128)S(1)} %fusion.22), channel_id=1, replica_groups=mesh['axial'=16,'azim'=16] {'azim'}, dimensions={0} | all-to-all | bytes 524288 | tf_op jit(solution)/shard_map/all_to_all | solution.py:117
  134.4 17.8 %all_to_all.123 = f32[32,16,256]{2,0,1:T(8,128)S(1)} all-to-all(f32[32,16,256]{2,0,1:T(8,128)S(1)} %copy.73), channel_id=1, replica_groups=mesh['axial'=16,'azim'=16] {'azim'}, dimensions={1} | all-to-all | bytes 1048576 | tf_op jit(solution)/shard_map/all_to_all | solution.py:114
  152.2 8.0 %fusion.12 = f32[16,32,256]{2,1,0:T(8,128)S(1)} fusion(f32[512,256,1]{1,0,2:T(8,128)S(1)} %bitcast.140, s32[16,32]{1,0:T(8,128)S(1)} %add_select_fusion.2, pred[16,32]{1,0:T(8,128)(4,1)S(1)} %fusion.99), kind=kOutput, calls=%fused_computation.22 | convolution fusion | flops 809238528 | bytes 1051136 | tf_op jit(solution)/shard_map/dot_general | solution.py:116
  160.2 17.1 %all_to_all.124 = f32[16,32,256]{2,1,0:T(8,128)S(1)} all-to-all(f32[16,32,256]{2,1,0:T(8,128)S(1)} %fusion.12), channel_id=1, replica_groups=mesh['axial'=16,'azim'=16] {'azim'}, dimensions={0} | all-to-all | bytes 1048576 | tf_op jit(solution)/shard_map/all_to_all | solution.py:117
  177.7 6.7 %collective-permute-start.6 = (f32[32,1,128]{2,1,0:T(1,128)S(1)}, f32[32,1,128]{2,1,0:T(1,128)S(1)}, u32[]{:S(2)}, u32[]{:S(2)}) collective-permute-start(f32[32,1,128]{2,1,0:T(1,128)S(1)} %get-tuple-element.39), channel_id=1, source_target_pairs={{16,0},{32,16},{48,32},{64,48},{80,64},{96,80},{112,96},{128,112},... | collective-permute-start | bytes 49160 | tf_op jit(solution)/shard_map/ppermute | solution.py:34
  184.4 1.9 collective-permute-start.7
  186.3 5.2 %collective-permute-done.7 = f32[32,1,128]{2,1,0:T(1,128)S(1)} collective-permute-done((f32[32,1,128]{2,1,0:T(1,128)S(1)}, f32[32,1,128]{2,1,0:T(1,128)S(1)}, u32[]{:S(2)}, u32[]{:S(2)}) %collective-permute-start.7) | collective-permute-done | bytes 16416 | tf_op jit(solution)/shard_map/ppermute | solution.py:31
  191.8 1.9 collective-permute-start.8
  193.8 2.4 collective-permute-start.9
  196.2 4.7 %collective-permute-done.9 = f32[32,1,128]{2,1,0:T(1,128)S(1)} collective-permute-done((f32[32,1,128]{2,1,0:T(1,128)S(1)}, f32[32,1,128]{2,1,0:T(1,128)S(1)}, u32[]{:S(2)}, u32[]{:S(2)}) %collective-permute-start.9) | collective-permute-done | bytes 16416 | tf_op jit(solution)/shard_map/ppermute | solution.py:31
  201.2 1.9 collective-permute-start.10
  203.1 2.4 collective-permute-start.11
  205.5 4.7 %collective-permute-done.11 = f32[32,1,128]{2,1,0:T(1,128)S(1)} collective-permute-done((f32[32,1,128]{2,1,0:T(1,128)S(1)}, f32[32,1,128]{2,1,0:T(1,128)S(1)}, u32[]{:S(2)}, u32[]{:S(2)}) %collective-permute-start.11) | collective-permute-done | bytes 16416 | tf_op jit(solution)/shard_map/ppermute | solution.py:31
  210.5 0.8 copy.77
  211.3 4.5 %all-to-all-start.6 = ((f32[32,16,128]{2,0,1:T(8,128)}), f32[32,16,128]{2,0,1:T(8,128)S(1)}, u32[]{:S(2)}, u32[]{:S(2)}) async-start(f32[32,16,128]{2,0,1:T(8,128)} %copy.77), calls=%async_computation.6 | async-start | bytes 524288 | tf_op jit(solution)/shard_map/all_to_all | solution.py:114
  215.8 12.2 %all-to-all-done.6 = f32[32,16,128]{2,0,1:T(8,128)S(1)} async-done(((f32[32,16,128]{2,0,1:T(8,128)}), f32[32,16,128]{2,0,1:T(8,128)S(1)}, u32[]{:S(2)}, u32[]{:S(2)}) %all-to-all-start.6) | async-done | bytes 262176 | tf_op jit(solution)/shard_map/all_to_all | solution.py:114
  228.1 6.8 %fusion.21 = f32[16,32,128]{2,1,0:T(8,128)} fusion(f32[512,128,1]{1,0,2:T(8,128)S(1)} %bitcast.141, f32[512]{0:T(512)S(1)} %fusion.101, s32[512]{0:T(512)S(1)} %add_select_fusion.3, s32[16,32]{1,0:T(8,128)S(1)} %multiply_add_fusion.3, pred[512]{0:T(512)(128)(4,1)S(1)} %iota_compare_fusion.4), kind=kOutput, calls=%fused_computation.51 | convolution fusion | flops 406847488 | bytes 530944 | tf_op jit(solution)/shard_map/dot_general | solution.py:116
  234.9 3.7 %all-to-all-start.7 = ((f32[16,32,128]{2,1,0:T(8,128)}), f32[16,32,128]{2,1,0:T(8,128)S(1)}, u32[]{:S(2)}, u32[]{:S(2)}) async-start(f32[16,32,128]{2,1,0:T(8,128)} %fusion.21), calls=%async_computation.7 | async-start | bytes 524288 | tf_op jit(solution)/shard_map/all_to_all | solution.py:117
  238.6 1.9 collective-permute-start.12
  240.6 2.5 collective-permute-start.13
  243.3 7.8 %all-to-all-done.7 = f32[16,32,128]{2,1,0:T(8,128)S(1)} async-done(((f32[16,32,128]{2,1,0:T(8,128)}), f32[16,32,128]{2,1,0:T(8,128)S(1)}, u32[]{:S(2)}, u32[]{:S(2)}) %all-to-all-start.7) | async-done | bytes 262176 | tf_op jit(solution)/shard_map/all_to_all | solution.py:117
  251.1 1.9 collective-permute-start.16
  253.0 2.4 collective-permute-start.17
  255.8 0.9 copy.89
  256.6 3.5 %collective-permute-done.17 = f32[32,1,128]{2,0,1:T(8,128)S(1)} collective-permute-done((f32[32,1,128]{2,0,1:T(8,128)S(1)}, f32[32,1,128]{2,0,1:T(8,128)S(1)}, u32[]{:S(2)}, u32[]{:S(2)}) %collective-permute-start.17) | collective-permute-done | bytes 16416 | tf_op jit(solution)/shard_map/ppermute | solution.py:31
  260.2 0.9 fusion.51
  261.0 0.4 fusion.70
  261.4 1.9 collective-permute-start.18
  263.3 0.4 fusion.68
  263.7 5.8 %collective-permute-start.19 = (f32[32,16,128]{2,0,1:T(8,128)S(1)}, f32[32,16,128]{2,0,1:T(8,128)S(1)}, u32[]{:S(2)}, u32[]{:S(2)}) collective-permute-start(f32[32,16,128]{2,0,1:T(8,128)S(1)} %fusion.68), channel_id=1, source_target_pairs={{16,0},{32,16},{48,32},{64,48},{80,64},{96,80},{112,96},{128,112},... | collective-permute-start | bytes 786440 | tf_op jit(solution)/shard_map/ppermute | solution.py:42
  269.8 1.9 collective-permute-start.14
  272.1 6.0 %collective-permute-start.15 = (f32[32,16,128]{2,0,1:T(8,128)S(1)}, f32[32,16,128]{2,0,1:T(8,128)}, u32[]{:S(2)}, u32[]{:S(2)}) collective-permute-start(f32[32,16,128]{2,0,1:T(8,128)S(1)} %fusion.73), channel_id=1, source_target_pairs={{16,0},{32,16},{48,32},{64,48},{80,64},{96,80},{112,96},{128,112},... | collective-permute-start | bytes 786440 | tf_op jit(solution)/shard_map/ppermute | solution.py:42
  278.1 0.4 fusion
  278.8 1.9 fusion.8
  281.3 0.4 collective-permute-done.15
  281.7 1.3 fusion.1
  283.4 1.9 fusion.10
  285.9 0.6 copy-done.2
  286.7 0.4 multiply_add_fusion
  287.1 0.9 copy.90
  288.0 0.9 copy.91
  288.8 0.9 copy.92
  (79 shorter events, 6.9 us)
Async XLA Ops:
  0.6 278.2 %copy-start = (f32[32,64,64]{2,1,0:T(8,128)S(1)}, f32[32,64,64]{2,1,0:T(8,128)}, u32[]{:S(2)}) copy-start(f32[32,64,64]{2,1,0:T(8,128)} %param.14) | copy-start | bytes 1572868
  0.6 0.7 copy-start.5
  6.2 29.0 %all-to-all-start = ((f32[32,16,256]{2,0,1:T(8,128)}), f32[32,16,256]{2,0,1:T(8,128)S(1)}, u32[]{:S(2)}, u32[]{:S(2)}) async-start(f32[32,16,256]{2,0,1:T(8,128)} %copy.68), calls=%async_computation | async-start | bytes 1048576 | tf_op jit(solution)/shard_map/all_to_all | solution.py:114
  43.8 21.8 %all-to-all-start.1 = ((f32[16,32,256]{2,1,0:T(8,128)}), f32[16,32,256]{2,1,0:T(8,128)S(1)}, u32[]{:S(2)}, u32[]{:S(2)}) async-start(f32[16,32,256]{2,1,0:T(8,128)} %fusion.14), calls=%async_computation.1 | async-start | bytes 1048576 | tf_op jit(solution)/shard_map/all_to_all | solution.py:117
  66.1 5.5 %collective-permute-start = (f32[32,1,128]{2,1,0:T(1,128)S(1)}, f32[32,1,128]{2,1,0:T(1,128)S(1)}, u32[]{:S(2)}, u32[]{:S(2)}) collective-permute-start(f32[32,1,128]{2,1,0:T(1,128)S(1)} %get-tuple-element.45), channel_id=1, source_target_pairs={{16,0},{32,16},{48,32},{64,48},{80,64},{96,80},{112,96},{128,112},... | collective-permute-start | bytes 49160 | tf_op jit(solution)/shard_map/ppermute | solution.py:34
  69.6 7.2 %collective-permute-start.1 = (f32[32,1,128]{2,1,0:T(1,128)S(1)}, f32[32,1,128]{2,1,0:T(1,128)S(1)}, u32[]{:S(2)}, u32[]{:S(2)}) collective-permute-start(f32[32,1,128]{2,1,0:T(1,128)S(1)} %get-tuple-element.46), channel_id=1, source_target_pairs={{0,16},{16,32},{32,48},{48,64},{64,80},{80,96},{96,112},{112,128},... | collective-permute-start | bytes 49160 | tf_op jit(solution)/shard_map/ppermute | solution.py:31
  77.1 4.3 %collective-permute-start.2 = (f32[32,1,128]{2,1,0:T(1,128)S(1)}, f32[32,1,128]{2,1,0:T(1,128)S(1)}, u32[]{:S(2)}, u32[]{:S(2)}) collective-permute-start(f32[32,1,128]{2,1,0:T(1,128)S(1)} %get-tuple-element.43), channel_id=1, source_target_pairs={{16,0},{32,16},{48,32},{64,48},{80,64},{96,80},{112,96},{128,112},... | collective-permute-start | bytes 49160 | tf_op jit(solution)/shard_map/ppermute | solution.py:34
  79.0 7.2 %collective-permute-start.3 = (f32[32,1,128]{2,1,0:T(1,128)S(1)}, f32[32,1,128]{2,1,0:T(1,128)S(1)}, u32[]{:S(2)}, u32[]{:S(2)}) collective-permute-start(f32[32,1,128]{2,1,0:T(1,128)S(1)} %get-tuple-element.44), channel_id=1, source_target_pairs={{0,16},{16,32},{32,48},{48,64},{64,80},{80,96},{96,112},{112,128},... | collective-permute-start | bytes 49160 | tf_op jit(solution)/shard_map/ppermute | solution.py:31
  86.4 4.3 %collective-permute-start.4 = (f32[32,1,128]{2,1,0:T(1,128)S(1)}, f32[32,1,128]{2,1,0:T(1,128)S(1)}, u32[]{:S(2)}, u32[]{:S(2)}) collective-permute-start(f32[32,1,128]{2,1,0:T(1,128)S(1)} %get-tuple-element.41), channel_id=1, source_target_pairs={{16,0},{32,16},{48,32},{64,48},{80,64},{96,80},{112,96},{128,112},... | collective-permute-start | bytes 49160 | tf_op jit(solution)/shard_map/ppermute | solution.py:34
  88.3 7.2 %collective-permute-start.5 = (f32[32,1,128]{2,1,0:T(1,128)S(1)}, f32[32,1,128]{2,1,0:T(1,128)S(1)}, u32[]{:S(2)}, u32[]{:S(2)}) collective-permute-start(f32[32,1,128]{2,1,0:T(1,128)S(1)} %get-tuple-element.42), channel_id=1, source_target_pairs={{0,16},{16,32},{32,48},{48,64},{64,80},{80,96},{96,112},{112,128},... | collective-permute-start | bytes 49160 | tf_op jit(solution)/shard_map/ppermute | solution.py:31
  96.5 16.7 %all-to-all-start.2 = ((f32[32,16,128]{2,0,1:T(8,128)}), f32[32,16,128]{2,0,1:T(8,128)S(1)}, u32[]{:S(2)}, u32[]{:S(2)}) async-start(f32[32,16,128]{2,0,1:T(8,128)} %copy.71), calls=%async_computation.2 | async-start | bytes 524288 | tf_op jit(solution)/shard_map/all_to_all | solution.py:114
  177.7 8.6 %collective-permute-start.6 = (f32[32,1,128]{2,1,0:T(1,128)S(1)}, f32[32,1,128]{2,1,0:T(1,128)S(1)}, u32[]{:S(2)}, u32[]{:S(2)}) collective-permute-start(f32[32,1,128]{2,1,0:T(1,128)S(1)} %get-tuple-element.39), channel_id=1, source_target_pairs={{16,0},{32,16},{48,32},{64,48},{80,64},{96,80},{112,96},{128,112},... | collective-permute-start | bytes 49160 | tf_op jit(solution)/shard_map/ppermute | solution.py:34
  184.4 7.2 %collective-permute-start.7 = (f32[32,1,128]{2,1,0:T(1,128)S(1)}, f32[32,1,128]{2,1,0:T(1,128)S(1)}, u32[]{:S(2)}, u32[]{:S(2)}) collective-permute-start(f32[32,1,128]{2,1,0:T(1,128)S(1)} %get-tuple-element.40), channel_id=1, source_target_pairs={{0,16},{16,32},{32,48},{48,64},{64,80},{80,96},{96,112},{112,128},... | collective-permute-start | bytes 49160 | tf_op jit(solution)/shard_map/ppermute | solution.py:31
  191.8 4.3 %collective-permute-start.8 = (f32[32,1,128]{2,1,0:T(1,128)S(1)}, f32[32,1,128]{2,1,0:T(1,128)S(1)}, u32[]{:S(2)}, u32[]{:S(2)}) collective-permute-start(f32[32,1,128]{2,1,0:T(1,128)S(1)} %get-tuple-element.37), channel_id=1, source_target_pairs={{16,0},{32,16},{48,32},{64,48},{80,64},{96,80},{112,96},{128,112},... | collective-permute-start | bytes 49160 | tf_op jit(solution)/shard_map/ppermute | solution.py:34
  193.8 7.2 %collective-permute-start.9 = (f32[32,1,128]{2,1,0:T(1,128)S(1)}, f32[32,1,128]{2,1,0:T(1,128)S(1)}, u32[]{:S(2)}, u32[]{:S(2)}) collective-permute-start(f32[32,1,128]{2,1,0:T(1,128)S(1)} %get-tuple-element.38), channel_id=1, source_target_pairs={{0,16},{16,32},{32,48},{48,64},{64,80},{80,96},{96,112},{112,128},... | collective-permute-start | bytes 49160 | tf_op jit(solution)/shard_map/ppermute | solution.py:31
  201.2 4.3 %collective-permute-start.10 = (f32[32,1,128]{2,1,0:T(1,128)S(1)}, f32[32,1,128]{2,1,0:T(1,128)S(1)}, u32[]{:S(2)}, u32[]{:S(2)}) collective-permute-start(f32[32,1,128]{2,1,0:T(1,128)S(1)} %get-tuple-element.35), channel_id=1, source_target_pairs={{16,0},{32,16},{48,32},{64,48},{80,64},{96,80},{112,96},{128,112},... | collective-permute-start | bytes 49160 | tf_op jit(solution)/shard_map/ppermute | solution.py:34
  203.1 7.2 %collective-permute-start.11 = (f32[32,1,128]{2,1,0:T(1,128)S(1)}, f32[32,1,128]{2,1,0:T(1,128)S(1)}, u32[]{:S(2)}, u32[]{:S(2)}) collective-permute-start(f32[32,1,128]{2,1,0:T(1,128)S(1)} %get-tuple-element.36), channel_id=1, source_target_pairs={{0,16},{16,32},{32,48},{48,64},{64,80},{80,96},{96,112},{112,128},... | collective-permute-start | bytes 49160 | tf_op jit(solution)/shard_map/ppermute | solution.py:31
  211.3 4.5 %copy-start.7 = (s32[2,32,1]{1,2,0:T(1,128)S(1)}, s32[2,32,1]{1,2,0:T(1,128)}, u32[]{:S(2)}) copy-start(s32[2,32,1]{1,2,0:T(1,128)} %param.15) | copy-start | bytes 772
  211.3 16.8 %all-to-all-start.6 = ((f32[32,16,128]{2,0,1:T(8,128)}), f32[32,16,128]{2,0,1:T(8,128)S(1)}, u32[]{:S(2)}, u32[]{:S(2)}) async-start(f32[32,16,128]{2,0,1:T(8,128)} %copy.77), calls=%async_computation.6 | async-start | bytes 524288 | tf_op jit(solution)/shard_map/all_to_all | solution.py:114
  234.9 3.7 %copy-start.6 = (s32[2,32,1]{1,2,0:T(1,128)S(1)}, s32[2,32,1]{1,2,0:T(1,128)}, u32[]{:S(2)}) copy-start(s32[2,32,1]{1,2,0:T(1,128)} %param.16) | copy-start | bytes 772
  234.9 16.2 %all-to-all-start.7 = ((f32[16,32,128]{2,1,0:T(8,128)}), f32[16,32,128]{2,1,0:T(8,128)S(1)}, u32[]{:S(2)}, u32[]{:S(2)}) async-start(f32[16,32,128]{2,1,0:T(8,128)} %fusion.21), calls=%async_computation.7 | async-start | bytes 524288 | tf_op jit(solution)/shard_map/all_to_all | solution.py:117
  238.6 18.0 %collective-permute-start.12 = (f32[32,1,128]{2,0,1:T(8,128)S(1)}, f32[32,1,128]{2,0,1:T(8,128)S(1)}, u32[]{:S(2)}, u32[]{:S(2)}) collective-permute-start(f32[32,1,128]{2,0,1:T(8,128)S(1)} %get-tuple-element.34), channel_id=1, source_target_pairs={{16,0},{32,16},{48,32},{64,48},{80,64},{96,80},{112,96},{128,112},... | collective-permute-start | bytes 49160 | tf_op jit(solution)/shard_map/ppermute | solution.py:34
  240.6 14.9 %copy-start.1 = (f32[32,16,128]{2,1,0:T(8,128)S(1)}, f32[32,16,128]{2,1,0:T(8,128)}, u32[]{:S(2)}) copy-start(f32[32,16,128]{2,1,0:T(8,128)} %param.13) | copy-start | bytes 786436
  240.6 16.1 %collective-permute-start.13 = (f32[32,1,128]{2,0,1:T(8,128)S(1)}, f32[32,1,128]{2,0,1:T(8,128)S(1)}, u32[]{:S(2)}, u32[]{:S(2)}) collective-permute-start(f32[32,1,128]{2,0,1:T(8,128)S(1)} %get-tuple-element.33), channel_id=1, source_target_pairs={{0,16},{16,32},{32,48},{48,64},{64,80},{80,96},{96,112},{112,128},... | collective-permute-start | bytes 49160 | tf_op jit(solution)/shard_map/ppermute | solution.py:31
  251.1 5.5 %collective-permute-start.16 = (f32[32,1,128]{2,0,1:T(8,128)S(1)}, f32[32,1,128]{2,0,1:T(8,128)S(1)}, u32[]{:S(2)}, u32[]{:S(2)}) collective-permute-start(f32[32,1,128]{2,0,1:T(8,128)S(1)} %get-tuple-element.30), channel_id=1, source_target_pairs={{16,0},{32,16},{48,32},{64,48},{80,64},{96,80},{112,96},{128,112},... | collective-permute-start | bytes 49160 | tf_op jit(solution)/shard_map/ppermute | solution.py:34
  253.0 7.2 %collective-permute-start.17 = (f32[32,1,128]{2,0,1:T(8,128)S(1)}, f32[32,1,128]{2,0,1:T(8,128)S(1)}, u32[]{:S(2)}, u32[]{:S(2)}) collective-permute-start(f32[32,1,128]{2,0,1:T(8,128)S(1)} %get-tuple-element.29), channel_id=1, source_target_pairs={{0,16},{16,32},{32,48},{48,64},{64,80},{80,96},{96,112},{112,128},... | collective-permute-start | bytes 49160 | tf_op jit(solution)/shard_map/ppermute | solution.py:31
  261.4 16.7 %collective-permute-start.18 = (f32[32,16,128]{2,0,1:T(8,128)S(1)}, f32[32,16,128]{2,0,1:T(8,128)S(1)}, u32[]{:S(2)}, u32[]{:S(2)}) collective-permute-start(f32[32,16,128]{2,0,1:T(8,128)S(1)} %fusion.70), channel_id=1, source_target_pairs={{0,16},{16,32},{32,48},{48,64},{64,80},{80,96},{96,112},{112,128},... | collective-permute-start | bytes 786440 | tf_op jit(solution)/shard_map/ppermute | solution.py:42
  263.7 14.4 %collective-permute-start.19 = (f32[32,16,128]{2,0,1:T(8,128)S(1)}, f32[32,16,128]{2,0,1:T(8,128)S(1)}, u32[]{:S(2)}, u32[]{:S(2)}) collective-permute-start(f32[32,16,128]{2,0,1:T(8,128)S(1)} %fusion.68), channel_id=1, source_target_pairs={{16,0},{32,16},{48,32},{64,48},{80,64},{96,80},{112,96},{128,112},... | collective-permute-start | bytes 786440 | tf_op jit(solution)/shard_map/ppermute | solution.py:42
  269.8 11.5 %collective-permute-start.14 = (f32[32,16,128]{2,0,1:T(8,128)S(1)}, f32[32,16,128]{2,0,1:T(8,128)S(1)}, u32[]{:S(2)}, u32[]{:S(2)}) collective-permute-start(f32[32,16,128]{2,0,1:T(8,128)S(1)} %fusion.75), channel_id=1, source_target_pairs={{0,16},{16,32},{32,48},{48,64},{64,80},{80,96},{96,112},{112,128},... | collective-permute-start | bytes 786440 | tf_op jit(solution)/shard_map/ppermute | solution.py:42
  272.1 9.6 %collective-permute-start.15 = (f32[32,16,128]{2,0,1:T(8,128)S(1)}, f32[32,16,128]{2,0,1:T(8,128)}, u32[]{:S(2)}, u32[]{:S(2)}) collective-permute-start(f32[32,16,128]{2,0,1:T(8,128)S(1)} %fusion.73), channel_id=1, source_target_pairs={{16,0},{32,16},{48,32},{64,48},{80,64},{96,80},{112,96},{128,112},... | collective-permute-start | bytes 786440 | tf_op jit(solution)/shard_map/ppermute | solution.py:42
  285.6 1.0 copy-start.2
  285.6 1.0 copy-start.3
  285.6 1.1 copy-start.4
where the time goes:
time: 293 us; the launch traced here: 290 us
  waiting for transfers between devices  103 us (35%)
  starting transfers between devices  82 us (28%)
  blocking collectives  50.1 us (17%)
  matrix products  35.4 us (12%)
  local copies, waits for them, and re-layouts  12.6 us (4%)
  other arithmetic  5.6 us (2%)
    all_to_all x3, waiting for transfers between devices, transform(): lax.all_to_all(columns_all, 'azim', split_axis=1, concat_axis=0, tiled=True)  43.2 us
    ppermute x8, waiting for transfers between devices, with_halo(): lax.ppermute(lax.slice_in_dim(block, block.shape[dim] - width, None, axis...  33 us
    all_to_all x2, blocking collectives, transform(): lax.all_to_all(mixed, 'azim', split_axis=0, concat_axis=1, tiled=True)  32.3 us
    dot_general x4, matrix products, transform(): jnp.dot(full_table.T, spread, precision=HIGH, preferred_element_type=jnp....  28.5 us
    all_to_all x2, waiting for transfers between devices, transform(): lax.all_to_all(mixed, 'azim', split_axis=0, concat_axis=1, tiled=True)  25.9 us
    ppermute x8, starting transfers between devices, with_halo(): lax.ppermute(lax.slice_in_dim(block, 0, width, axis=dim), axis, backward)  21.7 us
    all_to_all x3, starting transfers between devices, transform(): lax.all_to_all(columns_all, 'azim', split_axis=1, concat_axis=0, tiled=True)  19.1 us
    ppermute x8, starting transfers between devices, with_halo(): lax.ppermute(lax.slice_in_dim(block, block.shape[dim] - width, None, axis...  18.4 us
  transfers between devices with their start and end apart: 25, of which 13 were waited for; matrix products, arithmetic and copies ran while one was open for 2% of the time, Pallas kernels for 0%

commit v1 on v0

--- a/solution.py
+++ b/solution.py
@@ -108,12 +108,11 @@
     return (velocity, strain, plastic)
 
 
-def transform(parts, table_rows, all_index):
+def transform(parts, table):
     flat_shape = parts.shape
     columns_all = parts.reshape(flat_shape[0], -1)
     spread = lax.all_to_all(columns_all, "azim", split_axis=1, concat_axis=0, tiled=True)
-    full_table = table_rows(all_index, all_index)
-    mixed = jnp.dot(full_table.T, spread, precision=HIGH, preferred_element_type=jnp.float32)
+    mixed = jnp.dot(table, spread, precision=HIGH, preferred_element_type=jnp.float32)
     joined = lax.all_to_all(mixed, "azim", split_axis=0, concat_axis=1, tiled=True)
     return joined.reshape(flat_shape)
 
@@ -130,9 +129,7 @@
     strain,
     plastic,
 ):
-    local_count = potential.shape[0]
-    axial_cells = potential.shape[1]
-    radial_cells = potential.shape[2]
+    local_count, axial_cells, radial_cells = potential.shape
     band_width = tile_weight.shape[1]
     azim_total = local_count * lax.axis_size("azim")
     own_index = lax.axis_index("azim") * local_count + jnp.arange(local_count, dtype=jnp.int32)
@@ -143,31 +140,39 @@
     diagonal_term = (
         4.0 + conduct[None, None, :] + (orders[:, None, None] / radius[None, None, :]) ** 2
     )
-
-    def forward_rows(rows_in, rows_out):
-        return harmonic_table(rows_in, rows_out, azim_total)
-
-    def inverse_rows(rows_in, rows_out):
-        return (
-            harmonic_table(rows_out, rows_in, azim_total).T
-            * harmonic_weight(rows_in, azim_total)[:, None]
-        )
+    basis = harmonic_table(all_index, all_index, azim_total)
+    forward_table = basis.T
+    inverse_table = basis * harmonic_weight(all_index, azim_total)[None, :]
+
+    coil = coil_density[..., :band_start] * coil_mask[..., :band_start].astype(jnp.float32)
+    modes = transform(jnp.concatenate([potential, coil], axis=-1), forward_table)
+
+    reach = STEPS * SWEEPS + 1
+    modes = with_halo(modes, (("axial", 1),), reach)
+    field_modes = modes[..., :radial_cells]
+    coil_modes = jnp.pad(modes[..., radial_cells:], ((0, 0), (0, 0), (0, radial_cells - band_start)))
+    span = axial_cells + 2 * reach
+    global_z = lax.axis_index("axial") * axial_cells - reach + jnp.arange(span, dtype=jnp.int32)
+    inside = ((global_z >= 0) & (global_z < axial_cells * lax.axis_size("axial")))[None, :, None]
+
+    iterate = field_modes
+    kept = []
+    for step_index in range(STEPS):
+        right_side = MU_COIL * (drive[step_index] * coil_modes) + conduct * iterate
+        for sweep_index in range(SWEEPS):
+            axial_pad = jnp.pad(iterate, ((0, 0), (1, 1), (0, 0)))
+            nearby = axial_pad[:, 2:] + axial_pad[:, :-2] + radial_sum(iterate)
+            iterate = jnp.where(inside, (right_side + nearby) / diagonal_term, 0.0)
+        kept.append(iterate[:, reach - 1 : reach + axial_cells + 1])
+    fields = transform(jnp.concatenate(kept, axis=-1), inverse_table)
 
     slot_range = jnp.arange(local_count, dtype=jnp.int32)
-    field = potential
+    previous = potential
+    same, upward, downward = [], [], []
     for step_index in range(STEPS):
-        source = drive[step_index] * coil_density * coil_mask.astype(jnp.float32) * coil_zone
-        stacked = jnp.stack([source, field], axis=1)
-        modes = transform(stacked, forward_rows, all_index)
-        right_side = MU_COIL * modes[:, 0] + conduct * modes[:, 1]
-        iterate = modes[:, 1]
-        for sweep_index in range(SWEEPS):
-            axial_pad = with_halo(iterate, (("axial", 1),), 1)
-            nearby = axial_pad[:, 2:] + axial_pad[:, :-2] + radial_sum(iterate)
-            iterate = (right_side + nearby) / diagonal_term
-        new_field = transform(iterate[:, None], inverse_rows, all_index)[:, 0]
-        padded = with_halo(new_field, (("axial", 1),), 1)
-        tiles = lorentz(padded, field, conduct, radius, band_start, band_width)
+        padded = fields[..., step_index * radial_cells : (step_index + 1) * radial_cells]
+        tiles = lorentz(padded, previous, conduct, radius, band_start, band_width)
+        previous = padded[:, 1:-1]
         slot_table = (relay_slot[step_index, :, 0][:, None] == slot_range[None, :]).astype(
             jnp.float32
         )
@@ -179,17 +184,20 @@
                 "jcw,jp->pcw", tiles * chosen[:, None, None], slot_table, precision=HIGH
             )
 
-        from_below = shifted(place(2), "axial", 1)
-        from_above = shifted(place(0), "axial", -1)
-        received = (place(1) + from_below + from_above).reshape(
+        same.append(place(1))
+        upward.append(place(2))
+        downward.append(place(0))
+    from_below = shifted(jnp.stack(upward), "axial", 1)
+    from_above = shifted(jnp.stack(downward), "axial", -1)
+    for step_index in range(STEPS):
+        received = (same[step_index] + from_below[step_index] + from_above[step_index]).reshape(
             local_count, axial_cells, 2, band_width
         )
         load = jnp.einsum("aqr,azcr->azcq", tile_weight, received, precision=HIGH).reshape(
             local_count, axial_cells, 2 * band_width
         )
         velocity, strain, plastic = plastic_update(load, velocity, strain, plastic)
-        field = new_field
-    return (field, velocity, strain, plastic)
+    return (previous, velocity, strain, plastic)
 
 
 def solution(mesh):

time: 293 us -> 176 us (0.60)
  blocking collectives: 50.1 us -> 0 us
  starting transfers between devices: 82 us -> 36.5 us
  matrix products: 35.4 us -> 24.6 us
  waiting for transfers between devices: 103 us -> 92.2 us
    all_to_all x3 -> x0, blocking collectives: 50.1 us -> none  [the longest x2 32.3 us: transform(): lax.all_to_all(mixed, 'azim', split_axis=0, concat_axis=1, tiled=True)]
    ppermute x8 -> x1, waiting for transfers between devices: 33 us -> 0.5 us  [with_halo(): lax.ppermute(lax.slice_in_dim(block, block.shape[dim] - width, None, axis...]
    ppermute x8 -> x1, starting transfers between devices: 18.4 us -> 1.92 us  [with_halo(): lax.ppermute(lax.slice_in_dim(block, block.shape[dim] - width, None, axis...]
    ppermute x8 -> x1, starting transfers between devices: 21.7 us -> 5.75 us  [with_halo(): lax.ppermute(lax.slice_in_dim(block, 0, width, axis=dim), axis, backward)]
    all_to_all x2, waiting for transfers between devices: 25.9 us -> 39.7 us  [transform(): lax.all_to_all(mixed, 'azim', split_axis=0, concat_axis=1, tiled=True)]
    dot_general x4 -> x2, matrix products: 28.5 us -> 18.6 us  [transform(): jnp.dot(table, spread, precision=HIGH, preferred_element_type=jnp.float32)]
    ppermute x4 -> x2, starting transfers between devices: 15.6 us -> 7.87 us  [shifted(): return lax.ppermute(array, axis, pairs)]
    ppermute x4 -> x2, waiting for transfers between devices: 0.4 us -> 6.5 us  [shifted(): return lax.ppermute(array, axis, pairs)]
  transfers between devices with their start and end apart: 25 -> 8, of which waited for: 13 -> 8; matrix products, arithmetic and copies ran while one was open for 2% -> 1% of each run, Pallas kernels for 0% -> 0%
where the time goes in v1:
time: 176 us; the launch traced here: 174 us
  waiting for transfers between devices  92.2 us (52%)
  starting transfers between devices  36.5 us (21%)
  matrix products  24.6 us (14%)
  local copies, waits for them, and re-layouts  12.6 us (7%)
  other arithmetic  7.17 us (4%)
    all_to_all x2, waiting for transfers between devices, transform(): lax.all_to_all(columns_all, 'azim', split_axis=1, concat_axis=0, tiled=True)  43.7 us
    all_to_all x2, waiting for transfers between devices, transform(): lax.all_to_all(mixed, 'azim', split_axis=0, concat_axis=1, tiled=True)  39.7 us
    dot_general x2, matrix products, transform(): jnp.dot(table, spread, precision=HIGH, preferred_element_type=jnp.float32)  18.6 us
    all_to_all x2, starting transfers between devices, transform(): lax.all_to_all(columns_all, 'azim', split_axis=1, concat_axis=0, tiled=True)  13.7 us
    ppermute x2, starting transfers between devices, shifted(): return lax.ppermute(array, axis, pairs)  7.87 us
    all_to_all x2, starting transfers between devices, transform(): lax.all_to_all(mixed, 'azim', split_axis=0, concat_axis=1, tiled=True)  7.18 us
    ppermute x2, waiting for transfers between devices, shifted(): return lax.ppermute(array, axis, pairs)  6.5 us
    ppermute x1, starting transfers between devices, with_halo(): lax.ppermute(lax.slice_in_dim(block, 0, width, axis=dim), axis, backward)  5.75 us
  transfers between devices with their start and end apart: 8, of which 8 were waited for; matrix products, arithmetic and copies ran while one was open for 1% of the time, Pallas kernels for 0%

profile of v1, /device:TPU:2, one launch (start us, length us, event | category | flops | bytes accessed | tf_op | source)
XLA Modules:
  0.0 174.1 jit_solution(11632185539788582398)
XLA Ops:
  0.7 1.2 copy.41
  1.8 0.2 fusion.93
  2.0 0.8 pad_maximum_fusion.2
  2.8 10.1 %all-to-all-start = ((f32[32,16,160]{2,0,1:T(8,128)}), f32[32,16,160]{2,0,1:T(8,128)S(1)}, u32[]{:S(2)}, u32[]{:S(2)}) async-start(f32[32,16,160]{2,0,1:T(8,128)} %pad_maximum_fusion.2), calls=%async_computation | async-start | bytes 1048576 | tf_op jit(solution)/shard_map/all_to_all | solution.py:114
  13.0 18.8 %all-to-all-done = f32[32,16,160]{2,0,1:T(8,128)S(1)} async-done(((f32[32,16,160]{2,0,1:T(8,128)}), f32[32,16,160]{2,0,1:T(8,128)S(1)}, u32[]{:S(2)}, u32[]{:S(2)}) %all-to-all-start) | async-done | bytes 327712 | tf_op jit(solution)/shard_map/all_to_all | solution.py:114
  31.8 8.6 %fusion.10 = f32[16,32,160]{2,1,0:T(8,128)} fusion(f32[512,160,1]{1,0,2:T(8,128)S(1)} %bitcast.90, s32[16,32]{1,0:T(8,128)S(1)} %add_select_fusion.2, pred[16,32]{1,0:T(8,128)(4,1)S(1)} %fusion.121), kind=kOutput, calls=%fused_computation.34 | convolution fusion | flops 507248640 | bytes 657920 | tf_op jit(solution)/shard_map/dot_general | solution.py:115
  40.4 3.6 %all-to-all-start.1 = ((f32[16,32,160]{2,1,0:T(8,128)}), f32[16,32,160]{2,1,0:T(8,128)S(1)}, u32[]{:S(2)}, u32[]{:S(2)}) async-start(f32[16,32,160]{2,1,0:T(8,128)} %fusion.10), calls=%async_computation.1 | async-start | bytes 1048576 | tf_op jit(solution)/shard_map/all_to_all | solution.py:116
  44.1 18.1 %all-to-all-done.1 = f32[16,32,160]{2,1,0:T(8,128)S(1)} async-done(((f32[16,32,160]{2,1,0:T(8,128)}), f32[16,32,160]{2,1,0:T(8,128)S(1)}, u32[]{:S(2)}, u32[]{:S(2)}) %all-to-all-start.1) | async-done | bytes 327712 | tf_op jit(solution)/shard_map/all_to_all | solution.py:116
  62.3 1.9 %collective-permute-start = (f32[32,7,160]{2,0,1:T(8,128)S(1)}, f32[32,7,160]{2,0,1:T(8,128)S(1)}, u32[]{:S(2)}, u32[]{:S(2)}) collective-permute-start(f32[32,7,160]{2,0,1:T(8,128)S(1)} %get-tuple-element.25), channel_id=1, source_target_pairs={{0,16},{16,32},{32,48},{48,64},{64,80},{80,96},{96,112},{112,128},... | collective-permute-start | bytes 430088 | tf_op jit(solution)/shard_map/ppermute | solution.py:31
  64.2 5.8 %collective-permute-start.1 = (f32[32,7,160]{2,0,1:T(8,128)S(1)}, f32[32,7,160]{2,0,1:T(8,128)S(1)}, u32[]{:S(2)}, u32[]{:S(2)}) collective-permute-start(f32[32,7,160]{2,0,1:T(8,128)S(1)} %get-tuple-element.26), channel_id=1, source_target_pairs={{16,0},{32,16},{48,32},{64,48},{80,64},{96,80},{112,96},{128,112},... | collective-permute-start | bytes 430088 | tf_op jit(solution)/shard_map/ppermute | solution.py:34
  70.1 0.6 copy-done.9
  70.7 0.6 fusion.141
  71.2 0.5 collective-permute-done
  71.7 1.8 %collective-permute-done.1 = f32[32,7,160]{2,0,1:T(8,128)S(1)} collective-permute-done((f32[32,7,160]{2,0,1:T(8,128)S(1)}, f32[32,7,160]{2,0,1:T(8,128)S(1)}, u32[]{:S(2)}, u32[]{:S(2)}) %collective-permute-start.1) | collective-permute-done | bytes 143392 | tf_op jit(solution)/shard_map/ppermute | solution.py:34
  73.7 1.0 fusion.50
  74.7 0.4 fusion.55
  75.0 0.4 fusion.60
  75.4 0.8 copy-done.1
  76.2 1.0 fusion.65
  77.2 0.4 fusion.70
  77.6 0.4 pad_slice_fusion.17
  77.9 0.1 fusion.77
  78.0 0.8 slice-done
  78.9 0.4 copy.43
  79.3 0.5 all_to_all.51
  79.8 1.1 copy.44
  80.9 3.6 %all-to-all-start.2 = ((f32[32,16,288]{2,0,1:T(8,128)}), f32[32,16,288]{2,0,1:T(8,128)S(1)}, u32[]{:S(2)}, u32[]{:S(2)}) async-start(f32[32,16,288]{2,0,1:T(8,128)} %copy.44), calls=%async_computation.2 | async-start | bytes 1572864 | tf_op jit(solution)/shard_map/all_to_all | solution.py:114
  84.6 25.0 %all-to-all-done.2 = f32[32,16,288]{2,0,1:T(8,128)S(1)} async-done(((f32[32,16,288]{2,0,1:T(8,128)}), f32[32,16,288]{2,0,1:T(8,128)S(1)}, u32[]{:S(2)}, u32[]{:S(2)}) %all-to-all-start.2) | async-done | bytes 589856 | tf_op jit(solution)/shard_map/all_to_all | solution.py:114
  109.6 10.0 %fusion.18 = f32[16,32,288]{2,1,0:T(8,128)} fusion(f32[512,288,1]{1,0,2:T(8,128)S(1)} %bitcast.89, f32[512]{0:T(512)S(1)} %fusion.123, s32[512]{0:T(512)S(1)} %add_select_fusion.3, s32[16,32]{1,0:T(8,128)S(1)} %multiply_add_fusion.6, pred[512]{0:T(512)(128)(4,1)S(1)} %iota_compare_fusion.4), kind=kOutput, calls=%fused_computation.41 | convolution fusion | flops 910163968 | bytes 1186304 | tf_op jit(solution)/shard_map/dot_general | solution.py:115
  119.6 3.6 %all-to-all-start.3 = ((f32[16,32,288]{2,1,0:T(8,128)}), f32[16,32,288]{2,1,0:T(8,128)S(1)}, u32[]{:S(2)}, u32[]{:S(2)}) async-start(f32[16,32,288]{2,1,0:T(8,128)} %fusion.18), calls=%async_computation.3 | async-start | bytes 1572864 | tf_op jit(solution)/shard_map/all_to_all | solution.py:116
  123.3 0.7 copy-done.10
  123.9 0.7 copy-done.11
  124.6 21.6 %all-to-all-done.3 = f32[16,32,288]{2,1,0:T(8,128)S(1)} async-done(((f32[16,32,288]{2,1,0:T(8,128)}), f32[16,32,288]{2,1,0:T(8,128)S(1)}, u32[]{:S(2)}, u32[]{:S(2)}) %all-to-all-start.3) | async-done | bytes 589856 | tf_op jit(solution)/shard_map/all_to_all | solution.py:116
  146.2 0.5 copy.46
  146.7 0.6 reshape.304
  147.3 0.3 copy-done.3
  147.6 0.1 subtract_multiply_fusion
  147.8 0.2 pad_slice_fusion.15
  148.0 0.2 pad_slice_fusion.13
  148.2 0.3 copy-done.2
  148.5 0.9 fusion.91
  149.4 0.2 broadcast_multiply_fusion.5
  149.6 0.3 convolution_bitcast_fusion.3
  150.0 0.2 broadcast_multiply_fusion
  150.2 0.3 convolution_bitcast_fusion.2
  150.6 1.9 %collective-permute-start.2 = (f32[2,32,16,128]{3,1,2,0:T(8,128)S(1)}, f32[2,32,16,128]{3,1,2,0:T(8,128)S(1)}, u32[]{:S(2)}, u32[]{:S(2)}) collective-permute-start(f32[2,32,16,128]{3,1,2,0:T(8,128)S(1)} %pad_maximum_fusion.3), channel_id=1, source_target_pairs={{0,16},{16,32},{32,48},{48,64},{64,80},{80,96},{96,112},{112,128},... | collective-permute-start | bytes 1572872 | tf_op jit(solution)/shard_map/ppermute | solution.py:42
  152.5 0.3 convolution_bitcast_fusion.1
  152.9 0.3 convolution_bitcast_fusion
  153.3 5.9 %collective-permute-start.3 = (f32[2,32,16,128]{3,1,2,0:T(8,128)S(1)}, f32[2,32,16,128]{3,1,2,0:T(8,128)S(1)}, u32[]{:S(2)}, u32[]{:S(2)}) collective-permute-start(f32[2,32,16,128]{3,1,2,0:T(8,128)S(1)} %pad_maximum_fusion.4), channel_id=1, source_target_pairs={{16,0},{32,16},{48,32},{64,48},{80,64},{96,80},{112,96},{128,112},... | collective-permute-start | bytes 1572872 | tf_op jit(solution)/shard_map/ppermute | solution.py:42
  159.2 4.0 %collective-permute-done.2 = f32[2,32,16,128]{3,1,2,0:T(8,128)S(1)} collective-permute-done((f32[2,32,16,128]{3,1,2,0:T(8,128)S(1)}, f32[2,32,16,128]{3,1,2,0:T(8,128)S(1)}, u32[]{:S(2)}, u32[]{:S(2)}) %collective-permute-start.2) | collective-permute-done | bytes 524320 | tf_op jit(solution)/shard_map/ppermute | solution.py:42
  163.2 2.5 %collective-permute-done.3 = f32[2,32,16,128]{3,1,2,0:T(8,128)S(1)} collective-permute-done((f32[2,32,16,128]{3,1,2,0:T(8,128)S(1)}, f32[2,32,16,128]{3,1,2,0:T(8,128)S(1)}, u32[]{:S(2)}, u32[]{:S(2)}) %collective-permute-start.3) | collective-permute-done | bytes 524320 | tf_op jit(solution)/shard_map/ppermute | solution.py:42
  165.7 0.3 fusion.79
  166.1 0.3 reshape.307
  166.4 1.9 %fusion.6 = f32[32,16,2,64]{3,1,2,0:T(8,128)S(1)} fusion(f32[32,64,64]{2,1,0:T(8,128)S(1)} %copy-done, f32[32,16,2,64]{3,2,0,1:T(2,128)S(1)} %reshape.307), kind=kOutput, calls=%fused_computation.30 | convolution fusion | flops 50331648 | bytes 1048576 | tf_op jit(solution)/shard_map/aqr,azcr->azcq/dot_general | solution.py:196
  168.4 0.3 copy.56
  168.6 0.3 reshape.308
  168.9 0.4 fusion.81
  169.3 0.3 reshape.305
  169.6 1.9 %fusion.8 = f32[32,16,2,64]{3,1,2,0:T(8,128)S(1)} fusion(f32[32,64,64]{2,1,0:T(8,128)S(1)} %copy-done, f32[32,16,2,64]{3,2,0,1:T(2,128)S(1)} %reshape.305), kind=kOutput, calls=%fused_computation.32 | convolution fusion | flops 50331648 | bytes 1048576 | tf_op jit(solution)/shard_map/aqr,azcr->azcq/dot_general | solution.py:196
  171.6 0.3 copy.53
  171.9 0.3 reshape.306
  172.2 0.6 copy-done.6
  172.9 0.1 copy-done.8
  173.0 1.2 multiply_add_fusion.2
  (40 shorter events, 0.7 us)
Async XLA Ops:
  0.6 165.8 %copy-start = (f32[32,64,64]{2,1,0:T(8,128)S(1)}, f32[32,64,64]{2,1,0:T(8,128)}, u32[]{:S(2)}) copy-start(f32[32,64,64]{2,1,0:T(8,128)} %param.14) | copy-start | bytes 1572868
  0.6 1.2 copy-start.4
  0.7 1.2 copy-start.5
  2.8 29.0 %all-to-all-start = ((f32[32,16,160]{2,0,1:T(8,128)}), f32[32,16,160]{2,0,1:T(8,128)S(1)}, u32[]{:S(2)}, u32[]{:S(2)}) async-start(f32[32,16,160]{2,0,1:T(8,128)} %pad_maximum_fusion.2), calls=%async_computation | async-start | bytes 1048576 | tf_op jit(solution)/shard_map/all_to_all | solution.py:114
  40.4 21.8 %all-to-all-start.1 = ((f32[16,32,160]{2,1,0:T(8,128)}), f32[16,32,160]{2,1,0:T(8,128)S(1)}, u32[]{:S(2)}, u32[]{:S(2)}) async-start(f32[16,32,160]{2,1,0:T(8,128)} %fusion.10), calls=%async_computation.1 | async-start | bytes 1048576 | tf_op jit(solution)/shard_map/all_to_all | solution.py:116
  62.3 9.4 %collective-permute-start = (f32[32,7,160]{2,0,1:T(8,128)S(1)}, f32[32,7,160]{2,0,1:T(8,128)S(1)}, u32[]{:S(2)}, u32[]{:S(2)}) collective-permute-start(f32[32,7,160]{2,0,1:T(8,128)S(1)} %get-tuple-element.25), channel_id=1, source_target_pairs={{0,16},{16,32},{32,48},{48,64},{64,80},{80,96},{96,112},{112,128},... | collective-permute-start | bytes 430088 | tf_op jit(solution)/shard_map/ppermute | solution.py:31
  64.2 9.3 %collective-permute-start.1 = (f32[32,7,160]{2,0,1:T(8,128)S(1)}, f32[32,7,160]{2,0,1:T(8,128)S(1)}, u32[]{:S(2)}, u32[]{:S(2)}) collective-permute-start(f32[32,7,160]{2,0,1:T(8,128)S(1)} %get-tuple-element.26), channel_id=1, source_target_pairs={{16,0},{32,16},{48,32},{64,48},{80,64},{96,80},{112,96},{128,112},... | collective-permute-start | bytes 430088 | tf_op jit(solution)/shard_map/ppermute | solution.py:34
  70.0 0.7 copy-start.9
  75.4 0.8 copy-start.1
  77.9 1.0 slice-start
  80.9 28.6 %all-to-all-start.2 = ((f32[32,16,288]{2,0,1:T(8,128)}), f32[32,16,288]{2,0,1:T(8,128)S(1)}, u32[]{:S(2)}, u32[]{:S(2)}) async-start(f32[32,16,288]{2,0,1:T(8,128)} %copy.44), calls=%async_computation.2 | async-start | bytes 1572864 | tf_op jit(solution)/shard_map/all_to_all | solution.py:114
  119.6 26.7 %all-to-all-start.3 = ((f32[16,32,288]{2,1,0:T(8,128)}), f32[16,32,288]{2,1,0:T(8,128)S(1)}, u32[]{:S(2)}, u32[]{:S(2)}) async-start(f32[16,32,288]{2,1,0:T(8,128)} %fusion.18), calls=%async_computation.3 | async-start | bytes 1572864 | tf_op jit(solution)/shard_map/all_to_all | solution.py:116
  123.3 0.7 copy-start.10
  123.9 0.7 copy-start.11
  146.7 1.0 copy-start.3
  147.8 0.7 copy-start.2
  150.6 12.6 %collective-permute-start.2 = (f32[2,32,16,128]{3,1,2,0:T(8,128)S(1)}, f32[2,32,16,128]{3,1,2,0:T(8,128)S(1)}, u32[]{:S(2)}, u32[]{:S(2)}) collective-permute-start(f32[2,32,16,128]{3,1,2,0:T(8,128)S(1)} %pad_maximum_fusion.3), channel_id=1, source_target_pairs={{0,16},{16,32},{32,48},{48,64},{64,80},{80,96},{96,112},{112,128},... | collective-permute-start | bytes 1572872 | tf_op jit(solution)/shard_map/ppermute | solution.py:42
  153.3 12.5 %collective-permute-start.3 = (f32[2,32,16,128]{3,1,2,0:T(8,128)S(1)}, f32[2,32,16,128]{3,1,2,0:T(8,128)S(1)}, u32[]{:S(2)}, u32[]{:S(2)}) collective-permute-start(f32[2,32,16,128]{3,1,2,0:T(8,128)S(1)} %pad_maximum_fusion.4), channel_id=1, source_target_pairs={{16,0},{32,16},{48,32},{64,48},{80,64},{96,80},{112,96},{128,112},... | collective-permute-start | bytes 1572872 | tf_op jit(solution)/shard_map/ppermute | solution.py:42
  171.8 1.0 copy-start.6
  171.9 1.0 copy-start.7
  171.9 1.1 copy-start.8

commit v2 on v1

--- a/solution.py
+++ b/solution.py
@@ -1,6 +1,7 @@
 import math
 
 import jax
+import numpy as np
 import jax.numpy as jnp
 from jax import lax
 from jax.sharding import PartitionSpec as P
@@ -108,13 +109,45 @@
     return (velocity, strain, plastic)
 
 
-def transform(parts, table):
-    flat_shape = parts.shape
-    columns_all = parts.reshape(flat_shape[0], -1)
-    spread = lax.all_to_all(columns_all, "azim", split_axis=1, concat_axis=0, tiled=True)
-    mixed = jnp.dot(table, spread, precision=HIGH, preferred_element_type=jnp.float32)
-    joined = lax.all_to_all(mixed, "azim", split_axis=0, concat_axis=1, tiled=True)
-    return joined.reshape(flat_shape)
+def basis_constant(count_all):
+    half_count = count_all // 2
+    harmonic = np.arange(count_all)
+    orders = np.where(harmonic <= half_count, harmonic, harmonic - half_count)
+    phases = (harmonic[:, None] * orders[None, :]) % count_all
+    angles = phases.astype(np.float64) * (2.0 * math.pi / count_all)
+    table = np.where(harmonic[None, :] <= half_count, np.cos(angles), np.sin(angles))
+    return table.astype(np.float32)
+
+
+def transform(flat, basis, inverse):
+    rows, count = flat.shape
+    devices = lax.axis_size("azim")
+    unit = devices * 128 // math.gcd(rows, 128)
+    padded = -(-count // unit) * unit
+    flat = jnp.pad(flat, ((0, 0), (0, padded - count)))
+    width = padded // devices
+    dense = (devices, rows * width // 128, 128)
+    blocks = flat.reshape(rows, devices, width).transpose(1, 0, 2).reshape(dense)
+    spread = lax.all_to_all(blocks, "azim", 0, 0, tiled=True).reshape(devices * rows, width)
+    contract = 1 if inverse else 0
+    mixed = lax.dot_general(
+        basis, spread, (((contract,), (0,)), ((), ())), precision=HIGH,
+        preferred_element_type=jnp.float32,
+    )
+    joined = lax.all_to_all(mixed.reshape(dense), "azim", 0, 0, tiled=True)
+    return joined.reshape(devices, rows, width).transpose(1, 0, 2).reshape(rows, padded)[:, :count]
+
+
+def lorentz_window(padded, previous, conduct, radius):
+    current_field = padded[:, 1:-1]
+    axial_slope = (padded[:, 2:] - padded[:, :-2]) * 0.5
+    radial_pad = jnp.pad(current_field, ((0, 0), (0, 0), (1, 1)))
+    radial_slope = (radial_pad[:, :, 2:] - radial_pad[:, :, :-2]) * 0.5
+    b_axial = radial_slope + current_field / radius
+    eddy_current = -conduct * (current_field - previous)
+    force_radial = FORCE_K * eddy_current * b_axial
+    force_axial = FORCE_K * eddy_current * axial_slope
+    return jnp.concatenate([force_radial[..., 1:-1], force_axial[..., 1:-1]], axis=-1)
 
 
 def shards(
@@ -133,19 +166,27 @@
     band_width = tile_weight.shape[1]
     azim_total = local_count * lax.axis_size("azim")
     own_index = lax.axis_index("azim") * local_count + jnp.arange(local_count, dtype=jnp.int32)
-    all_index = jnp.arange(azim_total, dtype=jnp.int32)
     band_start = radial_cells // 4
     radius, conduct, coil_zone = radial_profiles(radial_cells, band_start, band_width)
     orders = harmonic_order(own_index, azim_total)
     diagonal_term = (
         4.0 + conduct[None, None, :] + (orders[:, None, None] / radius[None, None, :]) ** 2
     )
-    basis = harmonic_table(all_index, all_index, azim_total)
-    forward_table = basis.T
-    inverse_table = basis * harmonic_weight(all_index, azim_total)[None, :]
+    basis = jnp.asarray(basis_constant(azim_total))
 
     coil = coil_density[..., :band_start] * coil_mask[..., :band_start].astype(jnp.float32)
-    modes = transform(jnp.concatenate([potential, coil], axis=-1), forward_table)
+    flat = jnp.concatenate(
+        [potential.reshape(local_count, -1), coil.reshape(local_count, -1)], axis=1
+    )
+    modes = transform(flat, basis, inverse=False)
+    split_at = axial_cells * radial_cells
+    modes = jnp.concatenate(
+        [
+            modes[:, :split_at].reshape(local_count, axial_cells, radial_cells),
+            modes[:, split_at:].reshape(local_count, axial_cells, band_start),
+        ],
+        axis=-1,
+    )
 
     reach = STEPS * SWEEPS + 1
     modes = with_halo(modes, (("axial", 1),), reach)
@@ -155,6 +196,8 @@
     global_z = lax.axis_index("axial") * axial_cells - reach + jnp.arange(span, dtype=jnp.int32)
     inside = ((global_z >= 0) & (global_z < axial_cells * lax.axis_size("axial")))[None, :, None]
 
+    weight = harmonic_weight(own_index, azim_total)[:, None, None]
+    window = slice(band_start - 1, band_start + band_width + 1)
     iterate = field_modes
     kept = []
     for step_index in range(STEPS):
@@ -163,15 +206,29 @@
             axial_pad = jnp.pad(iterate, ((0, 0), (1, 1), (0, 0)))
             nearby = axial_pad[:, 2:] + axial_pad[:, :-2] + radial_sum(iterate)
             iterate = jnp.where(inside, (right_side + nearby) / diagonal_term, 0.0)
-        kept.append(iterate[:, reach - 1 : reach + axial_cells + 1])
-    fields = transform(jnp.concatenate(kept, axis=-1), inverse_table)
+        planes = iterate[:, reach - 1 : reach + axial_cells + 1] * weight
+        kept.append(planes if step_index == STEPS - 1 else planes[..., window])
+    pieces = [piece.shape for piece in kept]
+    flat = transform(
+        jnp.concatenate([piece.reshape(local_count, -1) for piece in kept], axis=1),
+        basis,
+        inverse=True,
+    )
+    fields, offset = [], 0
+    for shape in pieces:
+        size = math.prod(shape[1:])
+        fields.append(flat[:, offset : offset + size].reshape(shape))
+        offset += size
 
     slot_range = jnp.arange(local_count, dtype=jnp.int32)
-    previous = potential
+    previous = potential[..., window]
     same, upward, downward = [], [], []
     for step_index in range(STEPS):
-        padded = fields[..., step_index * radial_cells : (step_index + 1) * radial_cells]
-        tiles = lorentz(padded, previous, conduct, radius, band_start, band_width)
+        padded = fields[step_index]
+        if step_index == STEPS - 1:
+            field_out = padded[:, 1:-1]
+            padded = padded[..., window]
+        tiles = lorentz_window(padded, previous, conduct[window], radius[window])
         previous = padded[:, 1:-1]
         slot_table = (relay_slot[step_index, :, 0][:, None] == slot_range[None, :]).astype(
             jnp.float32
@@ -197,7 +254,7 @@
             local_count, axial_cells, 2 * band_width
         )
         velocity, strain, plastic = plastic_update(load, velocity, strain, plastic)
-    return (previous, velocity, strain, plastic)
+    return (field_out, velocity, strain, plastic)
 
 
 def solution(mesh):

time: 176 us -> 144 us (0.82)
  waiting for transfers between devices: 92.2 us -> 43.3 us
  blocking collectives: 0 us -> 42.3 us
  starting transfers between devices: 36.5 us -> 19.2 us
  matrix products: 24.6 us -> 8.74 us
  local copies, waits for them, and re-layouts: 12.6 us -> 20.6 us
    all_to_all x4 -> x2, waiting for transfers between devices: 83.5 us -> 27 us  [transform(): joined = lax.all_to_all(mixed.reshape(dense), 'azim', 0, 0, tiled=True)]
    all_to_all x0 -> x2, blocking collectives: none -> 42.3 us  [transform(): lax.all_to_all(blocks, 'azim', 0, 0, tiled=True)]
    dot_general x2, matrix products: 18.6 us -> 2.79 us  [transform(): lax.dot_general(basis, spread, (((contract,), (0,)), ((), ())), precision...]
    all_to_all x4 -> x2, starting transfers between devices: 20.9 us -> 7.1 us  [transform(): joined = lax.all_to_all(mixed.reshape(dense), 'azim', 0, 0, tiled=True)]
    reshape x1 -> x18, local copies, waits for them, and re-layouts: 0.61 us -> 7.89 us  [the longest x2 2.4 us: transform(): joined = lax.all_to_all(mixed.reshape(dense), 'azim', 0, 0, tiled=True)]
    ppermute x1, waiting for transfers between devices: 0.5 us -> 5.93 us  [with_halo(): lax.ppermute(lax.slice_in_dim(block, block.shape[dim] - width, None, axis...]
    ppermute x2, waiting for transfers between devices: 6.5 us -> 9.73 us  [shifted(): return lax.ppermute(array, axis, pairs)]
    ppermute x1, starting transfers between devices: 5.75 us -> 2.55 us  [with_halo(): lax.ppermute(lax.slice_in_dim(block, 0, width, axis=dim), axis, backward)]
  transfers between devices with their start and end apart: 8 -> 6, of which waited for: 8 -> 6; matrix products, arithmetic and copies ran while one was open for 1% -> 2% of each run, Pallas kernels for 0% -> 0%
where the time goes in v2:
time: 144 us
  waiting for transfers between devices  43.3 us (30%)
  blocking collectives  42.3 us (29%)
  local copies, waits for them, and re-layouts  20.6 us (14%)
  starting transfers between devices  19.2 us (13%)
  matrix products  8.74 us (6%)
  other arithmetic  8.19 us (6%)
    all_to_all x2, blocking collectives, transform(): lax.all_to_all(blocks, 'azim', 0, 0, tiled=True)  42.3 us
    all_to_all x2, waiting for transfers between devices, transform(): joined = lax.all_to_all(mixed.reshape(dense), 'azim', 0, 0, tiled=True)  27 us
    ppermute x2, waiting for transfers between devices, shifted(): return lax.ppermute(array, axis, pairs)  9.73 us
    ppermute x2, starting transfers between devices, shifted(): return lax.ppermute(array, axis, pairs)  7.67 us
    all_to_all x2, starting transfers between devices, transform(): joined = lax.all_to_all(mixed.reshape(dense), 'azim', 0, 0, tiled=True)  7.1 us
    ppermute x1, waiting for transfers between devices, with_halo(): lax.ppermute(lax.slice_in_dim(block, block.shape[dim] - width, None, axis...  5.93 us
    unnamed x29, local copies, waits for them, and re-layouts  5.76 us
    dot_general x2, matrix products, shards(): jnp.einsum('aqr,azcr->azcq', tile_weight, received, precision=HIGH)  3.85 us
  transfers between devices with their start and end apart: 6, of which 6 were waited for; matrix products, arithmetic and copies ran while one was open for 2% of the time, Pallas kernels for 0%

profile of v2, /device:TPU:2, one launch (start us, length us, event | category | flops | bytes accessed | tf_op | source)
XLA Modules:
  0.0 143.7 jit_solution(15608104540556394752)
XLA Ops:
  0.6 1.2 convert_multiply_fusion
  2.0 0.8 copy-done.4
  2.9 0.3 reshape.232
  3.2 0.3 copy.36
  3.5 0.4 reshape.233
  3.9 24.6 %all_to_all.20 = f32[16,40,128]{2,1,0:T(8,128)S(1)} all-to-all(f32[16,40,128]{2,1,0:T(8,128)S(1)} %reshape.233), channel_id=1, replica_groups=mesh['axial'=16,'azim'=16] {'azim'}, dimensions={0} | all-to-all | bytes 655360 | tf_op jit(solution)/shard_map/all_to_all | solution.py:131
  28.8 1.8 %fusion.85 = f32[512,160]{1,0:T(8,128)S(1)} fusion(f32[512,512]{1,0:T(8,128)S(1)} %copy-done.1, f32[512,160]{1,0:T(8,128)S(1)} %reshape.234), kind=kOutput, calls=%fused_computation.161 | convolution fusion | flops 503316480 | bytes 1703936 | tf_op jit(solution)/shard_map/dot_general | solution.py:133
  30.6 1.1 reshape.235
  31.7 3.5 %all-to-all-start.1 = ((f32[16,40,128]{2,1,0:T(8,128)}), f32[16,40,128]{2,1,0:T(8,128)S(1)}, u32[]{:S(2)}, u32[]{:S(2)}) async-start(f32[16,40,128]{2,1,0:T(8,128)} %reshape.235), calls=%async_computation.1 | async-start | bytes 655360 | tf_op jit(solution)/shard_map/all_to_all | solution.py:137
  35.4 13.9 %all-to-all-done.1 = f32[16,40,128]{2,1,0:T(8,128)S(1)} async-done(((f32[16,40,128]{2,1,0:T(8,128)}), f32[16,40,128]{2,1,0:T(8,128)S(1)}, u32[]{:S(2)}, u32[]{:S(2)}) %all-to-all-start.1) | async-done | bytes 327712 | tf_op jit(solution)/shard_map/all_to_all | solution.py:137
  49.5 0.3 copy.38
  50.2 0.7 copy-done.3
  50.9 0.8 slice-done.1
  51.9 2.6 %collective-permute-start.1 = (f32[32,7,160]{2,1,0:T(8,128)S(1)}, f32[32,7,160]{2,1,0:T(8,128)S(1)}, u32[]{:S(2)}, u32[]{:S(2)}) collective-permute-start(f32[32,7,160]{2,1,0:T(8,128)S(1)} %get-tuple-element.22), channel_id=1, source_target_pairs={{16,0},{32,16},{48,32},{64,48},{80,64},{96,80},{112,96},{128,112},... | collective-permute-start | bytes 430088 | tf_op jit(solution)/shard_map/ppermute | solution.py:35
  54.5 1.9 %collective-permute-start = (f32[32,7,160]{2,1,0:T(8,128)S(1)}, f32[32,7,160]{2,1,0:T(8,128)S(1)}, u32[]{:S(2)}, u32[]{:S(2)}) collective-permute-start(f32[32,7,160]{2,1,0:T(8,128)S(1)} %get-tuple-element.21), channel_id=1, source_target_pairs={{0,16},{16,32},{32,48},{48,64},{64,80},{80,96},{96,112},{112,128},... | collective-permute-start | bytes 430088 | tf_op jit(solution)/shard_map/ppermute | solution.py:32
  56.5 0.6 copy-done.9
  57.1 0.6 fusion.84
  57.7 0.7 collective-permute-done.1
  58.4 5.9 %collective-permute-done = f32[32,7,160]{2,1,0:T(8,128)S(1)} collective-permute-done((f32[32,7,160]{2,1,0:T(8,128)S(1)}, f32[32,7,160]{2,1,0:T(8,128)S(1)}, u32[]{:S(2)}, u32[]{:S(2)}) %collective-permute-start) | collective-permute-done | bytes 143392 | tf_op jit(solution)/shard_map/ppermute | solution.py:32
  64.5 1.0 fusion.8
  65.6 0.4 fusion.13
  65.9 0.4 fusion.18
  66.4 1.0 fusion.23
  67.4 0.4 fusion.28
  67.8 0.4 pad_slice_fusion.13
  69.0 0.8 reshape.242
  69.7 0.3 copy.81
  70.1 0.5 reshape.243
  70.6 17.7 %all_to_all.21 = f32[16,55,128]{2,1,0:T(8,128)S(1)} all-to-all(f32[16,55,128]{2,1,0:T(8,128)S(1)} %reshape.243), channel_id=1, replica_groups=mesh['axial'=16,'azim'=16] {'azim'}, dimensions={0} | all-to-all | bytes 901120 | tf_op jit(solution)/shard_map/all_to_all | solution.py:131
  88.3 0.8 reshape.244
  89.1 1.0 fusion.86
  90.0 1.3 reshape.245
  91.3 3.6 %all-to-all-start.3 = ((f32[16,55,128]{2,1,0:T(8,128)}), f32[16,55,128]{2,1,0:T(8,128)S(1)}, u32[]{:S(2)}, u32[]{:S(2)}) async-start(f32[16,55,128]{2,1,0:T(8,128)} %reshape.245), calls=%async_computation.3 | async-start | bytes 917504 | tf_op jit(solution)/shard_map/all_to_all | solution.py:137
  95.0 0.6 copy-done.10
  95.7 0.7 copy-done.11
  96.3 13.1 %all-to-all-done.3 = f32[16,55,128]{2,1,0:T(8,128)S(1)} async-done(((f32[16,55,128]{2,1,0:T(8,128)}), f32[16,55,128]{2,1,0:T(8,128)S(1)}, u32[]{:S(2)}, u32[]{:S(2)}) %all-to-all-start.3) | async-done | bytes 450592 | tf_op jit(solution)/shard_map/all_to_all | solution.py:137
  109.4 0.8 reshape.246
  110.2 0.3 copy.41
  110.5 0.3 reshape.247
  111.0 0.6 copy-done.2
  111.7 0.9 slice-done
  112.7 0.8 copy-done.5
  113.5 0.3 subtract_multiply_fusion.1
  114.2 0.9 fusion.47
  115.4 0.4 convolution_bitcast_fusion
  116.0 0.3 convolution_bitcast_fusion.1
  116.4 5.5 %collective-permute-start.3 = (f32[2,32,16,128]{3,1,2,0:T(8,128)S(1)}, f32[2,32,16,128]{3,1,2,0:T(8,128)S(1)}, u32[]{:S(2)}, u32[]{:S(2)}) collective-permute-start(f32[2,32,16,128]{3,1,2,0:T(8,128)S(1)} %pad_maximum_fusion.2), channel_id=1, source_target_pairs={{16,0},{32,16},{48,32},{64,48},{80,64},{96,80},{112,96},{128,112},... | collective-permute-start | bytes 1572872 | tf_op jit(solution)/shard_map/ppermute | solution.py:43
  121.9 0.3 convolution_bitcast_fusion.2
  122.3 0.3 convolution_bitcast_fusion.3
  122.7 2.1 %collective-permute-start.2 = (f32[2,32,16,128]{3,1,2,0:T(8,128)S(1)}, f32[2,32,16,128]{3,1,2,0:T(8,128)S(1)}, u32[]{:S(2)}, u32[]{:S(2)}) collective-permute-start(f32[2,32,16,128]{3,1,2,0:T(8,128)S(1)} %pad_maximum_fusion.1), channel_id=1, source_target_pairs={{0,16},{16,32},{32,48},{48,64},{64,80},{80,96},{96,112},{112,128},... | collective-permute-start | bytes 1572872 | tf_op jit(solution)/shard_map/ppermute | solution.py:43
  124.8 0.7 slice.289
  125.5 3.0 %collective-permute-done.3 = f32[2,32,16,128]{3,1,2,0:T(8,128)S(1)} collective-permute-done((f32[2,32,16,128]{3,1,2,0:T(8,128)S(1)}, f32[2,32,16,128]{3,1,2,0:T(8,128)S(1)}, u32[]{:S(2)}, u32[]{:S(2)}) %collective-permute-start.3) | collective-permute-done | bytes 524320 | tf_op jit(solution)/shard_map/ppermute | solution.py:43
  128.6 6.7 %collective-permute-done.2 = f32[2,32,16,128]{3,1,2,0:T(8,128)S(1)} collective-permute-done((f32[2,32,16,128]{3,1,2,0:T(8,128)S(1)}, f32[2,32,16,128]{3,1,2,0:T(8,128)S(1)}, u32[]{:S(2)}, u32[]{:S(2)}) %collective-permute-start.2) | collective-permute-done | bytes 524320 | tf_op jit(solution)/shard_map/ppermute | solution.py:43
  135.3 0.4 fusion.37
  135.6 0.3 reshape.250
  136.0 1.9 %fusion.2 = f32[32,16,2,64]{3,1,2,0:T(8,128)S(1)} fusion(f32[32,64,64]{2,1,0:T(8,128)S(1)} %copy-done, f32[32,16,2,64]{3,2,0,1:T(2,128)S(1)} %reshape.250), kind=kOutput, calls=%fused_computation.19 | convolution fusion | flops 50331648 | bytes 1048576 | tf_op jit(solution)/shard_map/aqr,azcr->azcq/dot_general | solution.py:253
  137.9 0.3 copy.48
  138.2 0.3 reshape.251
  138.5 0.3 fusion.35
  138.8 0.3 reshape.252
  139.2 1.9 %fusion = f32[32,16,2,64]{3,1,2,0:T(8,128)S(1)} fusion(f32[32,64,64]{2,1,0:T(8,128)S(1)} %copy-done, f32[32,16,2,64]{3,2,0,1:T(2,128)S(1)} %reshape.252), kind=kOutput, calls=%fused_computation.17 | convolution fusion | flops 50331648 | bytes 1048576 | tf_op jit(solution)/shard_map/aqr,azcr->azcq/dot_general | solution.py:253
  141.4 0.3 reshape.253
  141.7 0.6 copy-done.6
  142.5 1.2 multiply_add_fusion.2
  (60 shorter events, 4.4 us)
Async XLA Ops:
  0.6 135.3 %copy-start = (f32[32,64,64]{2,1,0:T(8,128)S(1)}, f32[32,64,64]{2,1,0:T(8,128)}, u32[]{:S(2)}) copy-start(f32[32,64,64]{2,1,0:T(8,128)} %param.15) | copy-start | bytes 1572868
  1.8 1.0 copy-start.4
  3.5 25.3 %copy-start.1 = (f32[512,512]{1,0:T(8,128)S(1)}, f32[512,512]{1,0:T(8,128)}, u32[]{:S(2)}) copy-start(f32[512,512]{1,0:T(8,128)} %constant.58.clone) | copy-start | bytes 3145732
  31.7 17.6 %all-to-all-start.1 = ((f32[16,40,128]{2,1,0:T(8,128)}), f32[16,40,128]{2,1,0:T(8,128)S(1)}, u32[]{:S(2)}, u32[]{:S(2)}) async-start(f32[16,40,128]{2,1,0:T(8,128)} %reshape.235), calls=%async_computation.1 | async-start | bytes 655360 | tf_op jit(solution)/shard_map/all_to_all | solution.py:137
  50.1 0.7 copy-start.3
  50.9 0.8 slice-start.1
  51.9 6.4 %collective-permute-start.1 = (f32[32,7,160]{2,1,0:T(8,128)S(1)}, f32[32,7,160]{2,1,0:T(8,128)S(1)}, u32[]{:S(2)}, u32[]{:S(2)}) collective-permute-start(f32[32,7,160]{2,1,0:T(8,128)S(1)} %get-tuple-element.22), channel_id=1, source_target_pairs={{16,0},{32,16},{48,32},{64,48},{80,64},{96,80},{112,96},{128,112},... | collective-permute-start | bytes 430088 | tf_op jit(solution)/shard_map/ppermute | solution.py:35
  54.5 9.8 %collective-permute-start = (f32[32,7,160]{2,1,0:T(8,128)S(1)}, f32[32,7,160]{2,1,0:T(8,128)S(1)}, u32[]{:S(2)}, u32[]{:S(2)}) collective-permute-start(f32[32,7,160]{2,1,0:T(8,128)S(1)} %get-tuple-element.21), channel_id=1, source_target_pairs={{0,16},{16,32},{32,48},{48,64},{64,80},{80,96},{96,112},{112,128},... | collective-permute-start | bytes 430088 | tf_op jit(solution)/shard_map/ppermute | solution.py:32
  56.4 0.7 copy-start.9
  91.3 18.1 %all-to-all-start.3 = ((f32[16,55,128]{2,1,0:T(8,128)}), f32[16,55,128]{2,1,0:T(8,128)S(1)}, u32[]{:S(2)}, u32[]{:S(2)}) async-start(f32[16,55,128]{2,1,0:T(8,128)} %reshape.245), calls=%async_computation.3 | async-start | bytes 917504 | tf_op jit(solution)/shard_map/all_to_all | solution.py:137
  95.0 0.7 copy-start.10
  95.7 0.7 copy-start.11
  110.8 0.8 copy-start.2
  111.6 0.9 slice-start
  112.5 0.9 copy-start.5
  116.4 12.2 %collective-permute-start.3 = (f32[2,32,16,128]{3,1,2,0:T(8,128)S(1)}, f32[2,32,16,128]{3,1,2,0:T(8,128)S(1)}, u32[]{:S(2)}, u32[]{:S(2)}) collective-permute-start(f32[2,32,16,128]{3,1,2,0:T(8,128)S(1)} %pad_maximum_fusion.2), channel_id=1, source_target_pairs={{16,0},{32,16},{48,32},{64,48},{80,64},{96,80},{112,96},{128,112},... | collective-permute-start | bytes 1572872 | tf_op jit(solution)/shard_map/ppermute | solution.py:43
  122.7 12.6 %collective-permute-start.2 = (f32[2,32,16,128]{3,1,2,0:T(8,128)S(1)}, f32[2,32,16,128]{3,1,2,0:T(8,128)S(1)}, u32[]{:S(2)}, u32[]{:S(2)}) collective-permute-start(f32[2,32,16,128]{3,1,2,0:T(8,128)S(1)} %pad_maximum_fusion.1), channel_id=1, source_target_pairs={{0,16},{16,32},{32,48},{48,64},{64,80},{80,96},{96,112},{112,128},... | collective-permute-start | bytes 1572872 | tf_op jit(solution)/shard_map/ppermute | solution.py:43
  141.4 1.0 copy-start.6
  141.4 1.0 copy-start.7
  141.4 1.1 copy-start.8

commit v3 on v2

--- a/solution.py
+++ b/solution.py
@@ -220,40 +220,37 @@
         fields.append(flat[:, offset : offset + size].reshape(shape))
         offset += size
 
-    slot_range = jnp.arange(local_count, dtype=jnp.int32)
     previous = potential[..., window]
-    same, upward, downward = [], [], []
+    tiles = []
     for step_index in range(STEPS):
         padded = fields[step_index]
         if step_index == STEPS - 1:
             field_out = padded[:, 1:-1]
             padded = padded[..., window]
-        tiles = lorentz_window(padded, previous, conduct[window], radius[window])
+        tiles.append(lorentz_window(padded, previous, conduct[window], radius[window]))
         previous = padded[:, 1:-1]
-        slot_table = (relay_slot[step_index, :, 0][:, None] == slot_range[None, :]).astype(
-            jnp.float32
-        )
-        owner_now = relay_owner[step_index, :, 0]
-
-        def place(target):
-            chosen = (owner_now == target).astype(jnp.float32)
-            return jnp.einsum(
-                "jcw,jp->pcw", tiles * chosen[:, None, None], slot_table, precision=HIGH
-            )
-
-        same.append(place(1))
-        upward.append(place(2))
-        downward.append(place(0))
-    from_below = shifted(jnp.stack(upward), "axial", 1)
-    from_above = shifted(jnp.stack(downward), "axial", -1)
+    tiles = jnp.stack(tiles)
+
+    slot_range = jnp.arange(local_count, dtype=jnp.int32)
+    slot_table = relay_slot[:, :, 0][:, :, None] == slot_range[None, None, :]
+    owner_at = jnp.sum(jnp.where(slot_table, relay_owner[:, :, 0][:, :, None], 0), axis=1)
+    moved = jnp.einsum(
+        "sjcw,sjp->spcw", tiles, slot_table.astype(jnp.float32), precision=HIGH
+    )
+
+    def place(target):
+        return jnp.where((owner_at == target)[:, :, None, None], moved, 0.0)
+
+    from_below = shifted(place(2), "axial", 1)
+    from_above = shifted(place(0), "axial", -1)
+    received = (place(1) + from_below + from_above).reshape(
+        STEPS, local_count, axial_cells, 2, band_width
+    )
+    loads = jnp.einsum("aqr,sazcr->sazcq", tile_weight, received, precision=HIGH).reshape(
+        STEPS, local_count, axial_cells, 2 * band_width
+    )
     for step_index in range(STEPS):
-        received = (same[step_index] + from_below[step_index] + from_above[step_index]).reshape(
-            local_count, axial_cells, 2, band_width
-        )
-        load = jnp.einsum("aqr,azcr->azcq", tile_weight, received, precision=HIGH).reshape(
-            local_count, axial_cells, 2 * band_width
-        )
-        velocity, strain, plastic = plastic_update(load, velocity, strain, plastic)
+        velocity, strain, plastic = plastic_update(loads[step_index], velocity, strain, plastic)
     return (field_out, velocity, strain, plastic)
 
 

time: 144 us -> 143 us (level); the launches traced: 144 us -> 140 us
  waiting for transfers between devices: 43.3 us -> 36 us
  starting transfers between devices: 19.2 us -> 22.6 us
  blocking collectives: 42.3 us -> 45.5 us
  matrix products: 8.74 us -> 5.55 us
    ppermute x1, waiting for transfers between devices: 5.93 us -> 0.84 us  [with_halo(): lax.ppermute(lax.slice_in_dim(block, block.shape[dim] - width, None, axis...]
    ppermute x2, waiting for transfers between devices: 9.73 us -> 5.95 us  [shifted(): return lax.ppermute(array, axis, pairs)]
    ppermute x1, starting transfers between devices: 2.55 us -> 5.75 us  [with_halo(): lax.ppermute(lax.slice_in_dim(block, 0, width, axis=dim), axis, backward)]
    dot_general x8 -> x2, matrix products: 5.95 us -> 2.75 us  [the longest x1 2.33 us: shards(): jnp.einsum('aqr,sazcr->sazcq', tile_weight, received, precision=HIGH)]
    all_to_all x2, blocking collectives: 42.3 us -> 45.5 us  [transform(): lax.all_to_all(blocks, 'azim', 0, 0, tiled=True)]
    unnamed x29 -> x45, local copies, waits for them, and re-layouts: 5.76 us -> 5.8 us
where the time goes in v3:
time: 143 us; the launch traced here: 140 us
  blocking collectives  45.5 us (32%)
  waiting for transfers between devices  36 us (25%)
  starting transfers between devices  22.6 us (16%)
  local copies, waits for them, and re-layouts  20.9 us (15%)
  other arithmetic  8.52 us (6%)
  matrix products  5.55 us (4%)
    all_to_all x2, blocking collectives, transform(): lax.all_to_all(blocks, 'azim', 0, 0, tiled=True)  45.5 us
    all_to_all x2, waiting for transfers between devices, transform(): joined = lax.all_to_all(mixed.reshape(dense), 'azim', 0, 0, tiled=True)  27.4 us
    ppermute x2, starting transfers between devices, shifted(): return lax.ppermute(array, axis, pairs)  7.67 us
    all_to_all x2, starting transfers between devices, transform(): joined = lax.all_to_all(mixed.reshape(dense), 'azim', 0, 0, tiled=True)  7.24 us
    ppermute x2, waiting for transfers between devices, shifted(): return lax.ppermute(array, axis, pairs)  5.95 us
    unnamed x45, local copies, waits for them, and re-layouts  5.8 us
    ppermute x1, starting transfers between devices, with_halo(): lax.ppermute(lax.slice_in_dim(block, 0, width, axis=dim), axis, backward)  5.75 us
    select_n x5, other arithmetic, shards(): iterate = jnp.where(inside, (right_side + nearby) / diagonal_term, 0.0)  3.15 us
  transfers between devices with their start and end apart: 6, of which 6 were waited for; matrix products, arithmetic and copies ran while one was open for 2% of the time, Pallas kernels for 0%

profile of v3, /device:TPU:2, one launch (start us, length us, event | category | flops | bytes accessed | tf_op | source)
XLA Modules:
  0.0 140.4 jit_solution(11922501172069452210)
XLA Ops:
  0.6 1.2 convert_multiply_fusion
  2.0 0.8 copy-done.2
  2.9 0.3 reshape.175
  3.2 0.3 copy.32
  3.5 0.4 reshape.176
  3.9 24.6 %all_to_all.20 = f32[16,40,128]{2,1,0:T(8,128)S(1)} all-to-all(f32[16,40,128]{2,1,0:T(8,128)S(1)} %reshape.176), channel_id=1, replica_groups=mesh['axial'=16,'azim'=16] {'azim'}, dimensions={0} | all-to-all | bytes 655360 | tf_op jit(solution)/shard_map/all_to_all | solution.py:131
  28.5 0.2 reshape.177
  28.8 1.8 %fusion.57 = f32[512,160]{1,0:T(8,128)S(1)} fusion(f32[512,512]{1,0:T(8,128)S(1)} %copy-done.1, f32[512,160]{1,0:T(8,128)S(1)} %reshape.177), kind=kOutput, calls=%fused_computation.125 | convolution fusion | flops 503316480 | bytes 1703936 | tf_op jit(solution)/shard_map/dot_general | solution.py:133
  30.6 1.1 reshape.178
  31.7 3.5 %all-to-all-start.1 = ((f32[16,40,128]{2,1,0:T(8,128)}), f32[16,40,128]{2,1,0:T(8,128)S(1)}, u32[]{:S(2)}, u32[]{:S(2)}) async-start(f32[16,40,128]{2,1,0:T(8,128)} %reshape.178), calls=%async_computation.1 | async-start | bytes 655360 | tf_op jit(solution)/shard_map/all_to_all | solution.py:137
  35.3 0.5 or_select_fusion
  35.8 0.5 copy-done.18
  36.4 12.9 %all-to-all-done.1 = f32[16,40,128]{2,1,0:T(8,128)S(1)} async-done(((f32[16,40,128]{2,1,0:T(8,128)}), f32[16,40,128]{2,1,0:T(8,128)S(1)}, u32[]{:S(2)}, u32[]{:S(2)}) %all-to-all-start.1) | async-done | bytes 327712 | tf_op jit(solution)/shard_map/all_to_all | solution.py:137
  49.3 0.2 reshape.179
  49.5 0.3 copy.34
  49.9 0.3 reshape.180
  50.5 1.9 %collective-permute-start = (f32[32,7,160]{2,1,0:T(8,128)S(1)}, f32[32,7,160]{2,1,0:T(8,128)S(1)}, u32[]{:S(2)}, u32[]{:S(2)}) collective-permute-start(f32[32,7,160]{2,1,0:T(8,128)S(1)} %get-tuple-element.23), channel_id=1, source_target_pairs={{0,16},{16,32},{32,48},{48,64},{64,80},{80,96},{96,112},{112,128},... | collective-permute-start | bytes 430088 | tf_op jit(solution)/shard_map/ppermute | solution.py:32
  52.4 5.8 %collective-permute-start.1 = (f32[32,7,160]{2,1,0:T(8,128)S(1)}, f32[32,7,160]{2,1,0:T(8,128)S(1)}, u32[]{:S(2)}, u32[]{:S(2)}) collective-permute-start(f32[32,7,160]{2,1,0:T(8,128)S(1)} %get-tuple-element.24), channel_id=1, source_target_pairs={{16,0},{32,16},{48,32},{64,48},{80,64},{96,80},{112,96},{128,112},... | collective-permute-start | bytes 430088 | tf_op jit(solution)/shard_map/ppermute | solution.py:35
  58.2 0.6 slice.265
  58.8 0.6 fusion.56
  59.4 0.8 collective-permute-done
  60.3 1.8 %collective-permute-done.1 = f32[32,7,160]{2,1,0:T(8,128)S(1)} collective-permute-done((f32[32,7,160]{2,1,0:T(8,128)S(1)}, f32[32,7,160]{2,1,0:T(8,128)S(1)}, u32[]{:S(2)}, u32[]{:S(2)}) %collective-permute-start.1) | collective-permute-done | bytes 143392 | tf_op jit(solution)/shard_map/ppermute | solution.py:35
  62.3 1.0 fusion.6
  63.3 0.4 fusion.11
  63.7 0.4 fusion.16
  64.1 1.1 fusion.21
  65.4 0.8 reshape.183
  66.2 0.7 copy-done.9
  66.9 0.3 fusion.26
  67.2 0.4 pad_slice_fusion.13
  67.6 0.6 copy-done.13
  68.3 0.2 fusion.33
  68.6 0.8 copy-done.4
  69.6 0.8 reshape.185
  70.4 0.3 copy.91
  70.7 0.5 reshape.186
  71.2 20.9 %all_to_all.21 = f32[16,55,128]{2,1,0:T(8,128)S(1)} all-to-all(f32[16,55,128]{2,1,0:T(8,128)S(1)} %reshape.186), channel_id=1, replica_groups=mesh['axial'=16,'azim'=16] {'azim'}, dimensions={0} | all-to-all | bytes 901120 | tf_op jit(solution)/shard_map/all_to_all | solution.py:131
  92.1 0.8 reshape.187
  92.8 1.0 fusion.58
  93.8 1.3 reshape.188
  95.1 3.7 %all-to-all-start.3 = ((f32[16,55,128]{2,1,0:T(8,128)}), f32[16,55,128]{2,1,0:T(8,128)S(1)}, u32[]{:S(2)}, u32[]{:S(2)}) async-start(f32[16,55,128]{2,1,0:T(8,128)} %reshape.188), calls=%async_computation.3 | async-start | bytes 917504 | tf_op jit(solution)/shard_map/all_to_all | solution.py:137
  99.1 0.5 copy-done.16
  99.8 0.6 copy-done.15
  100.5 14.6 %all-to-all-done.3 = f32[16,55,128]{2,1,0:T(8,128)S(1)} async-done(((f32[16,55,128]{2,1,0:T(8,128)}), f32[16,55,128]{2,1,0:T(8,128)S(1)}, u32[]{:S(2)}, u32[]{:S(2)}) %all-to-all-start.3) | async-done | bytes 450592 | tf_op jit(solution)/shard_map/all_to_all | solution.py:137
  115.1 0.8 reshape.189
  115.8 0.3 copy.37
  116.2 0.3 reshape.190
  117.5 0.3 fusion.45
  117.9 0.2 pad_slice_fusion.17
  118.1 0.7 fusion.43
  119.2 0.4 broadcast_select_fusion.1
  119.6 1.9 %collective-permute-start.2 = (f32[2,32,16,128]{3,1,2,0:T(8,128)S(1)}, f32[2,32,16,128]{3,1,2,0:T(8,128)S(1)}, u32[]{:S(2)}, u32[]{:S(2)}) collective-permute-start(f32[2,32,16,128]{3,1,2,0:T(8,128)S(1)} %get-tuple-element.17), channel_id=1, source_target_pairs={{0,16},{16,32},{32,48},{48,64},{64,80},{80,96},{96,112},{112,128},... | collective-permute-start | bytes 1572872 | tf_op jit(solution)/shard_map/ppermute | solution.py:43
  121.5 5.8 %collective-permute-start.3 = (f32[2,32,16,128]{3,1,2,0:T(8,128)S(1)}, f32[2,32,16,128]{3,1,2,0:T(8,128)S(1)}, u32[]{:S(2)}, u32[]{:S(2)}) collective-permute-start(f32[2,32,16,128]{3,1,2,0:T(8,128)S(1)} %get-tuple-element.18), channel_id=1, source_target_pairs={{16,0},{32,16},{48,32},{64,48},{80,64},{96,80},{112,96},{128,112},... | collective-permute-start | bytes 1572872 | tf_op jit(solution)/shard_map/ppermute | solution.py:43
  127.3 0.7 slice.267
  128.0 4.2 %collective-permute-done.2 = f32[2,32,16,128]{3,1,2,0:T(8,128)S(1)} collective-permute-done((f32[2,32,16,128]{3,1,2,0:T(8,128)S(1)}, f32[2,32,16,128]{3,1,2,0:T(8,128)S(1)}, u32[]{:S(2)}, u32[]{:S(2)}) %collective-permute-start.2) | collective-permute-done | bytes 524320 | tf_op jit(solution)/shard_map/ppermute | solution.py:43
  132.2 1.8 %collective-permute-done.3 = f32[2,32,16,128]{3,1,2,0:T(8,128)S(1)} collective-permute-done((f32[2,32,16,128]{3,1,2,0:T(8,128)S(1)}, f32[2,32,16,128]{3,1,2,0:T(8,128)S(1)}, u32[]{:S(2)}, u32[]{:S(2)}) %collective-permute-start.3) | collective-permute-done | bytes 524320 | tf_op jit(solution)/shard_map/ppermute | solution.py:43
  134.2 0.6 reshape.193
  134.8 2.3 %convolution_bitcast_fusion = f32[2,32,16,2,64]{4,2,3,0,1:T(8,128)S(1)} fusion(f32[32,64,64]{2,1,0:T(8,128)S(1)} %copy-done, f32[2,32,16,2,64]{4,3,1,2,0:T(2,128)S(1)} %reshape.193), kind=kOutput, calls=%fused_computation | convolution fusion | flops 100663296 | bytes 1572864 | tf_op jit(solution)/shard_map/aqr,sazcr->sazcq/dot_general | solution.py:249
  137.2 0.3 copy.47
  137.5 0.3 squeeze.15
  137.8 0.3 copy.46
  138.1 0.3 squeeze.14
  138.4 0.6 copy-done.5
  139.2 1.2 multiply_add_fusion.2
  (72 shorter events, 3.8 us)
Async XLA Ops:
  0.6 134.2 %copy-start = (f32[32,64,64]{2,1,0:T(8,128)S(1)}, f32[32,64,64]{2,1,0:T(8,128)}, u32[]{:S(2)}) copy-start(f32[32,64,64]{2,1,0:T(8,128)} %param.15) | copy-start | bytes 1572868
  1.8 1.0 copy-start.2
  3.5 25.3 %copy-start.1 = (f32[512,512]{1,0:T(8,128)S(1)}, f32[512,512]{1,0:T(8,128)}, u32[]{:S(2)}) copy-start(f32[512,512]{1,0:T(8,128)} %constant.59.clone) | copy-start | bytes 3145732
  31.7 17.6 %all-to-all-start.1 = ((f32[16,40,128]{2,1,0:T(8,128)}), f32[16,40,128]{2,1,0:T(8,128)S(1)}, u32[]{:S(2)}, u32[]{:S(2)}) async-start(f32[16,40,128]{2,1,0:T(8,128)} %reshape.178), calls=%async_computation.1 | async-start | bytes 655360 | tf_op jit(solution)/shard_map/all_to_all | solution.py:137
  35.3 28.8 %copy-start.14 = (f32[128]{0:T(128)}, f32[128]{0:T(128)S(1)}, u32[]{:S(2)}) copy-start(f32[128]{0:T(128)S(1)} %and_select_fusion) | copy-start | bytes 1540
  35.8 0.5 copy-start.18
  50.5 9.8 %collective-permute-start = (f32[32,7,160]{2,1,0:T(8,128)S(1)}, f32[32,7,160]{2,1,0:T(8,128)S(1)}, u32[]{:S(2)}, u32[]{:S(2)}) collective-permute-start(f32[32,7,160]{2,1,0:T(8,128)S(1)} %get-tuple-element.23), channel_id=1, source_target_pairs={{0,16},{16,32},{32,48},{48,64},{64,80},{80,96},{96,112},{112,128},... | collective-permute-start | bytes 430088 | tf_op jit(solution)/shard_map/ppermute | solution.py:32
  52.4 9.6 %collective-permute-start.1 = (f32[32,7,160]{2,1,0:T(8,128)S(1)}, f32[32,7,160]{2,1,0:T(8,128)S(1)}, u32[]{:S(2)}, u32[]{:S(2)}) collective-permute-start(f32[32,7,160]{2,1,0:T(8,128)S(1)} %get-tuple-element.24), channel_id=1, source_target_pairs={{16,0},{32,16},{48,32},{64,48},{80,64},{96,80},{112,96},{128,112},... | collective-permute-start | bytes 430088 | tf_op jit(solution)/shard_map/ppermute | solution.py:35
  58.2 5.9 %copy-start.8 = (pred[30]{0:T(512)(128)(4,1)}, pred[30]{0:T(512)(128)(4,1)S(1)}, u32[]{:S(2)}) copy-start(pred[30]{0:T(512)(128)(4,1)S(1)} %compare_and_fusion) | copy-start | bytes 94
  58.2 0.7 copy-start.11
  64.1 1.1 copy-start.12
  66.2 0.7 copy-start.9
  67.6 0.7 copy-start.13
  67.6 0.7 copy-start.17
  68.5 0.9 copy-start.4
  95.1 3.7 %copy-start.19 = (f32[128]{0:T(128)S(1)}, f32[128]{0:T(128)}, u32[]{:S(2)}) copy-start(f32[128]{0:T(128)} %copy-done.18) | copy-start | bytes 1540
  95.1 3.8 %copy-start.3 = (f32[32,16,128]{2,1,0:T(8,128)S(1)}, f32[32,16,128]{2,1,0:T(8,128)}, u32[]{:S(2)}) copy-start(f32[32,16,128]{2,1,0:T(8,128)} %param.14) | copy-start | bytes 786436
  95.1 19.9 %all-to-all-start.3 = ((f32[16,55,128]{2,1,0:T(8,128)}), f32[16,55,128]{2,1,0:T(8,128)S(1)}, u32[]{:S(2)}, u32[]{:S(2)}) async-start(f32[16,55,128]{2,1,0:T(8,128)} %reshape.188), calls=%async_computation.3 | async-start | bytes 917504 | tf_op jit(solution)/shard_map/all_to_all | solution.py:137
  98.9 0.7 copy-start.16
  99.0 0.7 copy-start.10
  99.7 0.7 copy-start.15
  119.6 12.6 %collective-permute-start.2 = (f32[2,32,16,128]{3,1,2,0:T(8,128)S(1)}, f32[2,32,16,128]{3,1,2,0:T(8,128)S(1)}, u32[]{:S(2)}, u32[]{:S(2)}) collective-permute-start(f32[2,32,16,128]{3,1,2,0:T(8,128)S(1)} %get-tuple-element.17), channel_id=1, source_target_pairs={{0,16},{16,32},{32,48},{48,64},{64,80},{80,96},{96,112},{112,128},... | collective-permute-start | bytes 1572872 | tf_op jit(solution)/shard_map/ppermute | solution.py:43
  121.5 12.4 %collective-permute-start.3 = (f32[2,32,16,128]{3,1,2,0:T(8,128)S(1)}, f32[2,32,16,128]{3,1,2,0:T(8,128)S(1)}, u32[]{:S(2)}, u32[]{:S(2)}) collective-permute-start(f32[2,32,16,128]{3,1,2,0:T(8,128)S(1)} %get-tuple-element.18), channel_id=1, source_target_pairs={{16,0},{32,16},{48,32},{64,48},{80,64},{96,80},{112,96},{128,112},... | collective-permute-start | bytes 1572872 | tf_op jit(solution)/shard_map/ppermute | solution.py:43
  138.1 1.0 copy-start.5
  138.1 1.0 copy-start.6
  138.1 1.1 copy-start.7

commit v4 on v3

--- a/solution.py
+++ b/solution.py
@@ -131,7 +131,7 @@
     spread = lax.all_to_all(blocks, "azim", 0, 0, tiled=True).reshape(devices * rows, width)
     contract = 1 if inverse else 0
     mixed = lax.dot_general(
-        basis, spread, (((contract,), (0,)), ((), ())), precision=HIGH,
+        basis, spread, (((contract,), (0,)), ((), ())), precision=lax.Precision.HIGH,
         preferred_element_type=jnp.float32,
     )
     joined = lax.all_to_all(mixed.reshape(dense), "azim", 0, 0, tiled=True)
@@ -246,7 +246,9 @@
     received = (place(1) + from_below + from_above).reshape(
         STEPS, local_count, axial_cells, 2, band_width
     )
-    loads = jnp.einsum("aqr,sazcr->sazcq", tile_weight, received, precision=HIGH).reshape(
+    loads = jnp.einsum(
+        "aqr,sazcr->sazcq", tile_weight, received, precision=lax.Precision.HIGH
+    ).reshape(
         STEPS, local_count, axial_cells, 2 * band_width
     )
     for step_index in range(STEPS):

time: 143 us -> 140 us (0.979)
  matrix products: 5.55 us -> 3.46 us
where the time goes in v4:
time: 140 us; the launch traced here: 138 us
  blocking collectives  45.5 us (32%)
  waiting for transfers between devices  35.8 us (26%)
  starting transfers between devices  22.8 us (16%)
  local copies, waits for them, and re-layouts  20.9 us (15%)
  other arithmetic  8.52 us (6%)
  matrix products  3.46 us (2%)
    all_to_all x2, blocking collectives, transform(): lax.all_to_all(blocks, 'azim', 0, 0, tiled=True)  45.5 us
    all_to_all x2, waiting for transfers between devices, transform(): joined = lax.all_to_all(mixed.reshape(dense), 'azim', 0, 0, tiled=True)  27.3 us
    ppermute x2, starting transfers between devices, shifted(): return lax.ppermute(array, axis, pairs)  7.67 us
    all_to_all x2, starting transfers between devices, transform(): joined = lax.all_to_all(mixed.reshape(dense), 'azim', 0, 0, tiled=True)  7.42 us
    ppermute x2, waiting for transfers between devices, shifted(): return lax.ppermute(array, axis, pairs)  5.95 us
    unnamed x45, local copies, waits for them, and re-layouts  5.8 us
    ppermute x1, starting transfers between devices, with_halo(): lax.ppermute(lax.slice_in_dim(block, 0, width, axis=dim), axis, backward)  5.75 us
    select_n x5, other arithmetic, shards(): iterate = jnp.where(inside, (right_side + nearby) / diagonal_term, 0.0)  3.15 us
  transfers between devices with their start and end apart: 6, of which 6 were waited for; matrix products, arithmetic and copies ran while one was open for 2% of the time, Pallas kernels for 0%

profile of v4, /device:TPU:2, one launch (start us, length us, event | category | flops | bytes accessed | tf_op | source)
XLA Modules:
  0.0 138.3 jit_solution(2956908915765812576)
XLA Ops:
  0.6 1.2 convert_multiply_fusion
  2.0 0.8 copy-done.2
  2.9 0.3 reshape.175
  3.2 0.3 copy.32
  3.5 0.4 reshape.176
  3.9 24.6 %all_to_all.20 = f32[16,40,128]{2,1,0:T(8,128)S(1)} all-to-all(f32[16,40,128]{2,1,0:T(8,128)S(1)} %reshape.176), channel_id=1, replica_groups=mesh['axial'=16,'azim'=16] {'azim'}, dimensions={0} | all-to-all | bytes 655360 | tf_op jit(solution)/shard_map/all_to_all | solution.py:131
  28.5 0.2 reshape.177
  28.8 1.0 fusion.57
  29.8 1.1 reshape.178
  30.9 3.5 %all-to-all-start.1 = ((f32[16,40,128]{2,1,0:T(8,128)}), f32[16,40,128]{2,1,0:T(8,128)S(1)}, u32[]{:S(2)}, u32[]{:S(2)}) async-start(f32[16,40,128]{2,1,0:T(8,128)} %reshape.178), calls=%async_computation.1 | async-start | bytes 655360 | tf_op jit(solution)/shard_map/all_to_all | solution.py:137
  34.5 0.5 or_select_fusion
  35.0 0.5 copy-done.18
  35.6 12.9 %all-to-all-done.1 = f32[16,40,128]{2,1,0:T(8,128)S(1)} async-done(((f32[16,40,128]{2,1,0:T(8,128)}), f32[16,40,128]{2,1,0:T(8,128)S(1)}, u32[]{:S(2)}, u32[]{:S(2)}) %all-to-all-start.1) | async-done | bytes 327712 | tf_op jit(solution)/shard_map/all_to_all | solution.py:137
  48.5 0.2 reshape.179
  48.7 0.3 copy.34
  49.0 0.3 reshape.180
  49.6 1.9 %collective-permute-start = (f32[32,7,160]{2,1,0:T(8,128)S(1)}, f32[32,7,160]{2,1,0:T(8,128)S(1)}, u32[]{:S(2)}, u32[]{:S(2)}) collective-permute-start(f32[32,7,160]{2,1,0:T(8,128)S(1)} %get-tuple-element.23), channel_id=1, source_target_pairs={{0,16},{16,32},{32,48},{48,64},{64,80},{80,96},{96,112},{112,128},... | collective-permute-start | bytes 430088 | tf_op jit(solution)/shard_map/ppermute | solution.py:32
  51.6 5.8 %collective-permute-start.1 = (f32[32,7,160]{2,1,0:T(8,128)S(1)}, f32[32,7,160]{2,1,0:T(8,128)S(1)}, u32[]{:S(2)}, u32[]{:S(2)}) collective-permute-start(f32[32,7,160]{2,1,0:T(8,128)S(1)} %get-tuple-element.24), channel_id=1, source_target_pairs={{16,0},{32,16},{48,32},{64,48},{80,64},{96,80},{112,96},{128,112},... | collective-permute-start | bytes 430088 | tf_op jit(solution)/shard_map/ppermute | solution.py:35
  57.4 0.6 slice.265
  58.0 0.6 fusion.56
  58.6 0.8 collective-permute-done
  59.4 1.8 %collective-permute-done.1 = f32[32,7,160]{2,1,0:T(8,128)S(1)} collective-permute-done((f32[32,7,160]{2,1,0:T(8,128)S(1)}, f32[32,7,160]{2,1,0:T(8,128)S(1)}, u32[]{:S(2)}, u32[]{:S(2)}) %collective-permute-start.1) | collective-permute-done | bytes 143392 | tf_op jit(solution)/shard_map/ppermute | solution.py:35
  61.5 1.0 fusion.6
  62.5 0.4 fusion.11
  62.9 0.4 fusion.16
  63.3 1.1 fusion.21
  64.6 0.8 reshape.183
  65.4 0.7 copy-done.9
  66.1 0.3 fusion.26
  66.4 0.4 pad_slice_fusion.13
  66.8 0.6 copy-done.13
  67.5 0.2 fusion.33
  67.8 0.8 copy-done.4
  68.8 0.8 reshape.185
  69.6 0.3 copy.91
  69.9 0.5 reshape.186
  70.4 20.9 %all_to_all.21 = f32[16,55,128]{2,1,0:T(8,128)S(1)} all-to-all(f32[16,55,128]{2,1,0:T(8,128)S(1)} %reshape.186), channel_id=1, replica_groups=mesh['axial'=16,'azim'=16] {'azim'}, dimensions={0} | all-to-all | bytes 901120 | tf_op jit(solution)/shard_map/all_to_all | solution.py:131
  91.3 0.8 reshape.187
  92.0 0.6 fusion.58
  92.6 1.3 reshape.188
  93.9 3.9 %all-to-all-start.3 = ((f32[16,55,128]{2,1,0:T(8,128)}), f32[16,55,128]{2,1,0:T(8,128)S(1)}, u32[]{:S(2)}, u32[]{:S(2)}) async-start(f32[16,55,128]{2,1,0:T(8,128)} %reshape.188), calls=%async_computation.3 | async-start | bytes 917504 | tf_op jit(solution)/shard_map/all_to_all | solution.py:137
  98.0 0.5 copy-done.16
  98.8 0.6 copy-done.15
  99.5 14.4 %all-to-all-done.3 = f32[16,55,128]{2,1,0:T(8,128)S(1)} async-done(((f32[16,55,128]{2,1,0:T(8,128)}), f32[16,55,128]{2,1,0:T(8,128)S(1)}, u32[]{:S(2)}, u32[]{:S(2)}) %all-to-all-start.3) | async-done | bytes 450592 | tf_op jit(solution)/shard_map/all_to_all | solution.py:137
  113.8 0.8 reshape.189
  114.6 0.3 copy.37
  115.0 0.3 reshape.190
  116.3 0.3 fusion.45
  116.7 0.2 pad_slice_fusion.17
  116.9 0.7 fusion.43
  118.0 0.4 broadcast_select_fusion.1
  118.4 1.9 %collective-permute-start.2 = (f32[2,32,16,128]{3,1,2,0:T(8,128)S(1)}, f32[2,32,16,128]{3,1,2,0:T(8,128)S(1)}, u32[]{:S(2)}, u32[]{:S(2)}) collective-permute-start(f32[2,32,16,128]{3,1,2,0:T(8,128)S(1)} %get-tuple-element.17), channel_id=1, source_target_pairs={{0,16},{16,32},{32,48},{48,64},{64,80},{80,96},{96,112},{112,128},... | collective-permute-start | bytes 1572872 | tf_op jit(solution)/shard_map/ppermute | solution.py:43
  120.3 5.8 %collective-permute-start.3 = (f32[2,32,16,128]{3,1,2,0:T(8,128)S(1)}, f32[2,32,16,128]{3,1,2,0:T(8,128)S(1)}, u32[]{:S(2)}, u32[]{:S(2)}) collective-permute-start(f32[2,32,16,128]{3,1,2,0:T(8,128)S(1)} %get-tuple-element.18), channel_id=1, source_target_pairs={{16,0},{32,16},{48,32},{64,48},{80,64},{96,80},{112,96},{128,112},... | collective-permute-start | bytes 1572872 | tf_op jit(solution)/shard_map/ppermute | solution.py:43
  126.1 0.7 slice.267
  126.8 4.2 %collective-permute-done.2 = f32[2,32,16,128]{3,1,2,0:T(8,128)S(1)} collective-permute-done((f32[2,32,16,128]{3,1,2,0:T(8,128)S(1)}, f32[2,32,16,128]{3,1,2,0:T(8,128)S(1)}, u32[]{:S(2)}, u32[]{:S(2)}) %collective-permute-start.2) | collective-permute-done | bytes 524320 | tf_op jit(solution)/shard_map/ppermute | solution.py:43
  131.0 1.8 %collective-permute-done.3 = f32[2,32,16,128]{3,1,2,0:T(8,128)S(1)} collective-permute-done((f32[2,32,16,128]{3,1,2,0:T(8,128)S(1)}, f32[2,32,16,128]{3,1,2,0:T(8,128)S(1)}, u32[]{:S(2)}, u32[]{:S(2)}) %collective-permute-start.3) | collective-permute-done | bytes 524320 | tf_op jit(solution)/shard_map/ppermute | solution.py:43
  133.0 0.6 reshape.193
  133.6 1.4 %convolution_bitcast_fusion = f32[2,32,16,2,64]{4,2,3,0,1:T(8,128)S(1)} fusion(f32[32,64,64]{2,1,0:T(8,128)S(1)} %copy-done, f32[2,32,16,2,64]{4,3,1,2,0:T(2,128)S(1)} %reshape.193), kind=kOutput, calls=%fused_computation | convolution fusion | flops 50331648 | bytes 1572864 | tf_op jit(solution)/shard_map/aqr,sazcr->sazcq/dot_general | solution.py:249
  135.1 0.3 copy.47
  135.4 0.3 squeeze.15
  135.7 0.3 copy.46
  136.0 0.3 squeeze.14
  136.3 0.6 copy-done.5
  137.1 1.2 multiply_add_fusion.2
  (72 shorter events, 3.8 us)
Async XLA Ops:
  0.6 132.9 %copy-start = (f32[32,64,64]{2,1,0:T(8,128)S(1)}, f32[32,64,64]{2,1,0:T(8,128)}, u32[]{:S(2)}) copy-start(f32[32,64,64]{2,1,0:T(8,128)} %param.15) | copy-start | bytes 1572868
  1.8 1.0 copy-start.2
  3.5 25.3 %copy-start.1 = (f32[512,512]{1,0:T(8,128)S(1)}, f32[512,512]{1,0:T(8,128)}, u32[]{:S(2)}) copy-start(f32[512,512]{1,0:T(8,128)} %constant.59.clone) | copy-start | bytes 3145732
  30.9 17.6 %all-to-all-start.1 = ((f32[16,40,128]{2,1,0:T(8,128)}), f32[16,40,128]{2,1,0:T(8,128)S(1)}, u32[]{:S(2)}, u32[]{:S(2)}) async-start(f32[16,40,128]{2,1,0:T(8,128)} %reshape.178), calls=%async_computation.1 | async-start | bytes 655360 | tf_op jit(solution)/shard_map/all_to_all | solution.py:137
  34.5 28.8 %copy-start.14 = (f32[128]{0:T(128)}, f32[128]{0:T(128)S(1)}, u32[]{:S(2)}) copy-start(f32[128]{0:T(128)S(1)} %and_select_fusion) | copy-start | bytes 1540
  35.0 0.5 copy-start.18
  49.6 9.8 %collective-permute-start = (f32[32,7,160]{2,1,0:T(8,128)S(1)}, f32[32,7,160]{2,1,0:T(8,128)S(1)}, u32[]{:S(2)}, u32[]{:S(2)}) collective-permute-start(f32[32,7,160]{2,1,0:T(8,128)S(1)} %get-tuple-element.23), channel_id=1, source_target_pairs={{0,16},{16,32},{32,48},{48,64},{64,80},{80,96},{96,112},{112,128},... | collective-permute-start | bytes 430088 | tf_op jit(solution)/shard_map/ppermute | solution.py:32
  51.6 9.6 %collective-permute-start.1 = (f32[32,7,160]{2,1,0:T(8,128)S(1)}, f32[32,7,160]{2,1,0:T(8,128)S(1)}, u32[]{:S(2)}, u32[]{:S(2)}) collective-permute-start(f32[32,7,160]{2,1,0:T(8,128)S(1)} %get-tuple-element.24), channel_id=1, source_target_pairs={{16,0},{32,16},{48,32},{64,48},{80,64},{96,80},{112,96},{128,112},... | collective-permute-start | bytes 430088 | tf_op jit(solution)/shard_map/ppermute | solution.py:35
  57.4 5.9 %copy-start.8 = (pred[30]{0:T(512)(128)(4,1)}, pred[30]{0:T(512)(128)(4,1)S(1)}, u32[]{:S(2)}) copy-start(pred[30]{0:T(512)(128)(4,1)S(1)} %compare_and_fusion) | copy-start | bytes 94
  57.4 0.7 copy-start.11
  63.3 1.1 copy-start.12
  65.4 0.7 copy-start.9
  66.8 0.7 copy-start.13
  66.8 0.7 copy-start.17
  67.7 0.9 copy-start.4
  93.9 3.9 %copy-start.19 = (f32[128]{0:T(128)S(1)}, f32[128]{0:T(128)}, u32[]{:S(2)}) copy-start(f32[128]{0:T(128)} %copy-done.18) | copy-start | bytes 1540
  93.9 4.0 %copy-start.3 = (f32[32,16,128]{2,1,0:T(8,128)S(1)}, f32[32,16,128]{2,1,0:T(8,128)}, u32[]{:S(2)}) copy-start(f32[32,16,128]{2,1,0:T(8,128)} %param.14) | copy-start | bytes 786436
  93.9 19.9 %all-to-all-start.3 = ((f32[16,55,128]{2,1,0:T(8,128)}), f32[16,55,128]{2,1,0:T(8,128)S(1)}, u32[]{:S(2)}, u32[]{:S(2)}) async-start(f32[16,55,128]{2,1,0:T(8,128)} %reshape.188), calls=%async_computation.3 | async-start | bytes 917504 | tf_op jit(solution)/shard_map/all_to_all | solution.py:137
  97.9 0.7 copy-start.16
  98.0 0.7 copy-start.10
  98.7 0.7 copy-start.15
  118.4 12.6 %collective-permute-start.2 = (f32[2,32,16,128]{3,1,2,0:T(8,128)S(1)}, f32[2,32,16,128]{3,1,2,0:T(8,128)S(1)}, u32[]{:S(2)}, u32[]{:S(2)}) collective-permute-start(f32[2,32,16,128]{3,1,2,0:T(8,128)S(1)} %get-tuple-element.17), channel_id=1, source_target_pairs={{0,16},{16,32},{32,48},{48,64},{64,80},{80,96},{96,112},{112,128},... | collective-permute-start | bytes 1572872 | tf_op jit(solution)/shard_map/ppermute | solution.py:43
  120.3 12.4 %collective-permute-start.3 = (f32[2,32,16,128]{3,1,2,0:T(8,128)S(1)}, f32[2,32,16,128]{3,1,2,0:T(8,128)S(1)}, u32[]{:S(2)}, u32[]{:S(2)}) collective-permute-start(f32[2,32,16,128]{3,1,2,0:T(8,128)S(1)} %get-tuple-element.18), channel_id=1, source_target_pairs={{16,0},{32,16},{48,32},{64,48},{80,64},{96,80},{112,96},{128,112},... | collective-permute-start | bytes 1572872 | tf_op jit(solution)/shard_map/ppermute | solution.py:43
  136.0 1.0 copy-start.5
  136.0 1.0 copy-start.6
  136.0 1.1 copy-start.7

commit v5 on v4

--- a/solution.py
+++ b/solution.py
@@ -195,6 +195,7 @@
     span = axial_cells + 2 * reach
     global_z = lax.axis_index("axial") * axial_cells - reach + jnp.arange(span, dtype=jnp.int32)
     inside = ((global_z >= 0) & (global_z < axial_cells * lax.axis_size("axial")))[None, :, None]
+    divisor = jnp.where(inside, diagonal_term, jnp.inf)
 
     weight = harmonic_weight(own_index, azim_total)[:, None, None]
     window = slice(band_start - 1, band_start + band_width + 1)
@@ -205,7 +206,7 @@
         for sweep_index in range(SWEEPS):
             axial_pad = jnp.pad(iterate, ((0, 0), (1, 1), (0, 0)))
             nearby = axial_pad[:, 2:] + axial_pad[:, :-2] + radial_sum(iterate)
-            iterate = jnp.where(inside, (right_side + nearby) / diagonal_term, 0.0)
+            iterate = (right_side + nearby) / divisor
         planes = iterate[:, reach - 1 : reach + axial_cells + 1] * weight
         kept.append(planes if step_index == STEPS - 1 else planes[..., window])
     pieces = [piece.shape for piece in kept]
@@ -243,14 +244,16 @@
 
     from_below = shifted(place(2), "axial", 1)
     from_above = shifted(place(0), "axial", -1)
-    received = (place(1) + from_below + from_above).reshape(
-        STEPS, local_count, axial_cells, 2, band_width
-    )
-    loads = jnp.einsum(
-        "aqr,sazcr->sazcq", tile_weight, received, precision=lax.Precision.HIGH
-    ).reshape(
-        STEPS, local_count, axial_cells, 2 * band_width
-    )
+    received = place(1) + from_below + from_above
+    blank = jnp.zeros_like(tile_weight)
+    paired = jnp.concatenate(
+        [
+            jnp.concatenate([tile_weight, blank], axis=2),
+            jnp.concatenate([blank, tile_weight], axis=2),
+        ],
+        axis=1,
+    )
+    loads = jnp.einsum("aqr,sazr->sazq", paired, received, precision=lax.Precision.HIGH)
     for step_index in range(STEPS):
         velocity, strain, plastic = plastic_update(loads[step_index], velocity, strain, plastic)
     return (field_out, velocity, strain, plastic)

time: 140 us -> 135 us (0.964)
  local copies, waits for them, and re-layouts: 20.9 us -> 13.3 us
  waiting for transfers between devices: 35.8 us -> 38.7 us
    unnamed x45 -> x23, local copies, waits for them, and re-layouts: 5.8 us -> 1.31 us
    div x0 -> x5, other arithmetic: none -> 3.19 us  [shards(): iterate = (right_side + nearby) / divisor]
    select_n x5 -> x0, other arithmetic: 3.15 us -> none  [shards(): iterate = jnp.where(inside, (right_side + nearby) / diagonal_term, 0.0)]
    all_to_all x2, waiting for transfers between devices: 27.3 us -> 29.5 us  [transform(): joined = lax.all_to_all(mixed.reshape(dense), 'azim', 0, 0, tiled=True)]
  transfers between devices with their start and end apart: 6 -> 6, of which waited for: 6 -> 6; matrix products, arithmetic and copies ran while one was open for 2% -> 1% of each run, Pallas kernels for 0% -> 0%
where the time goes in v5:
time: 135 us; the launch traced here: 133 us
  blocking collectives  45.5 us (34%)
  waiting for transfers between devices  38.7 us (29%)
  starting transfers between devices  22.6 us (17%)
  local copies, waits for them, and re-layouts  13.3 us (10%)
  other arithmetic  8.04 us (6%)
  matrix products  3.85 us (3%)
    all_to_all x2, blocking collectives, transform(): lax.all_to_all(blocks, 'azim', 0, 0, tiled=True)  45.5 us
    all_to_all x2, waiting for transfers between devices, transform(): joined = lax.all_to_all(mixed.reshape(dense), 'azim', 0, 0, tiled=True)  29.5 us
    ppermute x2, starting transfers between devices, shifted(): return lax.ppermute(array, axis, pairs)  7.67 us
    all_to_all x2, starting transfers between devices, transform(): joined = lax.all_to_all(mixed.reshape(dense), 'azim', 0, 0, tiled=True)  7.28 us
    ppermute x2, waiting for transfers between devices, shifted(): return lax.ppermute(array, axis, pairs)  5.95 us
    ppermute x1, starting transfers between devices, with_halo(): lax.ppermute(lax.slice_in_dim(block, 0, width, axis=dim), axis, backward)  5.75 us
    div x5, other arithmetic, shards(): iterate = (right_side + nearby) / divisor  3.19 us
  transfers between devices with their start and end apart: 6, of which 6 were waited for; matrix products, arithmetic and copies ran while one was open for 1% of the time, Pallas kernels for 0%

profile of v5, /device:TPU:2, one launch (start us, length us, event | category | flops | bytes accessed | tf_op | source)
XLA Modules:
  0.0 133.3 jit_solution(13801606395510338885)
XLA Ops:
  0.6 1.1 convert_multiply_fusion
  1.8 0.1 reshape.166
  2.0 0.3 reshape.167
  2.3 0.3 copy.32
  2.6 0.4 reshape.168
  3.0 24.6 %all_to_all.20 = f32[16,40,128]{2,1,0:T(8,128)S(1)} all-to-all(f32[16,40,128]{2,1,0:T(8,128)S(1)} %reshape.168), channel_id=1, replica_groups=mesh['axial'=16,'azim'=16] {'azim'}, dimensions={0} | all-to-all | bytes 655360 | tf_op jit(solution)/shard_map/all_to_all | solution.py:131
  27.7 0.2 reshape.169
  27.9 1.0 fusion.64
  28.9 1.1 reshape.170
  30.1 3.5 %all-to-all-start.1 = ((f32[16,40,128]{2,1,0:T(8,128)}), f32[16,40,128]{2,1,0:T(8,128)S(1)}, u32[]{:S(2)}, u32[]{:S(2)}) async-start(f32[16,40,128]{2,1,0:T(8,128)} %reshape.170), calls=%async_computation.1 | async-start | bytes 655360 | tf_op jit(solution)/shard_map/all_to_all | solution.py:137
  33.7 13.9 %all-to-all-done.1 = f32[16,40,128]{2,1,0:T(8,128)S(1)} async-done(((f32[16,40,128]{2,1,0:T(8,128)}), f32[16,40,128]{2,1,0:T(8,128)S(1)}, u32[]{:S(2)}, u32[]{:S(2)}) %all-to-all-start.1) | async-done | bytes 327712 | tf_op jit(solution)/shard_map/all_to_all | solution.py:137
  47.6 0.2 reshape.171
  47.9 0.3 copy.34
  48.2 0.3 reshape.172
  48.8 1.9 %collective-permute-start = (f32[32,7,160]{2,1,0:T(8,128)S(1)}, f32[32,7,160]{2,1,0:T(8,128)S(1)}, u32[]{:S(2)}, u32[]{:S(2)}) collective-permute-start(f32[32,7,160]{2,1,0:T(8,128)S(1)} %get-tuple-element.21), channel_id=1, source_target_pairs={{0,16},{16,32},{32,48},{48,64},{64,80},{80,96},{96,112},{112,128},... | collective-permute-start | bytes 430088 | tf_op jit(solution)/shard_map/ppermute | solution.py:32
  50.7 5.8 %collective-permute-start.1 = (f32[32,7,160]{2,1,0:T(8,128)S(1)}, f32[32,7,160]{2,1,0:T(8,128)S(1)}, u32[]{:S(2)}, u32[]{:S(2)}) collective-permute-start(f32[32,7,160]{2,1,0:T(8,128)S(1)} %get-tuple-element.22), channel_id=1, source_target_pairs={{16,0},{32,16},{48,32},{64,48},{80,64},{96,80},{112,96},{128,112},... | collective-permute-start | bytes 430088 | tf_op jit(solution)/shard_map/ppermute | solution.py:35
  56.5 0.6 fusion.63
  57.1 1.5 %collective-permute-done = f32[32,7,160]{2,1,0:T(8,128)S(1)} collective-permute-done((f32[32,7,160]{2,1,0:T(8,128)S(1)}, f32[32,7,160]{2,1,0:T(8,128)S(1)}, u32[]{:S(2)}, u32[]{:S(2)}) %collective-permute-start) | collective-permute-done | bytes 143392 | tf_op jit(solution)/shard_map/ppermute | solution.py:32
  58.6 1.8 %collective-permute-done.1 = f32[32,7,160]{2,1,0:T(8,128)S(1)} collective-permute-done((f32[32,7,160]{2,1,0:T(8,128)S(1)}, f32[32,7,160]{2,1,0:T(8,128)S(1)}, u32[]{:S(2)}, u32[]{:S(2)}) %collective-permute-start.1) | collective-permute-done | bytes 143392 | tf_op jit(solution)/shard_map/ppermute | solution.py:35
  60.4 0.2 pad_maximum_fusion
  60.6 1.0 select_divide_fusion.4
  61.7 0.4 select_divide_fusion.3
  62.0 0.4 select_divide_fusion.2
  62.4 1.1 select_divide_fusion.1
  63.5 0.2 slice_multiply_fusion
  63.7 0.1 reshape.175
  63.9 0.4 select_divide_fusion
  64.2 0.4 pad_slice_fusion.13
  64.6 0.3 fusion.31
  65.0 0.1 select_maximum_fusion.1
  65.1 0.8 reshape.177
  65.9 0.3 copy.91
  66.2 0.5 reshape.178
  66.7 20.9 %all_to_all.21 = f32[16,55,128]{2,1,0:T(8,128)S(1)} all-to-all(f32[16,55,128]{2,1,0:T(8,128)S(1)} %reshape.178), channel_id=1, replica_groups=mesh['axial'=16,'azim'=16] {'azim'}, dimensions={0} | all-to-all | bytes 901120 | tf_op jit(solution)/shard_map/all_to_all | solution.py:131
  87.6 0.8 reshape.179
  88.4 0.6 fusion.65
  89.0 1.3 reshape.180
  90.3 3.7 %all-to-all-start.3 = ((f32[16,55,128]{2,1,0:T(8,128)}), f32[16,55,128]{2,1,0:T(8,128)S(1)}, u32[]{:S(2)}, u32[]{:S(2)}) async-start(f32[16,55,128]{2,1,0:T(8,128)} %reshape.180), calls=%async_computation.3 | async-start | bytes 917504 | tf_op jit(solution)/shard_map/all_to_all | solution.py:137
  94.1 0.1 slice.233
  94.5 15.6 %all-to-all-done.3 = f32[16,55,128]{2,1,0:T(8,128)S(1)} async-done(((f32[16,55,128]{2,1,0:T(8,128)}), f32[16,55,128]{2,1,0:T(8,128)S(1)}, u32[]{:S(2)}, u32[]{:S(2)}) %all-to-all-start.3) | async-done | bytes 450592 | tf_op jit(solution)/shard_map/all_to_all | solution.py:137
  110.1 0.8 reshape.181
  110.9 0.3 copy.37
  111.2 0.3 reshape.182
  111.5 0.1 slice.264
  111.7 0.2 reshape.184
  111.9 0.2 fusion.61
  112.1 0.1 slice.278
  112.3 0.2 fusion.62
  112.5 0.3 fusion.49
  112.7 0.2 pad_slice_fusion.15
  112.9 0.2 pad_slice_fusion.17
  113.2 0.7 fusion.47
  113.9 0.1 maximum_bitcast_fusion
  114.0 0.1 maximum_bitcast_fusion.1
  114.2 0.4 broadcast_select_fusion.1
  114.6 1.9 %collective-permute-start.2 = (f32[2,32,16,128]{3,1,2,0:T(8,128)S(1)}, f32[2,32,16,128]{3,1,2,0:T(8,128)S(1)}, u32[]{:S(2)}, u32[]{:S(2)}) collective-permute-start(f32[2,32,16,128]{3,1,2,0:T(8,128)S(1)} %get-tuple-element.15), channel_id=1, source_target_pairs={{0,16},{16,32},{32,48},{48,64},{64,80},{80,96},{96,112},{112,128},... | collective-permute-start | bytes 1572872 | tf_op jit(solution)/shard_map/ppermute | solution.py:43
  116.6 5.8 %collective-permute-start.3 = (f32[2,32,16,128]{3,1,2,0:T(8,128)S(1)}, f32[2,32,16,128]{3,1,2,0:T(8,128)S(1)}, u32[]{:S(2)}, u32[]{:S(2)}) collective-permute-start(f32[2,32,16,128]{3,1,2,0:T(8,128)S(1)} %get-tuple-element.16), channel_id=1, source_target_pairs={{16,0},{32,16},{48,32},{64,48},{80,64},{96,80},{112,96},{128,112},... | collective-permute-start | bytes 1572872 | tf_op jit(solution)/shard_map/ppermute | solution.py:43
  122.3 0.7 slice.265
  123.0 4.2 %collective-permute-done.2 = f32[2,32,16,128]{3,1,2,0:T(8,128)S(1)} collective-permute-done((f32[2,32,16,128]{3,1,2,0:T(8,128)S(1)}, f32[2,32,16,128]{3,1,2,0:T(8,128)S(1)}, u32[]{:S(2)}, u32[]{:S(2)}) %collective-permute-start.2) | collective-permute-done | bytes 524320 | tf_op jit(solution)/shard_map/ppermute | solution.py:43
  127.2 1.8 %collective-permute-done.3 = f32[2,32,16,128]{3,1,2,0:T(8,128)S(1)} collective-permute-done((f32[2,32,16,128]{3,1,2,0:T(8,128)S(1)}, f32[2,32,16,128]{3,1,2,0:T(8,128)S(1)}, u32[]{:S(2)}, u32[]{:S(2)}) %collective-permute-start.3) | collective-permute-done | bytes 524320 | tf_op jit(solution)/shard_map/ppermute | solution.py:43
  129.0 0.2 add_add_fusion
  129.2 1.0 copy-done.8
  130.2 1.8 %fusion.6 = f32[2,32,16,128]{3,2,0,1:T(8,128)S(1)} fusion(f32[32,64,64]{2,1,0:T(8,128)S(1)} %copy-done.8, f32[2,32,16,128]{3,1,2,0:T(8,128)S(1)} %add_add_fusion), kind=kOutput, calls=%fused_computation.20 | convolution fusion | flops 103284736 | bytes 1572864 | tf_op jit(solution)/shard_map/aqr,sazr->sazq/dot_general | solution.py:256
  132.1 1.2 multiply_add_fusion.2
  (43 shorter events, 1.1 us)
Async XLA Ops:
  0.6 1.3 copy-start.1
  2.6 25.3 %copy-start = (f32[512,512]{1,0:T(8,128)S(1)}, f32[512,512]{1,0:T(8,128)}, u32[]{:S(2)}) copy-start(f32[512,512]{1,0:T(8,128)} %constant.62.clone) | copy-start | bytes 3145732
  30.1 17.6 %all-to-all-start.1 = ((f32[16,40,128]{2,1,0:T(8,128)}), f32[16,40,128]{2,1,0:T(8,128)S(1)}, u32[]{:S(2)}, u32[]{:S(2)}) async-start(f32[16,40,128]{2,1,0:T(8,128)} %reshape.170), calls=%async_computation.1 | async-start | bytes 655360 | tf_op jit(solution)/shard_map/all_to_all | solution.py:137
  48.7 7.8 %copy-start.6 = (f32[2]{0:T(128)S(1)}, f32[2]{0:T(128)}, u32[]{:S(2)}) copy-start(f32[2]{0:T(128)} %param.13) | copy-start | bytes 28
  48.8 9.8 %collective-permute-start = (f32[32,7,160]{2,1,0:T(8,128)S(1)}, f32[32,7,160]{2,1,0:T(8,128)S(1)}, u32[]{:S(2)}, u32[]{:S(2)}) collective-permute-start(f32[32,7,160]{2,1,0:T(8,128)S(1)} %get-tuple-element.21), channel_id=1, source_target_pairs={{0,16},{16,32},{32,48},{48,64},{64,80},{80,96},{96,112},{112,128},... | collective-permute-start | bytes 430088 | tf_op jit(solution)/shard_map/ppermute | solution.py:32
  50.7 9.6 %collective-permute-start.1 = (f32[32,7,160]{2,1,0:T(8,128)S(1)}, f32[32,7,160]{2,1,0:T(8,128)S(1)}, u32[]{:S(2)}, u32[]{:S(2)}) collective-permute-start(f32[32,7,160]{2,1,0:T(8,128)S(1)} %get-tuple-element.22), channel_id=1, source_target_pairs={{16,0},{32,16},{48,32},{64,48},{80,64},{96,80},{112,96},{128,112},... | collective-permute-start | bytes 430088 | tf_op jit(solution)/shard_map/ppermute | solution.py:35
  89.0 5.3 %copy-start.5 = (s32[2,32,1]{1,2,0:T(1,128)S(1)}, s32[2,32,1]{1,2,0:T(1,128)}, u32[]{:S(2)}) copy-start(s32[2,32,1]{1,2,0:T(1,128)} %param.17) | copy-start | bytes 772
  89.0 5.3 %copy-start.7 = (s32[2,32,1]{1,2,0:T(1,128)S(1)}, s32[2,32,1]{1,2,0:T(1,128)}, u32[]{:S(2)}) copy-start(s32[2,32,1]{1,2,0:T(1,128)} %param.16) | copy-start | bytes 772
  90.3 19.8 %all-to-all-start.3 = ((f32[16,55,128]{2,1,0:T(8,128)}), f32[16,55,128]{2,1,0:T(8,128)S(1)}, u32[]{:S(2)}, u32[]{:S(2)}) async-start(f32[16,55,128]{2,1,0:T(8,128)} %reshape.180), calls=%async_computation.3 | async-start | bytes 917504 | tf_op jit(solution)/shard_map/all_to_all | solution.py:137
  114.6 12.6 %collective-permute-start.2 = (f32[2,32,16,128]{3,1,2,0:T(8,128)S(1)}, f32[2,32,16,128]{3,1,2,0:T(8,128)S(1)}, u32[]{:S(2)}, u32[]{:S(2)}) collective-permute-start(f32[2,32,16,128]{3,1,2,0:T(8,128)S(1)} %get-tuple-element.15), channel_id=1, source_target_pairs={{0,16},{16,32},{32,48},{48,64},{64,80},{80,96},{96,112},{112,128},... | collective-permute-start | bytes 1572872 | tf_op jit(solution)/shard_map/ppermute | solution.py:43
  116.6 12.4 %collective-permute-start.3 = (f32[2,32,16,128]{3,1,2,0:T(8,128)S(1)}, f32[2,32,16,128]{3,1,2,0:T(8,128)S(1)}, u32[]{:S(2)}, u32[]{:S(2)}) collective-permute-start(f32[2,32,16,128]{3,1,2,0:T(8,128)S(1)} %get-tuple-element.16), channel_id=1, source_target_pairs={{16,0},{32,16},{48,32},{64,48},{80,64},{96,80},{112,96},{128,112},... | collective-permute-start | bytes 1572872 | tf_op jit(solution)/shard_map/ppermute | solution.py:43
  129.0 1.2 copy-start.8
  130.2 1.8 %copy-start.2 = (f32[32,16,128]{2,1,0:T(8,128)S(1)}, f32[32,16,128]{2,1,0:T(8,128)}, u32[]{:S(2)}) copy-start(f32[32,16,128]{2,1,0:T(8,128)} %param.19) | copy-start | bytes 786436
  130.2 1.8 %copy-start.3 = (f32[32,16,128]{2,1,0:T(8,128)S(1)}, f32[32,16,128]{2,1,0:T(8,128)}, u32[]{:S(2)}) copy-start(f32[32,16,128]{2,1,0:T(8,128)} %param.20) | copy-start | bytes 786436
  130.2 1.8 %copy-start.4 = (f32[32,16,128]{2,1,0:T(8,128)S(1)}, f32[32,16,128]{2,1,0:T(8,128)}, u32[]{:S(2)}) copy-start(f32[32,16,128]{2,1,0:T(8,128)} %param.18) | copy-start | bytes 786436

commit v6 on v5

--- a/solution.py
+++ b/solution.py
@@ -119,23 +119,33 @@
     return table.astype(np.float32)
 
 
-def transform(flat, basis, inverse):
-    rows, count = flat.shape
-    devices = lax.axis_size("azim")
-    unit = devices * 128 // math.gcd(rows, 128)
+def transform(main, rest, basis, inverse):
+    devices, rows, lanes = main.shape
+    count = rest.shape[1]
+    unit = devices * lanes // math.gcd(rows, lanes)
     padded = -(-count // unit) * unit
-    flat = jnp.pad(flat, ((0, 0), (0, padded - count)))
     width = padded // devices
-    dense = (devices, rows * width // 128, 128)
-    blocks = flat.reshape(rows, devices, width).transpose(1, 0, 2).reshape(dense)
-    spread = lax.all_to_all(blocks, "azim", 0, 0, tiled=True).reshape(devices * rows, width)
+    packed = (devices, rows * width // lanes, lanes)
+    rest = jnp.pad(rest, ((0, 0), (0, padded - count)))
+    rest = rest.reshape(rows, devices, width).transpose(1, 0, 2).reshape(packed)
+    spread = lax.all_to_all(
+        jnp.concatenate([main, rest], axis=1), "azim", 0, 0, tiled=True
+    )
     contract = 1 if inverse else 0
-    mixed = lax.dot_general(
-        basis, spread, (((contract,), (0,)), ((), ())), precision=lax.Precision.HIGH,
-        preferred_element_type=jnp.float32,
-    )
-    joined = lax.all_to_all(mixed.reshape(dense), "azim", 0, 0, tiled=True)
-    return joined.reshape(devices, rows, width).transpose(1, 0, 2).reshape(rows, padded)[:, :count]
+
+    def mix(columns):
+        return lax.dot_general(
+            basis, columns, (((contract,), (0,)), ((), ())), precision=lax.Precision.HIGH,
+            preferred_element_type=jnp.float32,
+        )
+
+    mixed_main = mix(spread[:, :rows].reshape(devices * rows, lanes)).reshape(main.shape)
+    mixed_rest = mix(spread[:, rows:].reshape(devices * rows, width)).reshape(packed)
+    joined = lax.all_to_all(
+        jnp.concatenate([mixed_main, mixed_rest], axis=1), "azim", 0, 0, tiled=True
+    )
+    rest = joined[:, rows:].reshape(devices, rows, width).transpose(1, 0, 2)
+    return joined[:, :rows], rest.reshape(rows, padded)[:, :count]
 
 
 def lorentz_window(padded, previous, conduct, radius):
@@ -175,15 +185,13 @@
     basis = jnp.asarray(basis_constant(azim_total))
 
     coil = coil_density[..., :band_start] * coil_mask[..., :band_start].astype(jnp.float32)
-    flat = jnp.concatenate(
-        [potential.reshape(local_count, -1), coil.reshape(local_count, -1)], axis=1
-    )
-    modes = transform(flat, basis, inverse=False)
-    split_at = axial_cells * radial_cells
+    field_modes, coil_modes = transform(
+        potential.transpose(1, 0, 2), coil.reshape(local_count, -1), basis, inverse=False
+    )
     modes = jnp.concatenate(
         [
-            modes[:, :split_at].reshape(local_count, axial_cells, radial_cells),
-            modes[:, split_at:].reshape(local_count, axial_cells, band_start),
+            field_modes.transpose(1, 0, 2),
+            coil_modes.reshape(local_count, axial_cells, band_start),
         ],
         axis=-1,
     )
@@ -207,27 +215,31 @@
             axial_pad = jnp.pad(iterate, ((0, 0), (1, 1), (0, 0)))
             nearby = axial_pad[:, 2:] + axial_pad[:, :-2] + radial_sum(iterate)
             iterate = (right_side + nearby) / divisor
-        planes = iterate[:, reach - 1 : reach + axial_cells + 1] * weight
-        kept.append(planes if step_index == STEPS - 1 else planes[..., window])
-    pieces = [piece.shape for piece in kept]
-    flat = transform(
-        jnp.concatenate([piece.reshape(local_count, -1) for piece in kept], axis=1),
-        basis,
-        inverse=True,
-    )
-    fields, offset = [], 0
+        kept.append(iterate[:, reach - 1 : reach + axial_cells + 1] * weight)
+    last = kept[-1]
+    edges = jnp.concatenate([last[:, :1], last[:, -1:]], axis=1)[..., window]
+    pieces = [edges.shape] + [piece[..., window].shape for piece in kept[:-1]]
+    extra = jnp.concatenate(
+        [edges.reshape(local_count, -1)]
+        + [piece[..., window].reshape(local_count, -1) for piece in kept[:-1]],
+        axis=1,
+    )
+    planes, extra = transform(last[:, 1:-1].transpose(1, 0, 2), extra, basis, inverse=True)
+    field_out = planes.transpose(1, 0, 2)
+    unpacked, offset = [], 0
     for shape in pieces:
         size = math.prod(shape[1:])
-        fields.append(flat[:, offset : offset + size].reshape(shape))
+        unpacked.append(extra[:, offset : offset + size].reshape(shape))
         offset += size
+    edges = unpacked[0]
+    fields = unpacked[1:] + [
+        jnp.concatenate([edges[:, :1], field_out[..., window], edges[:, 1:]], axis=1)
+    ]
 
     previous = potential[..., window]
     tiles = []
     for step_index in range(STEPS):
         padded = fields[step_index]
-        if step_index == STEPS - 1:
-            field_out = padded[:, 1:-1]
-            padded = padded[..., window]
         tiles.append(lorentz_window(padded, previous, conduct[window], radius[window]))
         previous = padded[:, 1:-1]
     tiles = jnp.stack(tiles)

time: 135 us -> 134 us (level)
  local copies, waits for them, and re-layouts: 13.3 us -> 8.81 us
  matrix products: 3.85 us -> 5.44 us
    reshape x18 -> x14, local copies, waits for them, and re-layouts: 7.9 us -> 2.62 us  [the longest x3 0.58 us: transform(): rest = rest.reshape(rows, devices, width).transpose(1, 0, 2).reshape(packed)]
    unnamed x23 -> x20, local copies, waits for them, and re-layouts: 1.31 us -> 2.97 us
    concatenate x2 -> x6, other arithmetic: 0.17 us -> 1.78 us  [the longest x2 1.55 us: transform(): jnp.concatenate([mixed_main, mixed_rest], axis=1)]
    dot_general x2 -> x4, matrix products: 1.59 us -> 3.18 us  [mix(): lax.dot_general(basis, columns, (((contract,), (0,)), ((), ())), precisio...]
where the time goes in v6:
time: 134 us; the launch traced here: 131 us
  blocking collectives  45.6 us (34%)
  waiting for transfers between devices  38.4 us (29%)
  starting transfers between devices  22.6 us (17%)
  other arithmetic  9.38 us (7%)
  local copies, waits for them, and re-layouts  8.81 us (7%)
  matrix products  5.44 us (4%)
    all_to_all x2, blocking collectives, transform(): lax.all_to_all(jnp.concatenate([main, rest], axis=1), 'azim', 0, 0, tiled...  45.6 us
    all_to_all x2, waiting for transfers between devices, transform(): lax.all_to_all(jnp.concatenate([mixed_main, mixed_rest], axis=1), 'azim',...  29.6 us
    ppermute x2, starting transfers between devices, shifted(): return lax.ppermute(array, axis, pairs)  7.67 us
    all_to_all x2, starting transfers between devices, transform(): lax.all_to_all(jnp.concatenate([mixed_main, mixed_rest], axis=1), 'azim',...  7.28 us
    ppermute x2, waiting for transfers between devices, shifted(): return lax.ppermute(array, axis, pairs)  5.82 us
    ppermute x1, starting transfers between devices, with_halo(): lax.ppermute(lax.slice_in_dim(block, 0, width, axis=dim), axis, backward)  5.75 us
    dot_general x4, matrix products, mix(): lax.dot_general(basis, columns, (((contract,), (0,)), ((), ())), precisio...  3.18 us
    div x5, other arithmetic, shards(): iterate = (right_side + nearby) / divisor  3.1 us
  transfers between devices with their start and end apart: 6, of which 6 were waited for; matrix products, arithmetic and copies ran while one was open for 1% of the time, Pallas kernels for 0%

profile of v6, /device:TPU:2, one launch (start us, length us, event | category | flops | bytes accessed | tf_op | source)
XLA Modules:
  0.0 131.5 jit_solution(11160886068957192436)
XLA Ops:
  0.6 1.0 copy.61
  1.7 1.1 multiply_bitcast_fusion
  2.8 0.1 reshape.161
  3.0 24.8 %all_to_all.20 = f32[16,40,128]{2,1,0:T(8,128)S(1)} all-to-all(f32[16,40,128]{2,1,0:T(8,128)S(1)} %pad_maximum_fusion.3), channel_id=1, replica_groups=mesh['axial'=16,'azim'=16] {'azim'}, dimensions={0} | all-to-all | bytes 655360 | tf_op jit(solution)/shard_map/all_to_all | solution.py:131
  27.8 0.1 reshape.164
  27.9 1.0 fusion.71
  28.9 1.0 fusion.72
  29.9 0.1 reshape.165
  30.1 0.7 pad_maximum_fusion.4
  30.8 3.5 %all-to-all-start.1 = ((f32[16,40,128]{2,1,0:T(8,128)}), f32[16,40,128]{2,1,0:T(8,128)S(1)}, u32[]{:S(2)}, u32[]{:S(2)}) async-start(f32[16,40,128]{2,1,0:T(8,128)} %pad_maximum_fusion.4), calls=%async_computation.1 | async-start | bytes 655360 | tf_op jit(solution)/shard_map/all_to_all | solution.py:144
  34.5 13.9 %all-to-all-done.1 = f32[16,40,128]{2,1,0:T(8,128)S(1)} async-done(((f32[16,40,128]{2,1,0:T(8,128)}), f32[16,40,128]{2,1,0:T(8,128)S(1)}, u32[]{:S(2)}, u32[]{:S(2)}) %all-to-all-start.1) | async-done | bytes 327712 | tf_op jit(solution)/shard_map/all_to_all | solution.py:144
  48.4 0.1 reshape.166
  48.6 1.9 %collective-permute-start = (f32[32,7,160]{2,0,1:T(8,128)S(1)}, f32[32,7,160]{2,0,1:T(8,128)S(1)}, u32[]{:S(2)}, u32[]{:S(2)}) collective-permute-start(f32[32,7,160]{2,0,1:T(8,128)S(1)} %get-tuple-element.23), channel_id=1, source_target_pairs={{0,16},{16,32},{32,48},{48,64},{64,80},{80,96},{96,112},{112,128},... | collective-permute-start | bytes 430088 | tf_op jit(solution)/shard_map/ppermute | solution.py:32
  50.5 5.8 %collective-permute-start.1 = (f32[32,7,160]{2,0,1:T(8,128)S(1)}, f32[32,7,160]{2,0,1:T(8,128)S(1)}, u32[]{:S(2)}, u32[]{:S(2)}) collective-permute-start(f32[32,7,160]{2,0,1:T(8,128)S(1)} %get-tuple-element.24), channel_id=1, source_target_pairs={{16,0},{32,16},{48,32},{64,48},{80,64},{96,80},{112,96},{128,112},... | collective-permute-start | bytes 430088 | tf_op jit(solution)/shard_map/ppermute | solution.py:35
  56.3 0.6 fusion.70
  56.9 1.2 collective-permute-done
  58.0 1.8 %collective-permute-done.1 = f32[32,7,160]{2,0,1:T(8,128)S(1)} collective-permute-done((f32[32,7,160]{2,0,1:T(8,128)S(1)}, f32[32,7,160]{2,0,1:T(8,128)S(1)}, u32[]{:S(2)}, u32[]{:S(2)}) %collective-permute-start.1) | collective-permute-done | bytes 143392 | tf_op jit(solution)/shard_map/ppermute | solution.py:35
  59.9 1.0 select_divide_fusion.4
  60.9 0.4 select_divide_fusion.3
  61.3 0.4 select_divide_fusion.2
  61.7 1.0 select_divide_fusion.1
  62.7 0.4 select_divide_fusion
  63.1 0.4 pad_slice_fusion.13
  63.5 0.2 fusion.36
  63.7 0.7 slice-done
  64.4 0.1 slice_multiply_fusion
  64.6 0.2 copy.23
  64.8 0.1 reshape.168
  65.0 0.1 reshape.167
  65.1 0.1 select_maximum_fusion.1
  65.2 0.2 reshape.169
  65.5 0.1 copy.24
  65.6 0.2 reshape.170
  65.8 20.9 %all_to_all.21 = f32[16,53,128]{2,1,0:T(8,128)S(1)} all-to-all(f32[16,53,128]{2,1,0:T(8,128)S(1)} %pad_maximum_fusion.1), channel_id=1, replica_groups=mesh['axial'=16,'azim'=16] {'azim'}, dimensions={0} | all-to-all | bytes 868352 | tf_op jit(solution)/shard_map/all_to_all | solution.py:131
  86.7 0.6 fusion.73
  87.3 0.4 reshape.173
  87.8 0.6 fusion.74
  88.4 0.2 reshape.174
  88.6 0.8 pad_maximum_fusion.2
  89.4 3.7 %all-to-all-start.3 = ((f32[16,53,128]{2,1,0:T(8,128)}), f32[16,53,128]{2,1,0:T(8,128)S(1)}, u32[]{:S(2)}, u32[]{:S(2)}) async-start(f32[16,53,128]{2,1,0:T(8,128)} %pad_maximum_fusion.2), calls=%async_computation.3 | async-start | bytes 917504 | tf_op jit(solution)/shard_map/all_to_all | solution.py:144
  93.3 0.1 select_reduce_fusion
  93.4 15.8 %all-to-all-done.3 = f32[16,53,128]{2,1,0:T(8,128)S(1)} async-done(((f32[16,53,128]{2,1,0:T(8,128)}), f32[16,53,128]{2,1,0:T(8,128)S(1)}, u32[]{:S(2)}, u32[]{:S(2)}) %all-to-all-start.3) | async-done | bytes 434208 | tf_op jit(solution)/shard_map/all_to_all | solution.py:144
  109.2 0.4 reshape.175
  109.7 0.2 copy.26
  109.8 0.1 reshape.176
  110.0 0.1 slice.313
  110.1 0.2 reshape.177
  110.3 0.2 fusion.66
  110.7 0.2 fusion.55
  110.9 0.2 pad_slice_fusion.25
  111.1 0.2 pad_slice_fusion.27
  111.3 0.8 fusion.53
  112.1 0.1 maximum_bitcast_fusion
  112.3 0.1 maximum_bitcast_fusion.1
  112.4 0.4 broadcast_select_fusion.1
  112.8 1.9 %collective-permute-start.2 = (f32[2,32,16,128]{3,1,2,0:T(8,128)S(1)}, f32[2,32,16,128]{3,1,2,0:T(8,128)S(1)}, u32[]{:S(2)}, u32[]{:S(2)}) collective-permute-start(f32[2,32,16,128]{3,1,2,0:T(8,128)S(1)} %get-tuple-element.19), channel_id=1, source_target_pairs={{0,16},{16,32},{32,48},{48,64},{64,80},{80,96},{96,112},{112,128},... | collective-permute-start | bytes 1572872 | tf_op jit(solution)/shard_map/ppermute | solution.py:43
  114.8 5.8 %collective-permute-start.3 = (f32[2,32,16,128]{3,1,2,0:T(8,128)S(1)}, f32[2,32,16,128]{3,1,2,0:T(8,128)S(1)}, u32[]{:S(2)}, u32[]{:S(2)}) collective-permute-start(f32[2,32,16,128]{3,1,2,0:T(8,128)S(1)} %get-tuple-element.20), channel_id=1, source_target_pairs={{16,0},{32,16},{48,32},{64,48},{80,64},{96,80},{112,96},{128,112},... | collective-permute-start | bytes 1572872 | tf_op jit(solution)/shard_map/ppermute | solution.py:43
  120.5 0.9 copy.35
  121.4 4.1 %collective-permute-done.2 = f32[2,32,16,128]{3,1,2,0:T(8,128)S(1)} collective-permute-done((f32[2,32,16,128]{3,1,2,0:T(8,128)S(1)}, f32[2,32,16,128]{3,1,2,0:T(8,128)S(1)}, u32[]{:S(2)}, u32[]{:S(2)}) %collective-permute-start.2) | collective-permute-done | bytes 524320 | tf_op jit(solution)/shard_map/ppermute | solution.py:43
  125.4 1.8 %collective-permute-done.3 = f32[2,32,16,128]{3,1,2,0:T(8,128)S(1)} collective-permute-done((f32[2,32,16,128]{3,1,2,0:T(8,128)S(1)}, f32[2,32,16,128]{3,1,2,0:T(8,128)S(1)}, u32[]{:S(2)}, u32[]{:S(2)}) %collective-permute-start.3) | collective-permute-done | bytes 524320 | tf_op jit(solution)/shard_map/ppermute | solution.py:43
  127.2 0.2 add_add_fusion
  127.4 1.0 copy-done.8
  128.4 1.8 %fusion.6 = f32[2,32,16,128]{3,2,0,1:T(8,128)S(1)} fusion(f32[32,64,64]{2,1,0:T(8,128)S(1)} %copy-done.8, f32[2,32,16,128]{3,1,2,0:T(8,128)S(1)} %add_add_fusion), kind=kOutput, calls=%fused_computation.8 | convolution fusion | flops 103284736 | bytes 1572864 | tf_op jit(solution)/shard_map/aqr,sazr->sazq/dot_general | solution.py:268
  130.3 1.2 multiply_add_fusion.2
  (50 shorter events, 1.0 us)
Async XLA Ops:
  3.0 25.0 %copy-start = (f32[512,512]{1,0:T(8,128)S(1)}, f32[512,512]{1,0:T(8,128)}, u32[]{:S(2)}) copy-start(f32[512,512]{1,0:T(8,128)} %constant.62.clone) | copy-start | bytes 3145732
  30.8 17.6 %all-to-all-start.1 = ((f32[16,40,128]{2,1,0:T(8,128)}), f32[16,40,128]{2,1,0:T(8,128)S(1)}, u32[]{:S(2)}, u32[]{:S(2)}) async-start(f32[16,40,128]{2,1,0:T(8,128)} %pad_maximum_fusion.4), calls=%async_computation.1 | async-start | bytes 655360 | tf_op jit(solution)/shard_map/all_to_all | solution.py:144
  34.4 21.9 %copy-start.6 = (f32[2]{0:T(128)S(1)}, f32[2]{0:T(128)}, u32[]{:S(2)}) copy-start(f32[2]{0:T(128)} %param.13) | copy-start | bytes 28
  48.6 9.4 %collective-permute-start = (f32[32,7,160]{2,0,1:T(8,128)S(1)}, f32[32,7,160]{2,0,1:T(8,128)S(1)}, u32[]{:S(2)}, u32[]{:S(2)}) collective-permute-start(f32[32,7,160]{2,0,1:T(8,128)S(1)} %get-tuple-element.23), channel_id=1, source_target_pairs={{0,16},{16,32},{32,48},{48,64},{64,80},{80,96},{96,112},{112,128},... | collective-permute-start | bytes 430088 | tf_op jit(solution)/shard_map/ppermute | solution.py:32
  50.5 9.3 %collective-permute-start.1 = (f32[32,7,160]{2,0,1:T(8,128)S(1)}, f32[32,7,160]{2,0,1:T(8,128)S(1)}, u32[]{:S(2)}, u32[]{:S(2)}) collective-permute-start(f32[32,7,160]{2,0,1:T(8,128)S(1)} %get-tuple-element.24), channel_id=1, source_target_pairs={{16,0},{32,16},{48,32},{64,48},{80,64},{96,80},{112,96},{128,112},... | collective-permute-start | bytes 430088 | tf_op jit(solution)/shard_map/ppermute | solution.py:35
  61.7 1.0 copy-start.1
  63.5 1.0 slice-start
  88.4 4.9 %copy-start.5 = (s32[2,32,1]{1,2,0:T(1,128)S(1)}, s32[2,32,1]{1,2,0:T(1,128)}, u32[]{:S(2)}) copy-start(s32[2,32,1]{1,2,0:T(1,128)} %param.17) | copy-start | bytes 772
  88.4 4.9 %copy-start.7 = (s32[2,32,1]{1,2,0:T(1,128)S(1)}, s32[2,32,1]{1,2,0:T(1,128)}, u32[]{:S(2)}) copy-start(s32[2,32,1]{1,2,0:T(1,128)} %param.16) | copy-start | bytes 772
  89.4 19.8 %all-to-all-start.3 = ((f32[16,53,128]{2,1,0:T(8,128)}), f32[16,53,128]{2,1,0:T(8,128)S(1)}, u32[]{:S(2)}, u32[]{:S(2)}) async-start(f32[16,53,128]{2,1,0:T(8,128)} %pad_maximum_fusion.2), calls=%async_computation.3 | async-start | bytes 917504 | tf_op jit(solution)/shard_map/all_to_all | solution.py:144
  112.8 12.6 %collective-permute-start.2 = (f32[2,32,16,128]{3,1,2,0:T(8,128)S(1)}, f32[2,32,16,128]{3,1,2,0:T(8,128)S(1)}, u32[]{:S(2)}, u32[]{:S(2)}) collective-permute-start(f32[2,32,16,128]{3,1,2,0:T(8,128)S(1)} %get-tuple-element.19), channel_id=1, source_target_pairs={{0,16},{16,32},{32,48},{48,64},{64,80},{80,96},{96,112},{112,128},... | collective-permute-start | bytes 1572872 | tf_op jit(solution)/shard_map/ppermute | solution.py:43
  114.8 12.4 %collective-permute-start.3 = (f32[2,32,16,128]{3,1,2,0:T(8,128)S(1)}, f32[2,32,16,128]{3,1,2,0:T(8,128)S(1)}, u32[]{:S(2)}, u32[]{:S(2)}) collective-permute-start(f32[2,32,16,128]{3,1,2,0:T(8,128)S(1)} %get-tuple-element.20), channel_id=1, source_target_pairs={{16,0},{32,16},{48,32},{64,48},{80,64},{96,80},{112,96},{128,112},... | collective-permute-start | bytes 1572872 | tf_op jit(solution)/shard_map/ppermute | solution.py:43
  127.2 1.2 copy-start.8
  128.4 1.8 %copy-start.2 = (f32[32,16,128]{2,1,0:T(8,128)S(1)}, f32[32,16,128]{2,1,0:T(8,128)}, u32[]{:S(2)}) copy-start(f32[32,16,128]{2,1,0:T(8,128)} %param.19) | copy-start | bytes 786436
  128.4 1.8 %copy-start.3 = (f32[32,16,128]{2,1,0:T(8,128)S(1)}, f32[32,16,128]{2,1,0:T(8,128)}, u32[]{:S(2)}) copy-start(f32[32,16,128]{2,1,0:T(8,128)} %param.20) | copy-start | bytes 786436
  128.4 1.8 %copy-start.4 = (f32[32,16,128]{2,1,0:T(8,128)S(1)}, f32[32,16,128]{2,1,0:T(8,128)}, u32[]{:S(2)}) copy-start(f32[32,16,128]{2,1,0:T(8,128)} %param.18) | copy-start | bytes 786436

commit v7 on v6

--- a/solution.py
+++ b/solution.py
@@ -139,8 +139,17 @@
             preferred_element_type=jnp.float32,
         )
 
-    mixed_main = mix(spread[:, :rows].reshape(devices * rows, lanes)).reshape(main.shape)
-    mixed_rest = mix(spread[:, rows:].reshape(devices * rows, width)).reshape(packed)
+    mixed = mix(
+        jnp.concatenate(
+            [
+                spread[:, :rows].reshape(devices * rows, lanes),
+                spread[:, rows:].reshape(devices * rows, width),
+            ],
+            axis=1,
+        )
+    )
+    mixed_main = mixed[:, :lanes].reshape(main.shape)
+    mixed_rest = mixed[:, lanes:].reshape(packed)
     joined = lax.all_to_all(
         jnp.concatenate([mixed_main, mixed_rest], axis=1), "azim", 0, 0, tiled=True
     )
@@ -251,12 +260,6 @@
         "sjcw,sjp->spcw", tiles, slot_table.astype(jnp.float32), precision=HIGH
     )
 
-    def place(target):
-        return jnp.where((owner_at == target)[:, :, None, None], moved, 0.0)
-
-    from_below = shifted(place(2), "axial", 1)
-    from_above = shifted(place(0), "axial", -1)
-    received = place(1) + from_below + from_above
     blank = jnp.zeros_like(tile_weight)
     paired = jnp.concatenate(
         [
@@ -265,7 +268,14 @@
         ],
         axis=1,
     )
-    loads = jnp.einsum("aqr,sazr->sazq", paired, received, precision=lax.Precision.HIGH)
+    mapped = jnp.einsum("apr,sazr->sazp", paired, moved, precision=lax.Precision.HIGH)
+
+    def place(target):
+        return jnp.where((owner_at == target)[:, :, None, None], mapped, 0.0)
+
+    from_below = shifted(place(2), "axial", 1)
+    from_above = shifted(place(0), "axial", -1)
+    loads = place(1) + from_below + from_above
     for step_index in range(STEPS):
         velocity, strain, plastic = plastic_update(loads[step_index], velocity, strain, plastic)
     return (field_out, velocity, strain, plastic)

time: 134 us -> 131 us (0.978); the launches traced: 131 us -> 130 us
  waiting for transfers between devices: 38.4 us -> 44.4 us
  starting transfers between devices: 22.6 us -> 19.2 us
  blocking collectives: 45.6 us -> 42.5 us
  matrix products: 5.44 us -> 3.47 us
    ppermute x1, waiting for transfers between devices: 1.15 us -> 5.93 us  [with_halo(): lax.ppermute(lax.slice_in_dim(block, block.shape[dim] - width, None, axis...]
    ppermute x2, waiting for transfers between devices: 5.82 us -> 9.72 us  [shifted(): return lax.ppermute(array, axis, pairs)]
    ppermute x1, starting transfers between devices: 5.75 us -> 2.55 us  [with_halo(): lax.ppermute(lax.slice_in_dim(block, 0, width, axis=dim), axis, backward)]
    all_to_all x2, blocking collectives: 45.6 us -> 42.5 us  [transform(): lax.all_to_all(jnp.concatenate([main, rest], axis=1), 'azim', 0, 0, tiled...]
    dot_general x4 -> x2, matrix products: 3.18 us -> 1.23 us  [mix(): lax.dot_general(basis, columns, (((contract,), (0,)), ((), ())), precisio...]
    all_to_all x2, waiting for transfers between devices: 29.6 us -> 27.7 us  [transform(): lax.all_to_all(jnp.concatenate([mixed_main, mixed_rest], axis=1), 'azim',...]
    unnamed x20 -> x24, local copies, waits for them, and re-layouts: 2.97 us -> 2.75 us
  transfers between devices with their start and end apart: 6 -> 6, of which waited for: 6 -> 6; matrix products, arithmetic and copies ran while one was open for 1% -> 2% of each run, Pallas kernels for 0% -> 0%
where the time goes in v7:
time: 131 us; the launch traced here: 130 us
  waiting for transfers between devices  44.4 us (34%)
  blocking collectives  42.5 us (32%)
  starting transfers between devices  19.2 us (15%)
  local copies, waits for them, and re-layouts  9.79 us (7%)
  other arithmetic  9.34 us (7%)
  matrix products  3.47 us (3%)
    all_to_all x2, blocking collectives, transform(): lax.all_to_all(jnp.concatenate([main, rest], axis=1), 'azim', 0, 0, tiled...  42.5 us
    all_to_all x2, waiting for transfers between devices, transform(): lax.all_to_all(jnp.concatenate([mixed_main, mixed_rest], axis=1), 'azim',...  27.7 us
    ppermute x2, waiting for transfers between devices, shifted(): return lax.ppermute(array, axis, pairs)  9.72 us
    ppermute x2, starting transfers between devices, shifted(): return lax.ppermute(array, axis, pairs)  7.45 us
    all_to_all x2, starting transfers between devices, transform(): lax.all_to_all(jnp.concatenate([mixed_main, mixed_rest], axis=1), 'azim',...  7.28 us
    ppermute x1, waiting for transfers between devices, with_halo(): lax.ppermute(lax.slice_in_dim(block, block.shape[dim] - width, None, axis...  5.93 us
    div x5, other arithmetic, shards(): iterate = (right_side + nearby) / divisor  3.1 us
    unnamed x24, local copies, waits for them, and re-layouts  2.75 us
  transfers between devices with their start and end apart: 6, of which 6 were waited for; matrix products, arithmetic and copies ran while one was open for 2% of the time, Pallas kernels for 0%

profile of v7, /device:TPU:2, one launch (start us, length us, event | category | flops | bytes accessed | tf_op | source)
XLA Modules:
  0.0 129.9 jit_solution(5560203556485636254)
XLA Ops:
  0.6 1.1 multiply_bitcast_fusion
  1.8 0.1 reshape.161
  2.1 24.8 %all_to_all.20 = f32[16,40,128]{2,1,0:T(8,128)S(1)} all-to-all(f32[16,40,128]{2,1,0:T(8,128)S(1)} %pad_maximum_fusion.3), channel_id=1, replica_groups=mesh['axial'=16,'azim'=16] {'azim'}, dimensions={0} | all-to-all | bytes 655360 | tf_op jit(solution)/shard_map/all_to_all | solution.py:131
  26.9 0.1 reshape.163
  27.0 0.6 fusion.11
  27.7 0.1 copy.56
  27.9 0.1 reshape.165
  28.0 0.1 copy.55
  28.1 0.8 pad_maximum_fusion.4
  28.9 3.5 %all-to-all-start.1 = ((f32[16,40,128]{2,1,0:T(8,128)}), f32[16,40,128]{2,1,0:T(8,128)S(1)}, u32[]{:S(2)}, u32[]{:S(2)}) async-start(f32[16,40,128]{2,1,0:T(8,128)} %pad_maximum_fusion.4), calls=%async_computation.1 | async-start | bytes 655360 | tf_op jit(solution)/shard_map/all_to_all | solution.py:153
  32.6 13.9 %all-to-all-done.1 = f32[16,40,128]{2,1,0:T(8,128)S(1)} async-done(((f32[16,40,128]{2,1,0:T(8,128)}), f32[16,40,128]{2,1,0:T(8,128)S(1)}, u32[]{:S(2)}, u32[]{:S(2)}) %all-to-all-start.1) | async-done | bytes 327712 | tf_op jit(solution)/shard_map/all_to_all | solution.py:153
  46.5 0.1 reshape.166
  46.6 2.5 %collective-permute-start.1 = (f32[32,7,160]{2,0,1:T(8,128)S(1)}, f32[32,7,160]{2,0,1:T(8,128)S(1)}, u32[]{:S(2)}, u32[]{:S(2)}) collective-permute-start(f32[32,7,160]{2,0,1:T(8,128)S(1)} %get-tuple-element.28), channel_id=1, source_target_pairs={{16,0},{32,16},{48,32},{64,48},{80,64},{96,80},{112,96},{128,112},... | collective-permute-start | bytes 430088 | tf_op jit(solution)/shard_map/ppermute | solution.py:35
  49.2 1.9 %collective-permute-start = (f32[32,7,160]{2,0,1:T(8,128)S(1)}, f32[32,7,160]{2,0,1:T(8,128)S(1)}, u32[]{:S(2)}, u32[]{:S(2)}) collective-permute-start(f32[32,7,160]{2,0,1:T(8,128)S(1)} %get-tuple-element.27), channel_id=1, source_target_pairs={{0,16},{16,32},{32,48},{48,64},{64,80},{80,96},{96,112},{112,128},... | collective-permute-start | bytes 430088 | tf_op jit(solution)/shard_map/ppermute | solution.py:32
  51.2 0.6 fusion.80
  51.7 1.0 collective-permute-done.1
  52.7 5.9 %collective-permute-done = f32[32,7,160]{2,0,1:T(8,128)S(1)} collective-permute-done((f32[32,7,160]{2,0,1:T(8,128)S(1)}, f32[32,7,160]{2,0,1:T(8,128)S(1)}, u32[]{:S(2)}, u32[]{:S(2)}) %collective-permute-start) | collective-permute-done | bytes 143392 | tf_op jit(solution)/shard_map/ppermute | solution.py:32
  58.8 1.0 select_divide_fusion.4
  59.8 0.4 select_divide_fusion.3
  60.2 0.4 select_divide_fusion.2
  60.6 1.0 select_divide_fusion.1
  61.6 0.4 select_divide_fusion
  62.0 0.4 pad_slice_fusion.13
  62.3 0.2 fusion.44
  62.6 0.7 slice-done
  63.3 0.1 slice_multiply_fusion
  63.4 0.2 copy.58
  63.6 0.1 reshape.168
  64.1 0.2 reshape.169
  64.4 0.2 reshape.170
  64.7 17.7 %all_to_all.21 = f32[16,53,128]{2,1,0:T(8,128)S(1)} all-to-all(f32[16,53,128]{2,1,0:T(8,128)S(1)} %pad_maximum_fusion.1), channel_id=1, replica_groups=mesh['axial'=16,'azim'=16] {'azim'}, dimensions={0} | all-to-all | bytes 868352 | tf_op jit(solution)/shard_map/all_to_all | solution.py:131
  82.4 0.4 reshape.172
  82.9 0.6 fusion.15
  83.5 0.1 copy.61
  83.6 0.2 reshape.174
  83.9 0.1 copy.60
  84.0 0.8 pad_maximum_fusion.2
  84.8 3.7 %all-to-all-start.3 = ((f32[16,53,128]{2,1,0:T(8,128)}), f32[16,53,128]{2,1,0:T(8,128)S(1)}, u32[]{:S(2)}, u32[]{:S(2)}) async-start(f32[16,53,128]{2,1,0:T(8,128)} %pad_maximum_fusion.2), calls=%async_computation.3 | async-start | bytes 917504 | tf_op jit(solution)/shard_map/all_to_all | solution.py:153
  88.7 0.1 select_reduce_fusion
  89.1 13.9 %all-to-all-done.3 = f32[16,53,128]{2,1,0:T(8,128)S(1)} async-done(((f32[16,53,128]{2,1,0:T(8,128)}), f32[16,53,128]{2,1,0:T(8,128)S(1)}, u32[]{:S(2)}, u32[]{:S(2)}) %all-to-all-start.3) | async-done | bytes 434208 | tf_op jit(solution)/shard_map/all_to_all | solution.py:153
  102.9 0.4 reshape.175
  103.4 0.2 copy.63
  103.5 0.1 reshape.176
  103.8 0.2 reshape.177
  104.0 0.2 fusion.76
  104.2 0.1 copy-done.2
  104.4 0.2 fusion.63
  104.6 0.2 pad_slice_fusion.27
  104.8 0.3 slice-done.1
  105.3 0.2 pad_slice_fusion.25
  105.5 0.8 fusion.61
  106.2 0.1 maximum_bitcast_fusion.1
  106.4 0.1 maximum_bitcast_fusion
  106.5 0.4 fusion.19
  106.9 0.7 copy-done.10
  107.6 1.9 %broadcast_select_fusion.1 = (f32[2,32,16,128]{3,2,0,1:T(8,128)S(1)}, f32[2,32,16,128]{3,2,0,1:T(8,128)S(1)}, f32[2,32,16,128]{3,2,0,1:T(8,128)S(1)}) fusion(pred[2,32]{0,1:T(8,128)(4,1)S(1)} %copy.71, pred[2,32]{0,1:T(8,128)(4,1)S(1)} %copy.72, f32[32,64,64]{2,1,0:T(8,128)S(1)} %copy-done.10, f32[2,32,16,128]{3,1,2,0:T(8,128)S(1)} %fusion.19), kind=kOutput, calls=%fused_computation.127 | convolution fusion | flops 103546880 | bytes 2621568 | tf_op jit(solution)/shard_map/apr,sazr->sazp/dot_general | solution.py:271
  109.5 5.5 %collective-permute-start.3 = (f32[2,32,16,128]{3,2,0,1:T(8,128)S(1)}, f32[2,32,16,128]{3,2,0,1:T(8,128)S(1)}, u32[]{:S(2)}, u32[]{:S(2)}) collective-permute-start(f32[2,32,16,128]{3,2,0,1:T(8,128)S(1)} %get-tuple-element.24), channel_id=1, source_target_pairs={{16,0},{32,16},{48,32},{64,48},{80,64},{96,80},{112,96},{128,112},... | collective-permute-start | bytes 1572872 | tf_op jit(solution)/shard_map/ppermute | solution.py:43
  115.0 1.9 %collective-permute-start.2 = (f32[2,32,16,128]{3,2,0,1:T(8,128)S(1)}, f32[2,32,16,128]{3,2,0,1:T(8,128)S(1)}, u32[]{:S(2)}, u32[]{:S(2)}) collective-permute-start(f32[2,32,16,128]{3,2,0,1:T(8,128)S(1)} %get-tuple-element.23), channel_id=1, source_target_pairs={{0,16},{16,32},{32,48},{48,64},{64,80},{80,96},{96,112},{112,128},... | collective-permute-start | bytes 1572872 | tf_op jit(solution)/shard_map/ppermute | solution.py:43
  117.0 0.9 copy.74
  117.9 3.8 %collective-permute-done.3 = f32[2,32,16,128]{3,2,0,1:T(8,128)S(1)} collective-permute-done((f32[2,32,16,128]{3,2,0,1:T(8,128)S(1)}, f32[2,32,16,128]{3,2,0,1:T(8,128)S(1)}, u32[]{:S(2)}, u32[]{:S(2)}) %collective-permute-start.3) | collective-permute-done | bytes 524320 | tf_op jit(solution)/shard_map/ppermute | solution.py:43
  121.7 5.9 %collective-permute-done.2 = f32[2,32,16,128]{3,2,0,1:T(8,128)S(1)} collective-permute-done((f32[2,32,16,128]{3,2,0,1:T(8,128)S(1)}, f32[2,32,16,128]{3,2,0,1:T(8,128)S(1)}, u32[]{:S(2)}, u32[]{:S(2)}) %collective-permute-start.2) | collective-permute-done | bytes 524320 | tf_op jit(solution)/shard_map/ppermute | solution.py:43
  127.6 0.2 add_add_fusion
  127.8 0.8 copy-done.4
  128.7 1.2 multiply_add_fusion.2
  (64 shorter events, 2.0 us)
Async XLA Ops:
  0.6 1.3 %copy-start.3 = (f32[32,16,128]{2,1,0:T(8,128)S(1)}, f32[32,16,128]{2,1,0:T(8,128)}, u32[]{:S(2)}) copy-start(f32[32,16,128]{2,1,0:T(8,128)} %param.14) | copy-start | bytes 786436
  2.1 25.0 %copy-start = (f32[512,512]{1,0:T(8,128)S(1)}, f32[512,512]{1,0:T(8,128)}, u32[]{:S(2)}) copy-start(f32[512,512]{1,0:T(8,128)} %constant.62.clone) | copy-start | bytes 3145732
  28.9 17.6 %all-to-all-start.1 = ((f32[16,40,128]{2,1,0:T(8,128)}), f32[16,40,128]{2,1,0:T(8,128)S(1)}, u32[]{:S(2)}, u32[]{:S(2)}) async-start(f32[16,40,128]{2,1,0:T(8,128)} %pad_maximum_fusion.4), calls=%async_computation.1 | async-start | bytes 655360 | tf_op jit(solution)/shard_map/all_to_all | solution.py:153
  32.4 18.7 %copy-start.8 = (f32[2]{0:T(128)S(1)}, f32[2]{0:T(128)}, u32[]{:S(2)}) copy-start(f32[2]{0:T(128)} %param.13) | copy-start | bytes 28
  46.6 6.1 %collective-permute-start.1 = (f32[32,7,160]{2,0,1:T(8,128)S(1)}, f32[32,7,160]{2,0,1:T(8,128)S(1)}, u32[]{:S(2)}, u32[]{:S(2)}) collective-permute-start(f32[32,7,160]{2,0,1:T(8,128)S(1)} %get-tuple-element.28), channel_id=1, source_target_pairs={{16,0},{32,16},{48,32},{64,48},{80,64},{96,80},{112,96},{128,112},... | collective-permute-start | bytes 430088 | tf_op jit(solution)/shard_map/ppermute | solution.py:35
  49.2 9.4 %collective-permute-start = (f32[32,7,160]{2,0,1:T(8,128)S(1)}, f32[32,7,160]{2,0,1:T(8,128)S(1)}, u32[]{:S(2)}, u32[]{:S(2)}) collective-permute-start(f32[32,7,160]{2,0,1:T(8,128)S(1)} %get-tuple-element.27), channel_id=1, source_target_pairs={{0,16},{16,32},{32,48},{48,64},{64,80},{80,96},{96,112},{112,128},... | collective-permute-start | bytes 430088 | tf_op jit(solution)/shard_map/ppermute | solution.py:32
  60.5 1.0 copy-start.1
  62.3 1.0 slice-start
  84.0 4.6 %copy-start.7 = (s32[2,32,1]{1,2,0:T(1,128)S(1)}, s32[2,32,1]{1,2,0:T(1,128)}, u32[]{:S(2)}) copy-start(s32[2,32,1]{1,2,0:T(1,128)} %param.17) | copy-start | bytes 772
  84.0 4.6 %copy-start.9 = (s32[2,32,1]{1,2,0:T(1,128)S(1)}, s32[2,32,1]{1,2,0:T(1,128)}, u32[]{:S(2)}) copy-start(s32[2,32,1]{1,2,0:T(1,128)} %param.16) | copy-start | bytes 772
  84.8 18.1 %all-to-all-start.3 = ((f32[16,53,128]{2,1,0:T(8,128)}), f32[16,53,128]{2,1,0:T(8,128)S(1)}, u32[]{:S(2)}, u32[]{:S(2)}) async-start(f32[16,53,128]{2,1,0:T(8,128)} %pad_maximum_fusion.2), calls=%async_computation.3 | async-start | bytes 917504 | tf_op jit(solution)/shard_map/all_to_all | solution.py:153
  103.7 0.7 copy-start.2
  104.4 0.8 slice-start.1
  106.4 1.2 copy-start.10
  109.5 12.2 %collective-permute-start.3 = (f32[2,32,16,128]{3,2,0,1:T(8,128)S(1)}, f32[2,32,16,128]{3,2,0,1:T(8,128)S(1)}, u32[]{:S(2)}, u32[]{:S(2)}) collective-permute-start(f32[2,32,16,128]{3,2,0,1:T(8,128)S(1)} %get-tuple-element.24), channel_id=1, source_target_pairs={{16,0},{32,16},{48,32},{64,48},{80,64},{96,80},{112,96},{128,112},... | collective-permute-start | bytes 1572872 | tf_op jit(solution)/shard_map/ppermute | solution.py:43
  115.0 12.6 %collective-permute-start.2 = (f32[2,32,16,128]{3,2,0,1:T(8,128)S(1)}, f32[2,32,16,128]{3,2,0,1:T(8,128)S(1)}, u32[]{:S(2)}, u32[]{:S(2)}) collective-permute-start(f32[2,32,16,128]{3,2,0,1:T(8,128)S(1)} %get-tuple-element.23), channel_id=1, source_target_pairs={{0,16},{16,32},{32,48},{48,64},{64,80},{80,96},{96,112},{112,128},... | collective-permute-start | bytes 1572872 | tf_op jit(solution)/shard_map/ppermute | solution.py:43
  127.6 1.0 copy-start.4
  127.6 1.0 copy-start.5
  127.6 1.1 copy-start.6

commit v8 on v7

--- a/solution.py
+++ b/solution.py
@@ -218,13 +218,17 @@
     window = slice(band_start - 1, band_start + band_width + 1)
     iterate = field_modes
     kept = []
+    trim = 0
     for step_index in range(STEPS):
-        right_side = MU_COIL * (drive[step_index] * coil_modes) + conduct * iterate
+        right_side = MU_COIL * (drive[step_index] * coil_modes[:, trim : span - trim]) + (
+            conduct * iterate
+        )
         for sweep_index in range(SWEEPS):
-            axial_pad = jnp.pad(iterate, ((0, 0), (1, 1), (0, 0)))
-            nearby = axial_pad[:, 2:] + axial_pad[:, :-2] + radial_sum(iterate)
-            iterate = (right_side + nearby) / divisor
-        kept.append(iterate[:, reach - 1 : reach + axial_cells + 1] * weight)
+            trim += 1
+            nearby = iterate[:, 2:] + iterate[:, :-2] + radial_sum(iterate[:, 1:-1])
+            right_side = right_side[:, 1:-1]
+            iterate = (right_side + nearby) / divisor[:, trim : span - trim]
+        kept.append(iterate[:, reach - 1 - trim : reach - trim + axial_cells + 1] * weight)
     last = kept[-1]
     edges = jnp.concatenate([last[:, :1], last[:, -1:]], axis=1)[..., window]
     pieces = [edges.shape] + [piece[..., window].shape for piece in kept[:-1]]

time: 131 us -> 133 us (1.015)
  blocking collectives: 42.5 us -> 20.9 us
  starting transfers between devices: 19.2 us -> 32.6 us
  waiting for transfers between devices: 44.4 us -> 52.8 us
    all_to_all x2 -> x1, blocking collectives: 42.5 us -> 20.9 us  [transform(): lax.all_to_all(jnp.concatenate([main, rest], axis=1), 'azim', 0, 0, tiled...]
    all_to_all x0 -> x1, waiting for transfers between devices: none -> 14.7 us  [transform(): lax.all_to_all(jnp.concatenate([main, rest], axis=1), 'azim', 0, 0, tiled...]
    all_to_all x0 -> x1, starting transfers between devices: none -> 10.1 us  [transform(): lax.all_to_all(jnp.concatenate([main, rest], axis=1), 'azim', 0, 0, tiled...]
    ppermute x1, waiting for transfers between devices: 5.93 us -> 1.15 us  [with_halo(): lax.ppermute(lax.slice_in_dim(block, block.shape[dim] - width, None, axis...]
    ppermute x2, waiting for transfers between devices: 9.72 us -> 5.71 us  [shifted(): return lax.ppermute(array, axis, pairs)]
    ppermute x1, starting transfers between devices: 2.55 us -> 5.75 us  [with_halo(): lax.ppermute(lax.slice_in_dim(block, 0, width, axis=dim), axis, backward)]
    div x5 -> x4, other arithmetic: 3.1 us -> 1.1 us  [shards(): iterate = (right_side + nearby) / divisor[:, trim:span - trim]]
    all_to_all x2, waiting for transfers between devices: 27.7 us -> 29.5 us  [transform(): lax.all_to_all(jnp.concatenate([mixed_main, mixed_rest], axis=1), 'azim',...]
  transfers between devices with their start and end apart: 6 -> 7, of which waited for: 6 -> 7; matrix products, arithmetic and copies ran while one was open for 2% -> 2% of each run, Pallas kernels for 0% -> 0%
where the time goes in v8:
time: 133 us; the launch traced here: 131 us
  waiting for transfers between devices  52.8 us (40%)
  starting transfers between devices  32.6 us (25%)
  blocking collectives  20.9 us (16%)
  local copies, waits for them, and re-layouts  9.84 us (7%)
  other arithmetic  9.77 us (7%)
  matrix products  3.48 us (3%)
    all_to_all x2, waiting for transfers between devices, transform(): lax.all_to_all(jnp.concatenate([mixed_main, mixed_rest], axis=1), 'azim',...  29.5 us
    all_to_all x1, blocking collectives, transform(): lax.all_to_all(jnp.concatenate([main, rest], axis=1), 'azim', 0, 0, tiled...  20.9 us
    all_to_all x1, waiting for transfers between devices, transform(): lax.all_to_all(jnp.concatenate([main, rest], axis=1), 'azim', 0, 0, tiled...  14.7 us
    all_to_all x1, starting transfers between devices, transform(): lax.all_to_all(jnp.concatenate([main, rest], axis=1), 'azim', 0, 0, tiled...  10.1 us
    ppermute x2, starting transfers between devices, shifted(): return lax.ppermute(array, axis, pairs)  7.67 us
    all_to_all x2, starting transfers between devices, transform(): lax.all_to_all(jnp.concatenate([mixed_main, mixed_rest], axis=1), 'azim',...  7.1 us
    ppermute x1, starting transfers between devices, with_halo(): lax.ppermute(lax.slice_in_dim(block, 0, width, axis=dim), axis, backward)  5.75 us
    ppermute x2, waiting for transfers between devices, shifted(): return lax.ppermute(array, axis, pairs)  5.71 us
  transfers between devices with their start and end apart: 7, of which 7 were waited for; matrix products, arithmetic and copies ran while one was open for 2% of the time, Pallas kernels for 0%

profile of v8, /device:TPU:2, one launch (start us, length us, event | category | flops | bytes accessed | tf_op | source)
XLA Modules:
  0.0 130.6 jit_solution(17974228211371973401)
XLA Ops:
  0.6 1.0 copy.102
  1.7 1.1 multiply_bitcast_fusion
  3.0 0.7 pad_maximum_fusion.3
  3.7 10.1 %all-to-all-start = ((f32[16,40,128]{2,1,0:T(8,128)}), f32[16,40,128]{2,1,0:T(8,128)S(1)}, u32[]{:S(2)}, u32[]{:S(2)}) async-start(f32[16,40,128]{2,1,0:T(8,128)} %pad_maximum_fusion.3), calls=%async_computation | async-start | bytes 655360 | tf_op jit(solution)/shard_map/all_to_all | solution.py:131
  13.9 14.7 %all-to-all-done = f32[16,40,128]{2,1,0:T(8,128)S(1)} async-done(((f32[16,40,128]{2,1,0:T(8,128)}), f32[16,40,128]{2,1,0:T(8,128)S(1)}, u32[]{:S(2)}, u32[]{:S(2)}) %all-to-all-start) | async-done | bytes 327712 | tf_op jit(solution)/shard_map/all_to_all | solution.py:131
  28.6 0.1 reshape.163
  28.7 0.6 fusion.11
  29.4 0.1 copy.55
  29.5 0.1 copy.56
  29.7 0.1 reshape.165
  29.8 0.7 pad_maximum_fusion.4
  30.5 3.5 %all-to-all-start.1 = ((f32[16,40,128]{2,1,0:T(8,128)}), f32[16,40,128]{2,1,0:T(8,128)S(1)}, u32[]{:S(2)}, u32[]{:S(2)}) async-start(f32[16,40,128]{2,1,0:T(8,128)} %pad_maximum_fusion.4), calls=%async_computation.1 | async-start | bytes 655360 | tf_op jit(solution)/shard_map/all_to_all | solution.py:153
  34.3 13.8 %all-to-all-done.1 = f32[16,40,128]{2,1,0:T(8,128)S(1)} async-done(((f32[16,40,128]{2,1,0:T(8,128)}), f32[16,40,128]{2,1,0:T(8,128)S(1)}, u32[]{:S(2)}, u32[]{:S(2)}) %all-to-all-start.1) | async-done | bytes 327712 | tf_op jit(solution)/shard_map/all_to_all | solution.py:153
  48.1 0.1 reshape.166
  48.3 1.9 %collective-permute-start = (f32[32,7,160]{2,0,1:T(8,128)S(1)}, f32[32,7,160]{2,0,1:T(8,128)S(1)}, u32[]{:S(2)}, u32[]{:S(2)}) collective-permute-start(f32[32,7,160]{2,0,1:T(8,128)S(1)} %get-tuple-element.25), channel_id=1, source_target_pairs={{0,16},{16,32},{32,48},{48,64},{64,80},{80,96},{96,112},{112,128},... | collective-permute-start | bytes 430088 | tf_op jit(solution)/shard_map/ppermute | solution.py:32
  50.2 5.8 %collective-permute-start.1 = (f32[32,7,160]{2,0,1:T(8,128)S(1)}, f32[32,7,160]{2,0,1:T(8,128)S(1)}, u32[]{:S(2)}, u32[]{:S(2)}) collective-permute-start(f32[32,7,160]{2,0,1:T(8,128)S(1)} %get-tuple-element.26), channel_id=1, source_target_pairs={{16,0},{32,16},{48,32},{64,48},{80,64},{96,80},{112,96},{128,112},... | collective-permute-start | bytes 430088 | tf_op jit(solution)/shard_map/ppermute | solution.py:35
  56.0 0.6 fusion.87
  56.6 1.2 collective-permute-done
  57.8 1.8 %collective-permute-done.1 = f32[32,7,160]{2,0,1:T(8,128)S(1)} collective-permute-done((f32[32,7,160]{2,0,1:T(8,128)S(1)}, f32[32,7,160]{2,0,1:T(8,128)S(1)}, u32[]{:S(2)}, u32[]{:S(2)}) %collective-permute-start.1) | collective-permute-done | bytes 143392 | tf_op jit(solution)/shard_map/ppermute | solution.py:35
  59.7 0.7 fusion.24
  60.4 0.3 fusion.28
  60.8 0.3 fusion.32
  61.1 0.9 fusion.34
  62.1 0.3 fusion.42
  62.4 0.2 fusion.46
  62.7 0.2 fusion.51
  63.1 0.1 slice_multiply_fusion.1
  63.3 0.2 copy.58
  63.5 0.1 reshape.168
  63.7 0.2 reshape.169
  64.1 0.2 reshape.170
  64.3 20.9 %all_to_all.20 = f32[16,53,128]{2,1,0:T(8,128)S(1)} all-to-all(f32[16,53,128]{2,1,0:T(8,128)S(1)} %pad_maximum_fusion.1), channel_id=1, replica_groups=mesh['axial'=16,'azim'=16] {'azim'}, dimensions={0} | all-to-all | bytes 868352 | tf_op jit(solution)/shard_map/all_to_all | solution.py:131
  85.2 0.4 reshape.172
  85.7 0.6 fusion.15
  86.3 0.1 copy.61
  86.5 0.2 reshape.174
  86.7 0.1 copy.60
  86.8 0.8 pad_maximum_fusion.2
  87.6 3.6 %all-to-all-start.3 = ((f32[16,53,128]{2,1,0:T(8,128)}), f32[16,53,128]{2,1,0:T(8,128)S(1)}, u32[]{:S(2)}, u32[]{:S(2)}) async-start(f32[16,53,128]{2,1,0:T(8,128)} %pad_maximum_fusion.2), calls=%async_computation.3 | async-start | bytes 917504 | tf_op jit(solution)/shard_map/all_to_all | solution.py:153
  91.7 15.7 %all-to-all-done.3 = f32[16,53,128]{2,1,0:T(8,128)S(1)} async-done(((f32[16,53,128]{2,1,0:T(8,128)}), f32[16,53,128]{2,1,0:T(8,128)S(1)}, u32[]{:S(2)}, u32[]{:S(2)}) %all-to-all-start.3) | async-done | bytes 434208 | tf_op jit(solution)/shard_map/all_to_all | solution.py:153
  107.5 0.4 reshape.175
  107.9 0.2 copy.63
  108.0 0.1 reshape.176
  108.3 0.2 reshape.177
  108.5 0.2 fusion.83
  108.7 0.1 copy-done.1
  108.9 0.2 fusion.69
  109.1 0.2 pad_slice_fusion.16
  109.3 0.2 pad_slice_fusion.14
  109.5 0.3 slice-done
  110.0 0.7 fusion.67
  110.7 0.1 maximum_bitcast_fusion
  110.9 0.1 maximum_bitcast_fusion.1
  111.0 0.4 fusion.19
  111.4 0.7 copy-done.8
  112.1 1.9 %broadcast_select_fusion.1 = (f32[2,32,16,128]{3,2,0,1:T(8,128)S(1)}, f32[2,32,16,128]{3,2,0,1:T(8,128)S(1)}, f32[2,32,16,128]{3,2,0,1:T(8,128)S(1)}) fusion(pred[2,32]{0,1:T(8,128)(4,1)S(1)} %copy.71, pred[2,32]{0,1:T(8,128)(4,1)S(1)} %copy.72, f32[32,64,64]{2,1,0:T(8,128)S(1)} %copy-done.8, f32[2,32,16,128]{3,1,2,0:T(8,128)S(1)} %fusion.19), kind=kOutput, calls=%fused_computation.118 | convolution fusion | flops 103546880 | bytes 2621568 | tf_op jit(solution)/shard_map/apr,sazr->sazp/dot_general | solution.py:275
  114.0 1.9 %collective-permute-start.2 = (f32[2,32,16,128]{3,2,0,1:T(8,128)S(1)}, f32[2,32,16,128]{3,2,0,1:T(8,128)S(1)}, u32[]{:S(2)}, u32[]{:S(2)}) collective-permute-start(f32[2,32,16,128]{3,2,0,1:T(8,128)S(1)} %get-tuple-element.21), channel_id=1, source_target_pairs={{0,16},{16,32},{32,48},{48,64},{64,80},{80,96},{96,112},{112,128},... | collective-permute-start | bytes 1572872 | tf_op jit(solution)/shard_map/ppermute | solution.py:43
  115.9 5.8 %collective-permute-start.3 = (f32[2,32,16,128]{3,2,0,1:T(8,128)S(1)}, f32[2,32,16,128]{3,2,0,1:T(8,128)S(1)}, u32[]{:S(2)}, u32[]{:S(2)}) collective-permute-start(f32[2,32,16,128]{3,2,0,1:T(8,128)S(1)} %get-tuple-element.22), channel_id=1, source_target_pairs={{16,0},{32,16},{48,32},{64,48},{80,64},{96,80},{112,96},{128,112},... | collective-permute-start | bytes 1572872 | tf_op jit(solution)/shard_map/ppermute | solution.py:43
  121.8 0.9 copy.74
  122.6 4.0 %collective-permute-done.2 = f32[2,32,16,128]{3,2,0,1:T(8,128)S(1)} collective-permute-done((f32[2,32,16,128]{3,2,0,1:T(8,128)S(1)}, f32[2,32,16,128]{3,2,0,1:T(8,128)S(1)}, u32[]{:S(2)}, u32[]{:S(2)}) %collective-permute-start.2) | collective-permute-done | bytes 524320 | tf_op jit(solution)/shard_map/ppermute | solution.py:43
  126.6 1.8 %collective-permute-done.3 = f32[2,32,16,128]{3,2,0,1:T(8,128)S(1)} collective-permute-done((f32[2,32,16,128]{3,2,0,1:T(8,128)S(1)}, f32[2,32,16,128]{3,2,0,1:T(8,128)S(1)}, u32[]{:S(2)}, u32[]{:S(2)}) %collective-permute-start.3) | collective-permute-done | bytes 524320 | tf_op jit(solution)/shard_map/ppermute | solution.py:43
  128.3 0.2 add_add_fusion
  128.5 0.8 copy-done.2
  129.5 1.2 multiply_add_fusion
  (66 shorter events, 2.4 us)
Async XLA Ops:
  3.0 25.8 %copy-start = (f32[512,512]{1,0:T(8,128)S(1)}, f32[512,512]{1,0:T(8,128)}, u32[]{:S(2)}) copy-start(f32[512,512]{1,0:T(8,128)} %constant.62.clone) | copy-start | bytes 3145732
  3.7 24.8 %all-to-all-start = ((f32[16,40,128]{2,1,0:T(8,128)}), f32[16,40,128]{2,1,0:T(8,128)S(1)}, u32[]{:S(2)}, u32[]{:S(2)}) async-start(f32[16,40,128]{2,1,0:T(8,128)} %pad_maximum_fusion.3), calls=%async_computation | async-start | bytes 655360 | tf_op jit(solution)/shard_map/all_to_all | solution.py:131
  30.5 17.6 %all-to-all-start.1 = ((f32[16,40,128]{2,1,0:T(8,128)}), f32[16,40,128]{2,1,0:T(8,128)S(1)}, u32[]{:S(2)}, u32[]{:S(2)}) async-start(f32[16,40,128]{2,1,0:T(8,128)} %pad_maximum_fusion.4), calls=%async_computation.1 | async-start | bytes 655360 | tf_op jit(solution)/shard_map/all_to_all | solution.py:153
  34.3 21.7 %copy-start.6 = (f32[2]{0:T(128)S(1)}, f32[2]{0:T(128)}, u32[]{:S(2)}) copy-start(f32[2]{0:T(128)} %param.13) | copy-start | bytes 28
  48.3 9.4 %collective-permute-start = (f32[32,7,160]{2,0,1:T(8,128)S(1)}, f32[32,7,160]{2,0,1:T(8,128)S(1)}, u32[]{:S(2)}, u32[]{:S(2)}) collective-permute-start(f32[32,7,160]{2,0,1:T(8,128)S(1)} %get-tuple-element.25), channel_id=1, source_target_pairs={{0,16},{16,32},{32,48},{48,64},{64,80},{80,96},{96,112},{112,128},... | collective-permute-start | bytes 430088 | tf_op jit(solution)/shard_map/ppermute | solution.py:32
  50.2 9.3 %collective-permute-start.1 = (f32[32,7,160]{2,0,1:T(8,128)S(1)}, f32[32,7,160]{2,0,1:T(8,128)S(1)}, u32[]{:S(2)}, u32[]{:S(2)}) collective-permute-start(f32[32,7,160]{2,0,1:T(8,128)S(1)} %get-tuple-element.26), channel_id=1, source_target_pairs={{16,0},{32,16},{48,32},{64,48},{80,64},{96,80},{112,96},{128,112},... | collective-permute-start | bytes 430088 | tf_op jit(solution)/shard_map/ppermute | solution.py:35
  86.8 4.5 %copy-start.5 = (s32[2,32,1]{1,2,0:T(1,128)S(1)}, s32[2,32,1]{1,2,0:T(1,128)}, u32[]{:S(2)}) copy-start(s32[2,32,1]{1,2,0:T(1,128)} %param.17) | copy-start | bytes 772
  86.8 4.5 %copy-start.7 = (s32[2,32,1]{1,2,0:T(1,128)S(1)}, s32[2,32,1]{1,2,0:T(1,128)}, u32[]{:S(2)}) copy-start(s32[2,32,1]{1,2,0:T(1,128)} %param.16) | copy-start | bytes 772
  87.6 19.8 %all-to-all-start.3 = ((f32[16,53,128]{2,1,0:T(8,128)}), f32[16,53,128]{2,1,0:T(8,128)S(1)}, u32[]{:S(2)}, u32[]{:S(2)}) async-start(f32[16,53,128]{2,1,0:T(8,128)} %pad_maximum_fusion.2), calls=%async_computation.3 | async-start | bytes 917504 | tf_op jit(solution)/shard_map/all_to_all | solution.py:153
  108.2 0.7 copy-start.1
  109.1 0.8 slice-start
  110.9 1.2 copy-start.8
  114.0 12.6 %collective-permute-start.2 = (f32[2,32,16,128]{3,2,0,1:T(8,128)S(1)}, f32[2,32,16,128]{3,2,0,1:T(8,128)S(1)}, u32[]{:S(2)}, u32[]{:S(2)}) collective-permute-start(f32[2,32,16,128]{3,2,0,1:T(8,128)S(1)} %get-tuple-element.21), channel_id=1, source_target_pairs={{0,16},{16,32},{32,48},{48,64},{64,80},{80,96},{96,112},{112,128},... | collective-permute-start | bytes 1572872 | tf_op jit(solution)/shard_map/ppermute | solution.py:43
  115.9 12.4 %collective-permute-start.3 = (f32[2,32,16,128]{3,2,0,1:T(8,128)S(1)}, f32[2,32,16,128]{3,2,0,1:T(8,128)S(1)}, u32[]{:S(2)}, u32[]{:S(2)}) collective-permute-start(f32[2,32,16,128]{3,2,0,1:T(8,128)S(1)} %get-tuple-element.22), channel_id=1, source_target_pairs={{16,0},{32,16},{48,32},{64,48},{80,64},{96,80},{112,96},{128,112},... | collective-permute-start | bytes 1572872 | tf_op jit(solution)/shard_map/ppermute | solution.py:43
  128.3 0.9 copy-start.2
  128.3 1.0 copy-start.3
  128.3 1.1 copy-start.4

commit v9 on v7

--- a/solution.py
+++ b/solution.py
@@ -276,7 +276,19 @@
     from_below = shifted(place(2), "axial", 1)
     from_above = shifted(place(0), "axial", -1)
     loads = place(1) + from_below + from_above
-    for step_index in range(STEPS):
+    trial_stress = E_MOD * (strain - plastic)
+    excess = jnp.abs(trial_stress) - YIELD_ZERO
+    increment = (
+        trial_stress
+        * jnp.maximum(excess, 0.0)
+        / ((E_MOD + HARDEN) * jnp.maximum(jnp.abs(trial_stress), YIELD_ZERO))
+    )
+    plastic = plastic + increment
+    stress = E_MOD * (strain - plastic)
+    damped, stress = lax.optimization_barrier((DAMPING * velocity, STIFFNESS * stress))
+    velocity = damped + TIME_STEP * (loads[0] - stress)
+    strain = strain + TIME_STEP * velocity
+    for step_index in range(1, STEPS):
         velocity, strain, plastic = plastic_update(loads[step_index], velocity, strain, plastic)
     return (field_out, velocity, strain, plastic)
 

time: 131 us -> 130 us (level)
  no operation moved by 1% of the time
where the time goes in v9:
time: 130 us
  waiting for transfers between devices  44.2 us (34%)
  blocking collectives  42.5 us (33%)
  starting transfers between devices  19.2 us (15%)
  other arithmetic  9.44 us (7%)
  local copies, waits for them, and re-layouts  8.86 us (7%)
  matrix products  4.27 us (3%)
  between operations  1.31 us (1%)
    all_to_all x2, blocking collectives, transform(): lax.all_to_all(jnp.concatenate([main, rest], axis=1), 'azim', 0, 0, tiled...  42.5 us
    all_to_all x2, waiting for transfers between devices, transform(): lax.all_to_all(jnp.concatenate([mixed_main, mixed_rest], axis=1), 'azim',...  27.7 us
    ppermute x2, waiting for transfers between devices, shifted(): return lax.ppermute(array, axis, pairs)  9.57 us
    ppermute x2, starting transfers between devices, shifted(): return lax.ppermute(array, axis, pairs)  7.44 us
    all_to_all x2, starting transfers between devices, transform(): lax.all_to_all(jnp.concatenate([mixed_main, mixed_rest], axis=1), 'azim',...  7.28 us
    ppermute x1, waiting for transfers between devices, with_halo(): lax.ppermute(lax.slice_in_dim(block, block.shape[dim] - width, None, axis...  5.93 us
    div x5, other arithmetic, shards(): iterate = (right_side + nearby) / divisor  3.1 us
    dot_general x1, matrix products, shards(): jnp.einsum('apr,sazr->sazp', paired, moved, precision=lax.Precision.HIGH)  2.66 us
  transfers between devices with their start and end apart: 6, of which 6 were waited for; matrix products, arithmetic and copies ran while one was open for 2% of the time, Pallas kernels for 0%

profile of v9, /device:TPU:2, one launch (start us, length us, event | category | flops | bytes accessed | tf_op | source)
XLA Modules:
  0.0 129.7 jit_solution(3237162783363473885)
XLA Ops:
  0.6 1.1 multiply_bitcast_fusion
  1.8 0.1 reshape.161
  2.1 24.8 %all_to_all.20 = f32[16,40,128]{2,1,0:T(8,128)S(1)} all-to-all(f32[16,40,128]{2,1,0:T(8,128)S(1)} %pad_maximum_fusion.3), channel_id=1, replica_groups=mesh['axial'=16,'azim'=16] {'azim'}, dimensions={0} | all-to-all | bytes 655360 | tf_op jit(solution)/shard_map/all_to_all | solution.py:131
  26.9 0.1 reshape.163
  27.0 0.6 fusion.11
  27.7 0.1 copy.56
  27.9 0.1 reshape.165
  28.0 0.1 copy.55
  28.1 0.7 pad_maximum_fusion.4
  28.9 3.5 %all-to-all-start.1 = ((f32[16,40,128]{2,1,0:T(8,128)}), f32[16,40,128]{2,1,0:T(8,128)S(1)}, u32[]{:S(2)}, u32[]{:S(2)}) async-start(f32[16,40,128]{2,1,0:T(8,128)} %pad_maximum_fusion.4), calls=%async_computation.1 | async-start | bytes 655360 | tf_op jit(solution)/shard_map/all_to_all | solution.py:153
  32.6 13.9 %all-to-all-done.1 = f32[16,40,128]{2,1,0:T(8,128)S(1)} async-done(((f32[16,40,128]{2,1,0:T(8,128)}), f32[16,40,128]{2,1,0:T(8,128)S(1)}, u32[]{:S(2)}, u32[]{:S(2)}) %all-to-all-start.1) | async-done | bytes 327712 | tf_op jit(solution)/shard_map/all_to_all | solution.py:153
  46.5 0.1 reshape.166
  46.6 2.5 %collective-permute-start.1 = (f32[32,7,160]{2,0,1:T(8,128)S(1)}, f32[32,7,160]{2,0,1:T(8,128)S(1)}, u32[]{:S(2)}, u32[]{:S(2)}) collective-permute-start(f32[32,7,160]{2,0,1:T(8,128)S(1)} %get-tuple-element.32), channel_id=1, source_target_pairs={{16,0},{32,16},{48,32},{64,48},{80,64},{96,80},{112,96},{128,112},... | collective-permute-start | bytes 430088 | tf_op jit(solution)/shard_map/ppermute | solution.py:35
  49.2 1.9 %collective-permute-start = (f32[32,7,160]{2,0,1:T(8,128)S(1)}, f32[32,7,160]{2,0,1:T(8,128)S(1)}, u32[]{:S(2)}, u32[]{:S(2)}) collective-permute-start(f32[32,7,160]{2,0,1:T(8,128)S(1)} %get-tuple-element.31), channel_id=1, source_target_pairs={{0,16},{16,32},{32,48},{48,64},{64,80},{80,96},{96,112},{112,128},... | collective-permute-start | bytes 430088 | tf_op jit(solution)/shard_map/ppermute | solution.py:32
  51.2 0.6 fusion.80
  51.7 1.0 collective-permute-done.1
  52.7 5.9 %collective-permute-done = f32[32,7,160]{2,0,1:T(8,128)S(1)} collective-permute-done((f32[32,7,160]{2,0,1:T(8,128)S(1)}, f32[32,7,160]{2,0,1:T(8,128)S(1)}, u32[]{:S(2)}, u32[]{:S(2)}) %collective-permute-start) | collective-permute-done | bytes 143392 | tf_op jit(solution)/shard_map/ppermute | solution.py:32
  58.8 1.0 select_divide_fusion.4
  59.8 0.4 select_divide_fusion.3
  60.2 0.4 select_divide_fusion.2
  60.6 1.0 select_divide_fusion.1
  61.6 0.4 select_divide_fusion
  62.0 0.4 pad_slice_fusion.13
  62.3 0.2 fusion.44
  62.6 0.7 slice-done
  63.3 0.1 slice_multiply_fusion
  63.4 0.2 copy.58
  63.6 0.1 reshape.168
  64.1 0.2 reshape.169
  64.4 0.2 reshape.170
  64.7 17.7 %all_to_all.21 = f32[16,53,128]{2,1,0:T(8,128)S(1)} all-to-all(f32[16,53,128]{2,1,0:T(8,128)S(1)} %pad_maximum_fusion.1), channel_id=1, replica_groups=mesh['axial'=16,'azim'=16] {'azim'}, dimensions={0} | all-to-all | bytes 868352 | tf_op jit(solution)/shard_map/all_to_all | solution.py:131
  82.4 0.4 reshape.172
  82.9 0.6 fusion.15
  83.5 0.1 copy.61
  83.6 0.2 reshape.174
  83.9 0.1 copy.60
  84.0 0.8 pad_maximum_fusion.2
  84.8 3.7 %all-to-all-start.3 = ((f32[16,53,128]{2,1,0:T(8,128)}), f32[16,53,128]{2,1,0:T(8,128)S(1)}, u32[]{:S(2)}, u32[]{:S(2)}) async-start(f32[16,53,128]{2,1,0:T(8,128)} %pad_maximum_fusion.2), calls=%async_computation.3 | async-start | bytes 917504 | tf_op jit(solution)/shard_map/all_to_all | solution.py:153
  88.7 0.1 select_reduce_fusion
  89.1 13.9 %all-to-all-done.3 = f32[16,53,128]{2,1,0:T(8,128)S(1)} async-done(((f32[16,53,128]{2,1,0:T(8,128)}), f32[16,53,128]{2,1,0:T(8,128)S(1)}, u32[]{:S(2)}, u32[]{:S(2)}) %all-to-all-start.3) | async-done | bytes 434208 | tf_op jit(solution)/shard_map/all_to_all | solution.py:153
  102.9 0.4 reshape.175
  103.4 0.2 copy.63
  103.5 0.1 reshape.176
  103.8 0.2 reshape.177
  104.0 0.2 fusion.76
  104.2 0.1 copy-done.4
  104.4 0.2 fusion.63
  104.6 0.2 pad_slice_fusion.27
  104.8 0.3 slice-done.1
  105.3 0.2 pad_slice_fusion.25
  105.5 0.8 fusion.61
  106.2 0.1 maximum_bitcast_fusion.1
  106.4 0.1 maximum_bitcast_fusion
  106.5 0.4 fusion.19
  106.9 0.7 copy-done.10
  107.6 2.7 %broadcast_select_fusion.1 = (f32[2,32,16,128]{3,2,0,1:T(8,128)S(1)}, f32[2,32,16,128]{3,2,0,1:T(8,128)}, f32[2,32,16,128]{3,2,0,1:T(8,128)S(1)}) fusion(pred[2,32]{0,1:T(8,128)(4,1)S(1)} %copy.71, pred[2,32]{0,1:T(8,128)(4,1)S(1)} %copy.72, f32[32,64,64]{2,1,0:T(8,128)S(1)} %copy-done.10, f32[2,32,16,128]{3,1,2,0:T(8,128)S(1)} %fusion.19), kind=kOutput, calls=%fused_computation.126 | convolution fusion | flops 103546880 | bytes 2621568 | tf_op jit(solution)/shard_map/apr,sazr->sazp/dot_general | solution.py:271
  110.3 5.5 %collective-permute-start.3 = (f32[2,32,16,128]{3,2,0,1:T(8,128)}, f32[2,32,16,128]{3,2,0,1:T(8,128)S(1)}, u32[]{:S(2)}, u32[]{:S(2)}) collective-permute-start(f32[2,32,16,128]{3,2,0,1:T(8,128)} %get-tuple-element.28), channel_id=1, source_target_pairs={{16,0},{32,16},{48,32},{64,48},{80,64},{96,80},{112,96},{128,112},... | collective-permute-start | bytes 1572872 | tf_op jit(solution)/shard_map/ppermute | solution.py:43
  115.8 1.9 %collective-permute-start.2 = (f32[2,32,16,128]{3,2,0,1:T(8,128)S(1)}, f32[2,32,16,128]{3,2,0,1:T(8,128)S(1)}, u32[]{:S(2)}, u32[]{:S(2)}) collective-permute-start(f32[2,32,16,128]{3,2,0,1:T(8,128)S(1)} %get-tuple-element.27), channel_id=1, source_target_pairs={{0,16},{16,32},{32,48},{48,64},{64,80},{80,96},{96,112},{112,128},... | collective-permute-start | bytes 1572872 | tf_op jit(solution)/shard_map/ppermute | solution.py:43
  117.8 0.1 subtract_multiply_fusion.1
  118.0 0.9 copy.74
  118.8 4.0 %collective-permute-done.3 = f32[2,32,16,128]{3,2,0,1:T(8,128)S(1)} collective-permute-done((f32[2,32,16,128]{3,2,0,1:T(8,128)}, f32[2,32,16,128]{3,2,0,1:T(8,128)S(1)}, u32[]{:S(2)}, u32[]{:S(2)}) %collective-permute-start.3) | collective-permute-done | bytes 524320 | tf_op jit(solution)/shard_map/ppermute | solution.py:43
  122.8 5.6 %collective-permute-done.2 = f32[2,32,16,128]{3,2,0,1:T(8,128)S(1)} collective-permute-done((f32[2,32,16,128]{3,2,0,1:T(8,128)S(1)}, f32[2,32,16,128]{3,2,0,1:T(8,128)S(1)}, u32[]{:S(2)}, u32[]{:S(2)}) %collective-permute-start.2) | collective-permute-done | bytes 524320 | tf_op jit(solution)/shard_map/ppermute | solution.py:43
  128.4 0.2 add_add_fusion
  128.6 1.2 multiply_add_fusion.2
  (65 shorter events, 1.9 us)
Async XLA Ops:
  0.6 1.3 %copy-start.6 = (f32[32,16,128]{2,1,0:T(8,128)S(1)}, f32[32,16,128]{2,1,0:T(8,128)}, u32[]{:S(2)}) copy-start(f32[32,16,128]{2,1,0:T(8,128)} %param.14) | copy-start | bytes 786436
  2.1 25.0 %copy-start = (f32[512,512]{1,0:T(8,128)S(1)}, f32[512,512]{1,0:T(8,128)}, u32[]{:S(2)}) copy-start(f32[512,512]{1,0:T(8,128)} %constant.62.clone) | copy-start | bytes 3145732
  28.9 17.6 %all-to-all-start.1 = ((f32[16,40,128]{2,1,0:T(8,128)}), f32[16,40,128]{2,1,0:T(8,128)S(1)}, u32[]{:S(2)}, u32[]{:S(2)}) async-start(f32[16,40,128]{2,1,0:T(8,128)} %pad_maximum_fusion.4), calls=%async_computation.1 | async-start | bytes 655360 | tf_op jit(solution)/shard_map/all_to_all | solution.py:153
  32.4 18.7 %copy-start.8 = (f32[2]{0:T(128)S(1)}, f32[2]{0:T(128)}, u32[]{:S(2)}) copy-start(f32[2]{0:T(128)} %param.13) | copy-start | bytes 28
  46.6 6.1 %collective-permute-start.1 = (f32[32,7,160]{2,0,1:T(8,128)S(1)}, f32[32,7,160]{2,0,1:T(8,128)S(1)}, u32[]{:S(2)}, u32[]{:S(2)}) collective-permute-start(f32[32,7,160]{2,0,1:T(8,128)S(1)} %get-tuple-element.32), channel_id=1, source_target_pairs={{16,0},{32,16},{48,32},{64,48},{80,64},{96,80},{112,96},{128,112},... | collective-permute-start | bytes 430088 | tf_op jit(solution)/shard_map/ppermute | solution.py:35
  49.2 9.4 %collective-permute-start = (f32[32,7,160]{2,0,1:T(8,128)S(1)}, f32[32,7,160]{2,0,1:T(8,128)S(1)}, u32[]{:S(2)}, u32[]{:S(2)}) collective-permute-start(f32[32,7,160]{2,0,1:T(8,128)S(1)} %get-tuple-element.31), channel_id=1, source_target_pairs={{0,16},{16,32},{32,48},{48,64},{64,80},{80,96},{96,112},{112,128},... | collective-permute-start | bytes 430088 | tf_op jit(solution)/shard_map/ppermute | solution.py:32
  60.5 1.0 copy-start.1
  62.3 1.0 slice-start
  84.0 4.7 %copy-start.7 = (s32[2,32,1]{1,2,0:T(1,128)S(1)}, s32[2,32,1]{1,2,0:T(1,128)}, u32[]{:S(2)}) copy-start(s32[2,32,1]{1,2,0:T(1,128)} %param.17) | copy-start | bytes 772
  84.0 4.6 %copy-start.9 = (s32[2,32,1]{1,2,0:T(1,128)S(1)}, s32[2,32,1]{1,2,0:T(1,128)}, u32[]{:S(2)}) copy-start(s32[2,32,1]{1,2,0:T(1,128)} %param.16) | copy-start | bytes 772
  84.8 18.1 %all-to-all-start.3 = ((f32[16,53,128]{2,1,0:T(8,128)}), f32[16,53,128]{2,1,0:T(8,128)S(1)}, u32[]{:S(2)}, u32[]{:S(2)}) async-start(f32[16,53,128]{2,1,0:T(8,128)} %pad_maximum_fusion.2), calls=%async_computation.3 | async-start | bytes 917504 | tf_op jit(solution)/shard_map/all_to_all | solution.py:153
  103.7 0.7 copy-start.4
  104.4 0.8 slice-start.1
  106.4 1.2 copy-start.10
  107.6 10.2 %copy-start.2 = (f32[32,16,128]{2,1,0:T(8,128)S(1)}, f32[32,16,128]{2,1,0:T(8,128)}, u32[]{:S(2)}) copy-start(f32[32,16,128]{2,1,0:T(8,128)} %param.19) | copy-start | bytes 786436
  107.6 10.2 %copy-start.3 = (f32[32,16,128]{2,1,0:T(8,128)S(1)}, f32[32,16,128]{2,1,0:T(8,128)}, u32[]{:S(2)}) copy-start(f32[32,16,128]{2,1,0:T(8,128)} %param.20) | copy-start | bytes 786436
  107.6 10.2 %copy-start.5 = (f32[32,16,128]{2,1,0:T(8,128)S(1)}, f32[32,16,128]{2,1,0:T(8,128)}, u32[]{:S(2)}) copy-start(f32[32,16,128]{2,1,0:T(8,128)} %param.18) | copy-start | bytes 786436
  110.3 12.5 %collective-permute-start.3 = (f32[2,32,16,128]{3,2,0,1:T(8,128)}, f32[2,32,16,128]{3,2,0,1:T(8,128)S(1)}, u32[]{:S(2)}, u32[]{:S(2)}) collective-permute-start(f32[2,32,16,128]{3,2,0,1:T(8,128)} %get-tuple-element.28), channel_id=1, source_target_pairs={{16,0},{32,16},{48,32},{64,48},{80,64},{96,80},{112,96},{128,112},... | collective-permute-start | bytes 1572872 | tf_op jit(solution)/shard_map/ppermute | solution.py:43
  115.8 12.6 %collective-permute-start.2 = (f32[2,32,16,128]{3,2,0,1:T(8,128)S(1)}, f32[2,32,16,128]{3,2,0,1:T(8,128)S(1)}, u32[]{:S(2)}, u32[]{:S(2)}) collective-permute-start(f32[2,32,16,128]{3,2,0,1:T(8,128)S(1)} %get-tuple-element.27), channel_id=1, source_target_pairs={{0,16},{16,32},{32,48},{48,64},{64,80},{80,96},{96,112},{112,128},... | collective-permute-start | bytes 1572872 | tf_op jit(solution)/shard_map/ppermute | solution.py:43

commit v10 on v9

--- a/solution.py
+++ b/solution.py
@@ -257,7 +257,7 @@
     slot_table = relay_slot[:, :, 0][:, :, None] == slot_range[None, None, :]
     owner_at = jnp.sum(jnp.where(slot_table, relay_owner[:, :, 0][:, :, None], 0), axis=1)
     moved = jnp.einsum(
-        "sjcw,sjp->spcw", tiles, slot_table.astype(jnp.float32), precision=HIGH
+        "sjcw,sjp->spcw", tiles, slot_table.astype(jnp.float32), precision=lax.Precision.HIGH
     )
 
     blank = jnp.zeros_like(tile_weight)

time: 130 us -> 130 us (level)
  no operation moved by 1% of the time
where the time goes in v10:
time: 130 us
  waiting for transfers between devices  44.2 us (34%)
  blocking collectives  42.5 us (33%)
  starting transfers between devices  19.2 us (15%)
  other arithmetic  9.44 us (7%)
  local copies, waits for them, and re-layouts  8.95 us (7%)
  matrix products  4.18 us (3%)
  between operations  1.31 us (1%)
    all_to_all x2, blocking collectives, transform(): lax.all_to_all(jnp.concatenate([main, rest], axis=1), 'azim', 0, 0, tiled...  42.5 us
    all_to_all x2, waiting for transfers between devices, transform(): lax.all_to_all(jnp.concatenate([mixed_main, mixed_rest], axis=1), 'azim',...  27.7 us
    ppermute x2, waiting for transfers between devices, shifted(): return lax.ppermute(array, axis, pairs)  9.57 us
    ppermute x2, starting transfers between devices, shifted(): return lax.ppermute(array, axis, pairs)  7.44 us
    all_to_all x2, starting transfers between devices, transform(): lax.all_to_all(jnp.concatenate([mixed_main, mixed_rest], axis=1), 'azim',...  7.28 us
    ppermute x1, waiting for transfers between devices, with_halo(): lax.ppermute(lax.slice_in_dim(block, block.shape[dim] - width, None, axis...  5.93 us
    div x5, other arithmetic, shards(): iterate = (right_side + nearby) / divisor  3.1 us
    dot_general x1, matrix products, shards(): jnp.einsum('apr,sazr->sazp', paired, moved, precision=lax.Precision.HIGH)  2.66 us
  transfers between devices with their start and end apart: 6, of which 6 were waited for; matrix products, arithmetic and copies ran while one was open for 2% of the time, Pallas kernels for 0%

profile of v10, /device:TPU:2, one launch (start us, length us, event | category | flops | bytes accessed | tf_op | source)
XLA Modules:
  0.0 129.7 jit_solution(12254832011939268799)
XLA Ops:
  0.6 1.1 multiply_bitcast_fusion
  1.8 0.1 reshape.161
  2.1 24.8 %all_to_all.20 = f32[16,40,128]{2,1,0:T(8,128)S(1)} all-to-all(f32[16,40,128]{2,1,0:T(8,128)S(1)} %pad_maximum_fusion.3), channel_id=1, replica_groups=mesh['axial'=16,'azim'=16] {'azim'}, dimensions={0} | all-to-all | bytes 655360 | tf_op jit(solution)/shard_map/all_to_all | solution.py:131
  26.9 0.1 reshape.163
  27.0 0.6 fusion.11
  27.7 0.1 copy.56
  27.9 0.1 reshape.165
  28.0 0.1 copy.55
  28.1 0.7 pad_maximum_fusion.4
  28.9 3.5 %all-to-all-start.1 = ((f32[16,40,128]{2,1,0:T(8,128)}), f32[16,40,128]{2,1,0:T(8,128)S(1)}, u32[]{:S(2)}, u32[]{:S(2)}) async-start(f32[16,40,128]{2,1,0:T(8,128)} %pad_maximum_fusion.4), calls=%async_computation.1 | async-start | bytes 655360 | tf_op jit(solution)/shard_map/all_to_all | solution.py:153
  32.6 13.9 %all-to-all-done.1 = f32[16,40,128]{2,1,0:T(8,128)S(1)} async-done(((f32[16,40,128]{2,1,0:T(8,128)}), f32[16,40,128]{2,1,0:T(8,128)S(1)}, u32[]{:S(2)}, u32[]{:S(2)}) %all-to-all-start.1) | async-done | bytes 327712 | tf_op jit(solution)/shard_map/all_to_all | solution.py:153
  46.5 0.1 reshape.166
  46.6 2.5 %collective-permute-start.1 = (f32[32,7,160]{2,0,1:T(8,128)S(1)}, f32[32,7,160]{2,0,1:T(8,128)S(1)}, u32[]{:S(2)}, u32[]{:S(2)}) collective-permute-start(f32[32,7,160]{2,0,1:T(8,128)S(1)} %get-tuple-element.32), channel_id=1, source_target_pairs={{16,0},{32,16},{48,32},{64,48},{80,64},{96,80},{112,96},{128,112},... | collective-permute-start | bytes 430088 | tf_op jit(solution)/shard_map/ppermute | solution.py:35
  49.2 1.9 %collective-permute-start = (f32[32,7,160]{2,0,1:T(8,128)S(1)}, f32[32,7,160]{2,0,1:T(8,128)S(1)}, u32[]{:S(2)}, u32[]{:S(2)}) collective-permute-start(f32[32,7,160]{2,0,1:T(8,128)S(1)} %get-tuple-element.31), channel_id=1, source_target_pairs={{0,16},{16,32},{32,48},{48,64},{64,80},{80,96},{96,112},{112,128},... | collective-permute-start | bytes 430088 | tf_op jit(solution)/shard_map/ppermute | solution.py:32
  51.2 0.6 fusion.80
  51.7 1.0 collective-permute-done.1
  52.7 5.9 %collective-permute-done = f32[32,7,160]{2,0,1:T(8,128)S(1)} collective-permute-done((f32[32,7,160]{2,0,1:T(8,128)S(1)}, f32[32,7,160]{2,0,1:T(8,128)S(1)}, u32[]{:S(2)}, u32[]{:S(2)}) %collective-permute-start) | collective-permute-done | bytes 143392 | tf_op jit(solution)/shard_map/ppermute | solution.py:32
  58.8 1.0 select_divide_fusion.4
  59.8 0.4 select_divide_fusion.3
  60.2 0.4 select_divide_fusion.2
  60.6 1.0 select_divide_fusion.1
  61.6 0.4 select_divide_fusion
  62.0 0.4 pad_slice_fusion.13
  62.3 0.2 fusion.44
  62.6 0.7 slice-done
  63.3 0.1 slice_multiply_fusion
  63.4 0.2 copy.58
  63.6 0.1 reshape.168
  64.1 0.2 reshape.169
  64.4 0.2 reshape.170
  64.7 17.7 %all_to_all.21 = f32[16,53,128]{2,1,0:T(8,128)S(1)} all-to-all(f32[16,53,128]{2,1,0:T(8,128)S(1)} %pad_maximum_fusion.1), channel_id=1, replica_groups=mesh['axial'=16,'azim'=16] {'azim'}, dimensions={0} | all-to-all | bytes 868352 | tf_op jit(solution)/shard_map/all_to_all | solution.py:131
  82.4 0.4 reshape.172
  82.9 0.6 fusion.15
  83.5 0.1 copy.61
  83.6 0.2 reshape.174
  83.9 0.1 copy.60
  84.0 0.8 pad_maximum_fusion.2
  84.8 3.7 %all-to-all-start.3 = ((f32[16,53,128]{2,1,0:T(8,128)}), f32[16,53,128]{2,1,0:T(8,128)S(1)}, u32[]{:S(2)}, u32[]{:S(2)}) async-start(f32[16,53,128]{2,1,0:T(8,128)} %pad_maximum_fusion.2), calls=%async_computation.3 | async-start | bytes 917504 | tf_op jit(solution)/shard_map/all_to_all | solution.py:153
  88.7 0.1 select_reduce_fusion
  89.1 13.9 %all-to-all-done.3 = f32[16,53,128]{2,1,0:T(8,128)S(1)} async-done(((f32[16,53,128]{2,1,0:T(8,128)}), f32[16,53,128]{2,1,0:T(8,128)S(1)}, u32[]{:S(2)}, u32[]{:S(2)}) %all-to-all-start.3) | async-done | bytes 434208 | tf_op jit(solution)/shard_map/all_to_all | solution.py:153
  102.9 0.4 reshape.175
  103.4 0.2 copy.63
  103.5 0.1 reshape.176
  103.8 0.2 reshape.177
  104.0 0.2 fusion.76
  104.2 0.1 copy-done.4
  104.4 0.2 fusion.63
  104.6 0.2 pad_slice_fusion.27
  104.8 0.3 slice-done.1
  105.3 0.2 pad_slice_fusion.25
  105.5 0.8 fusion.61
  106.2 0.1 maximum_bitcast_fusion.1
  106.4 0.1 maximum_bitcast_fusion
  106.5 0.3 fusion.19
  106.8 0.8 copy-done.10
  107.6 2.7 %broadcast_select_fusion.1 = (f32[2,32,16,128]{3,2,0,1:T(8,128)S(1)}, f32[2,32,16,128]{3,2,0,1:T(8,128)}, f32[2,32,16,128]{3,2,0,1:T(8,128)S(1)}) fusion(pred[2,32]{0,1:T(8,128)(4,1)S(1)} %copy.71, pred[2,32]{0,1:T(8,128)(4,1)S(1)} %copy.72, f32[32,64,64]{2,1,0:T(8,128)S(1)} %copy-done.10, f32[2,32,16,128]{3,1,2,0:T(8,128)S(1)} %fusion.19), kind=kOutput, calls=%fused_computation.126 | convolution fusion | flops 103546880 | bytes 2621568 | tf_op jit(solution)/shard_map/apr,sazr->sazp/dot_general | solution.py:271
  110.3 5.5 %collective-permute-start.3 = (f32[2,32,16,128]{3,2,0,1:T(8,128)}, f32[2,32,16,128]{3,2,0,1:T(8,128)S(1)}, u32[]{:S(2)}, u32[]{:S(2)}) collective-permute-start(f32[2,32,16,128]{3,2,0,1:T(8,128)} %get-tuple-element.28), channel_id=1, source_target_pairs={{16,0},{32,16},{48,32},{64,48},{80,64},{96,80},{112,96},{128,112},... | collective-permute-start | bytes 1572872 | tf_op jit(solution)/shard_map/ppermute | solution.py:43
  115.8 1.9 %collective-permute-start.2 = (f32[2,32,16,128]{3,2,0,1:T(8,128)S(1)}, f32[2,32,16,128]{3,2,0,1:T(8,128)S(1)}, u32[]{:S(2)}, u32[]{:S(2)}) collective-permute-start(f32[2,32,16,128]{3,2,0,1:T(8,128)S(1)} %get-tuple-element.27), channel_id=1, source_target_pairs={{0,16},{16,32},{32,48},{48,64},{64,80},{80,96},{96,112},{112,128},... | collective-permute-start | bytes 1572872 | tf_op jit(solution)/shard_map/ppermute | solution.py:43
  117.8 0.1 subtract_multiply_fusion.1
  118.0 0.9 copy.74
  118.8 4.0 %collective-permute-done.3 = f32[2,32,16,128]{3,2,0,1:T(8,128)S(1)} collective-permute-done((f32[2,32,16,128]{3,2,0,1:T(8,128)}, f32[2,32,16,128]{3,2,0,1:T(8,128)S(1)}, u32[]{:S(2)}, u32[]{:S(2)}) %collective-permute-start.3) | collective-permute-done | bytes 524320 | tf_op jit(solution)/shard_map/ppermute | solution.py:43
  122.8 5.6 %collective-permute-done.2 = f32[2,32,16,128]{3,2,0,1:T(8,128)S(1)} collective-permute-done((f32[2,32,16,128]{3,2,0,1:T(8,128)S(1)}, f32[2,32,16,128]{3,2,0,1:T(8,128)S(1)}, u32[]{:S(2)}, u32[]{:S(2)}) %collective-permute-start.2) | collective-permute-done | bytes 524320 | tf_op jit(solution)/shard_map/ppermute | solution.py:43
  128.4 0.2 add_add_fusion
  128.6 1.2 multiply_add_fusion.2
  (65 shorter events, 1.9 us)
Async XLA Ops:
  0.6 1.3 %copy-start.6 = (f32[32,16,128]{2,1,0:T(8,128)S(1)}, f32[32,16,128]{2,1,0:T(8,128)}, u32[]{:S(2)}) copy-start(f32[32,16,128]{2,1,0:T(8,128)} %param.14) | copy-start | bytes 786436
  2.1 25.0 %copy-start = (f32[512,512]{1,0:T(8,128)S(1)}, f32[512,512]{1,0:T(8,128)}, u32[]{:S(2)}) copy-start(f32[512,512]{1,0:T(8,128)} %constant.62.clone) | copy-start | bytes 3145732
  28.9 17.6 %all-to-all-start.1 = ((f32[16,40,128]{2,1,0:T(8,128)}), f32[16,40,128]{2,1,0:T(8,128)S(1)}, u32[]{:S(2)}, u32[]{:S(2)}) async-start(f32[16,40,128]{2,1,0:T(8,128)} %pad_maximum_fusion.4), calls=%async_computation.1 | async-start | bytes 655360 | tf_op jit(solution)/shard_map/all_to_all | solution.py:153
  32.4 18.7 %copy-start.8 = (f32[2]{0:T(128)S(1)}, f32[2]{0:T(128)}, u32[]{:S(2)}) copy-start(f32[2]{0:T(128)} %param.13) | copy-start | bytes 28
  46.6 6.1 %collective-permute-start.1 = (f32[32,7,160]{2,0,1:T(8,128)S(1)}, f32[32,7,160]{2,0,1:T(8,128)S(1)}, u32[]{:S(2)}, u32[]{:S(2)}) collective-permute-start(f32[32,7,160]{2,0,1:T(8,128)S(1)} %get-tuple-element.32), channel_id=1, source_target_pairs={{16,0},{32,16},{48,32},{64,48},{80,64},{96,80},{112,96},{128,112},... | collective-permute-start | bytes 430088 | tf_op jit(solution)/shard_map/ppermute | solution.py:35
  49.2 9.4 %collective-permute-start = (f32[32,7,160]{2,0,1:T(8,128)S(1)}, f32[32,7,160]{2,0,1:T(8,128)S(1)}, u32[]{:S(2)}, u32[]{:S(2)}) collective-permute-start(f32[32,7,160]{2,0,1:T(8,128)S(1)} %get-tuple-element.31), channel_id=1, source_target_pairs={{0,16},{16,32},{32,48},{48,64},{64,80},{80,96},{96,112},{112,128},... | collective-permute-start | bytes 430088 | tf_op jit(solution)/shard_map/ppermute | solution.py:32
  60.5 1.0 copy-start.1
  62.3 1.0 slice-start
  84.0 4.7 %copy-start.7 = (s32[2,32,1]{1,2,0:T(1,128)S(1)}, s32[2,32,1]{1,2,0:T(1,128)}, u32[]{:S(2)}) copy-start(s32[2,32,1]{1,2,0:T(1,128)} %param.17) | copy-start | bytes 772
  84.0 4.6 %copy-start.9 = (s32[2,32,1]{1,2,0:T(1,128)S(1)}, s32[2,32,1]{1,2,0:T(1,128)}, u32[]{:S(2)}) copy-start(s32[2,32,1]{1,2,0:T(1,128)} %param.16) | copy-start | bytes 772
  84.8 18.1 %all-to-all-start.3 = ((f32[16,53,128]{2,1,0:T(8,128)}), f32[16,53,128]{2,1,0:T(8,128)S(1)}, u32[]{:S(2)}, u32[]{:S(2)}) async-start(f32[16,53,128]{2,1,0:T(8,128)} %pad_maximum_fusion.2), calls=%async_computation.3 | async-start | bytes 917504 | tf_op jit(solution)/shard_map/all_to_all | solution.py:153
  103.7 0.7 copy-start.4
  104.4 0.8 slice-start.1
  106.4 1.2 copy-start.10
  107.6 10.2 %copy-start.2 = (f32[32,16,128]{2,1,0:T(8,128)S(1)}, f32[32,16,128]{2,1,0:T(8,128)}, u32[]{:S(2)}) copy-start(f32[32,16,128]{2,1,0:T(8,128)} %param.19) | copy-start | bytes 786436
  107.6 10.2 %copy-start.3 = (f32[32,16,128]{2,1,0:T(8,128)S(1)}, f32[32,16,128]{2,1,0:T(8,128)}, u32[]{:S(2)}) copy-start(f32[32,16,128]{2,1,0:T(8,128)} %param.20) | copy-start | bytes 786436
  107.6 10.2 %copy-start.5 = (f32[32,16,128]{2,1,0:T(8,128)S(1)}, f32[32,16,128]{2,1,0:T(8,128)}, u32[]{:S(2)}) copy-start(f32[32,16,128]{2,1,0:T(8,128)} %param.18) | copy-start | bytes 786436
  110.3 12.5 %collective-permute-start.3 = (f32[2,32,16,128]{3,2,0,1:T(8,128)}, f32[2,32,16,128]{3,2,0,1:T(8,128)S(1)}, u32[]{:S(2)}, u32[]{:S(2)}) collective-permute-start(f32[2,32,16,128]{3,2,0,1:T(8,128)} %get-tuple-element.28), channel_id=1, source_target_pairs={{16,0},{32,16},{48,32},{64,48},{80,64},{96,80},{112,96},{128,112},... | collective-permute-start | bytes 1572872 | tf_op jit(solution)/shard_map/ppermute | solution.py:43
  115.8 12.6 %collective-permute-start.2 = (f32[2,32,16,128]{3,2,0,1:T(8,128)S(1)}, f32[2,32,16,128]{3,2,0,1:T(8,128)S(1)}, u32[]{:S(2)}, u32[]{:S(2)}) collective-permute-start(f32[2,32,16,128]{3,2,0,1:T(8,128)S(1)} %get-tuple-element.27), channel_id=1, source_target_pairs={{0,16},{16,32},{32,48},{48,64},{64,80},{80,96},{96,112},{112,128},... | collective-permute-start | bytes 1572872 | tf_op jit(solution)/shard_map/ppermute | solution.py:43

commit v11 on v9

--- a/solution.py
+++ b/solution.py
@@ -268,6 +268,7 @@
         ],
         axis=1,
     )
+    paired = lax.optimization_barrier(paired)
     mapped = jnp.einsum("apr,sazr->sazp", paired, moved, precision=lax.Precision.HIGH)
 
     def place(target):

time: 130 us -> 137 us (1.054); the launches traced: 130 us -> 135 us
  waiting for transfers between devices: 44.2 us -> 35.3 us
  other arithmetic: 9.44 us -> 14.5 us
  starting transfers between devices: 19.2 us -> 22.7 us
  blocking collectives: 42.5 us -> 45.5 us
  local copies, waits for them, and re-layouts: 8.86 us -> 10.7 us
    ppermute x1, waiting for transfers between devices: 5.93 us -> 1.15 us  [with_halo(): lax.ppermute(lax.slice_in_dim(block, block.shape[dim] - width, None, axis...]
    ppermute x2, waiting for transfers between devices: 9.57 us -> 4.94 us  [shifted(): return lax.ppermute(array, axis, pairs)]
    ppermute x1, starting transfers between devices: 2.55 us -> 5.75 us  [with_halo(): lax.ppermute(lax.slice_in_dim(block, 0, width, axis=dim), axis, backward)]
    all_to_all x2, blocking collectives: 42.5 us -> 45.5 us  [transform(): lax.all_to_all(jnp.concatenate([main, rest], axis=1), 'azim', 0, 0, tiled...]
    concatenate x0 -> x1, other arithmetic: none -> 1.94 us  [shards(): jnp.concatenate([jnp.concatenate([tile_weight, blank], axis=2), jnp.conca...]
  transfers between devices with their start and end apart: 6 -> 6, of which waited for: 6 -> 6; matrix products, arithmetic and copies ran while one was open for 2% -> 4% of each run, Pallas kernels for 0% -> 0%
where the time goes in v11:
time: 137 us; the launch traced here: 135 us
  blocking collectives  45.5 us (33%)
  waiting for transfers between devices  35.3 us (26%)
  starting transfers between devices  22.7 us (17%)
  other arithmetic  14.5 us (11%)
  local copies, waits for them, and re-layouts  10.7 us (8%)
  matrix products  4.49 us (3%)
    all_to_all x2, blocking collectives, transform(): lax.all_to_all(jnp.concatenate([main, rest], axis=1), 'azim', 0, 0, tiled...  45.5 us
    all_to_all x2, waiting for transfers between devices, transform(): lax.all_to_all(jnp.concatenate([mixed_main, mixed_rest], axis=1), 'azim',...  27.5 us
    ppermute x2, starting transfers between devices, shifted(): return lax.ppermute(array, axis, pairs)  7.79 us
    all_to_all x2, starting transfers between devices, transform(): lax.all_to_all(jnp.concatenate([mixed_main, mixed_rest], axis=1), 'azim',...  7.28 us
    ppermute x1, starting transfers between devices, with_halo(): lax.ppermute(lax.slice_in_dim(block, 0, width, axis=dim), axis, backward)  5.75 us
    ppermute x2, waiting for transfers between devices, shifted(): return lax.ppermute(array, axis, pairs)  4.94 us
    div x5, other arithmetic, shards(): iterate = (right_side + nearby) / divisor  3.12 us
    dot_general x1, matrix products, shards(): jnp.einsum('apr,sazr->sazp', paired, moved, precision=lax.Precision.HIGH)  2.88 us
  transfers between devices with their start and end apart: 6, of which 6 were waited for; matrix products, arithmetic and copies ran while one was open for 4% of the time, Pallas kernels for 0%

profile of v11, /device:TPU:2, one launch (start us, length us, event | category | flops | bytes accessed | tf_op | source)
XLA Modules:
  0.0 134.5 jit_solution(16855325652931760749)
XLA Ops:
  0.6 1.0 copy.102
  1.7 1.2 multiply_bitcast_fusion
  2.9 0.1 reshape.161
  3.1 24.6 %all_to_all.20 = f32[16,40,128]{2,1,0:T(8,128)S(1)} all-to-all(f32[16,40,128]{2,1,0:T(8,128)S(1)} %pad_maximum_fusion.3), channel_id=1, replica_groups=mesh['axial'=16,'azim'=16] {'azim'}, dimensions={0} | all-to-all | bytes 655360 | tf_op jit(solution)/shard_map/all_to_all | solution.py:131
  27.7 0.1 reshape.163
  27.9 0.6 fusion.5
  28.6 0.1 copy.55
  28.7 0.1 copy.56
  28.9 0.1 reshape.165
  29.0 0.7 pad_maximum_fusion.4
  29.7 3.5 %all-to-all-start.1 = ((f32[16,40,128]{2,1,0:T(8,128)}), f32[16,40,128]{2,1,0:T(8,128)S(1)}, u32[]{:S(2)}, u32[]{:S(2)}) async-start(f32[16,40,128]{2,1,0:T(8,128)} %pad_maximum_fusion.4), calls=%async_computation.1 | async-start | bytes 655360 | tf_op jit(solution)/shard_map/all_to_all | solution.py:153
  33.4 13.9 %all-to-all-done.1 = f32[16,40,128]{2,1,0:T(8,128)S(1)} async-done(((f32[16,40,128]{2,1,0:T(8,128)}), f32[16,40,128]{2,1,0:T(8,128)S(1)}, u32[]{:S(2)}, u32[]{:S(2)}) %all-to-all-start.1) | async-done | bytes 327712 | tf_op jit(solution)/shard_map/all_to_all | solution.py:153
  47.3 0.1 reshape.166
  47.5 1.9 %collective-permute-start = (f32[32,7,160]{2,0,1:T(8,128)S(1)}, f32[32,7,160]{2,0,1:T(8,128)S(1)}, u32[]{:S(2)}, u32[]{:S(2)}) collective-permute-start(f32[32,7,160]{2,0,1:T(8,128)S(1)} %get-tuple-element.31), channel_id=1, source_target_pairs={{0,16},{16,32},{32,48},{48,64},{64,80},{80,96},{96,112},{112,128},... | collective-permute-start | bytes 430088 | tf_op jit(solution)/shard_map/ppermute | solution.py:32
  49.4 5.8 %collective-permute-start.1 = (f32[32,7,160]{2,0,1:T(8,128)S(1)}, f32[32,7,160]{2,0,1:T(8,128)S(1)}, u32[]{:S(2)}, u32[]{:S(2)}) collective-permute-start(f32[32,7,160]{2,0,1:T(8,128)S(1)} %get-tuple-element.32), channel_id=1, source_target_pairs={{16,0},{32,16},{48,32},{64,48},{80,64},{96,80},{112,96},{128,112},... | collective-permute-start | bytes 430088 | tf_op jit(solution)/shard_map/ppermute | solution.py:35
  55.2 0.6 fusion.71
  55.8 1.2 collective-permute-done
  56.9 1.8 %collective-permute-done.1 = f32[32,7,160]{2,0,1:T(8,128)S(1)} collective-permute-done((f32[32,7,160]{2,0,1:T(8,128)S(1)}, f32[32,7,160]{2,0,1:T(8,128)S(1)}, u32[]{:S(2)}, u32[]{:S(2)}) %collective-permute-start.1) | collective-permute-done | bytes 143392 | tf_op jit(solution)/shard_map/ppermute | solution.py:35
  58.9 1.0 select_divide_fusion.4
  59.9 0.4 select_divide_fusion.3
  60.2 0.4 select_divide_fusion.2
  60.6 1.0 select_divide_fusion.1
  61.7 0.4 select_divide_fusion
  62.0 0.3 pad_slice_fusion.13
  62.4 0.2 fusion.38
  62.8 0.1 slice-done
  63.0 0.1 slice_multiply_fusion
  63.1 0.2 copy.58
  63.3 0.1 reshape.168
  63.6 0.2 reshape.169
  63.9 0.2 reshape.170
  64.2 20.9 %all_to_all.21 = f32[16,53,128]{2,1,0:T(8,128)S(1)} all-to-all(f32[16,53,128]{2,1,0:T(8,128)S(1)} %pad_maximum_fusion.1), channel_id=1, replica_groups=mesh['axial'=16,'azim'=16] {'azim'}, dimensions={0} | all-to-all | bytes 868352 | tf_op jit(solution)/shard_map/all_to_all | solution.py:131
  85.1 0.4 reshape.172
  85.5 0.6 fusion.9
  86.2 0.1 copy.61
  86.3 0.2 reshape.174
  86.6 0.1 copy.60
  86.7 0.8 pad_maximum_fusion.2
  87.5 3.7 %all-to-all-start.3 = ((f32[16,53,128]{2,1,0:T(8,128)}), f32[16,53,128]{2,1,0:T(8,128)S(1)}, u32[]{:S(2)}, u32[]{:S(2)}) async-start(f32[16,53,128]{2,1,0:T(8,128)} %pad_maximum_fusion.2), calls=%async_computation.3 | async-start | bytes 917504 | tf_op jit(solution)/shard_map/all_to_all | solution.py:153
  91.3 0.1 select_reduce_fusion
  91.7 1.9 %select_maximum_fusion = f32[32,128,128]{2,1,0:T(8,128)S(1)} fusion(f32[32,64,64]{2,1,0:T(8,128)} %param.15), kind=kLoop, calls=%fused_computation | loop fusion | flops 2621440 | bytes 2621440 | tf_op jit(solution)/shard_map/concatenate | solution.py:264
  93.7 13.6 %all-to-all-done.3 = f32[16,53,128]{2,1,0:T(8,128)S(1)} async-done(((f32[16,53,128]{2,1,0:T(8,128)}), f32[16,53,128]{2,1,0:T(8,128)S(1)}, u32[]{:S(2)}, u32[]{:S(2)}) %all-to-all-start.3) | async-done | bytes 434208 | tf_op jit(solution)/shard_map/all_to_all | solution.py:153
  107.3 0.4 reshape.175
  107.7 0.2 copy.63
  107.9 0.1 reshape.176
  108.2 0.2 reshape.177
  108.4 1.0 fusion.67
  109.4 1.0 slice_bitcast_fusion.2
  110.4 1.0 fusion.57
  111.4 0.2 pad_slice_fusion.27
  111.6 1.0 pad_slice_fusion.25
  112.7 2.1 %fusion.55 = (f32[32,16,64]{2,0,1:T(8,128)S(1)}, f32[32,16,64]{2,0,1:T(8,128)S(1)}, f32[32,16,64]{2,0,1:T(8,128)S(1)}, f32[32,16,64]{2,0,1:T(8,128)S(1)}) fusion(f32[32,16,66]{2,0,1:T(8,128)S(1)} %get-tuple-element.48, f32[32,16,66]{2,0,1:T(8,128)S(1)} %get-tuple-element.47, f32[32,16,66]{2,0,1:T(8,128)S(1)} %get-tuple-element.46, ...), kind=kLoop, calls=%fused_computation.106 | loop fusion | flops 589824 | bytes 2654720 | tf_op jit(solution)/shard_map/mul | solution.py:167
  114.8 0.1 maximum_bitcast_fusion
  115.0 0.1 maximum_bitcast_fusion.1
  115.1 0.4 fusion.13
  115.5 2.9 %broadcast_select_fusion.1 = (f32[2,32,16,128]{3,2,0,1:T(8,128)}, f32[2,32,16,128]{3,2,0,1:T(8,128)}, f32[2,32,16,128]{3,2,0,1:T(8,128)}) fusion(pred[2,32]{0,1:T(8,128)(4,1)S(1)} %copy.71, pred[2,32]{0,1:T(8,128)(4,1)S(1)} %copy.72, f32[32,128,128]{2,1,0:T(8,128)S(1)} %select_maximum_fusion, f32[2,32,16,128]{3,1,2,0:T(8,128)S(1)} %fusion.13), kind=kOutput, calls=%fused_computation.121 | convolution fusion | flops 100925440 | bytes 4194432 | tf_op jit(solution)/shard_map/apr,sazr->sazp/dot_general | solution.py:272
  118.4 2.0 %collective-permute-start.2 = (f32[2,32,16,128]{3,2,0,1:T(8,128)}, f32[2,32,16,128]{3,2,0,1:T(8,128)S(1)}, u32[]{:S(2)}, u32[]{:S(2)}) collective-permute-start(f32[2,32,16,128]{3,2,0,1:T(8,128)} %get-tuple-element.27), channel_id=1, source_target_pairs={{0,16},{16,32},{32,48},{48,64},{64,80},{80,96},{96,112},{112,128},... | collective-permute-start | bytes 1572872 | tf_op jit(solution)/shard_map/ppermute | solution.py:43
  120.5 5.8 %collective-permute-start.3 = (f32[2,32,16,128]{3,2,0,1:T(8,128)}, f32[2,32,16,128]{3,2,0,1:T(8,128)S(1)}, u32[]{:S(2)}, u32[]{:S(2)}) collective-permute-start(f32[2,32,16,128]{3,2,0,1:T(8,128)} %get-tuple-element.28), channel_id=1, source_target_pairs={{16,0},{32,16},{48,32},{64,48},{80,64},{96,80},{112,96},{128,112},... | collective-permute-start | bytes 1572872 | tf_op jit(solution)/shard_map/ppermute | solution.py:43
  126.3 1.1 subtract_multiply_fusion.1
  127.4 0.9 copy.74
  128.3 3.1 %collective-permute-done.2 = f32[2,32,16,128]{3,2,0,1:T(8,128)S(1)} collective-permute-done((f32[2,32,16,128]{3,2,0,1:T(8,128)}, f32[2,32,16,128]{3,2,0,1:T(8,128)S(1)}, u32[]{:S(2)}, u32[]{:S(2)}) %collective-permute-start.2) | collective-permute-done | bytes 524320 | tf_op jit(solution)/shard_map/ppermute | solution.py:43
  131.4 1.9 %collective-permute-done.3 = f32[2,32,16,128]{3,2,0,1:T(8,128)S(1)} collective-permute-done((f32[2,32,16,128]{3,2,0,1:T(8,128)}, f32[2,32,16,128]{3,2,0,1:T(8,128)S(1)}, u32[]{:S(2)}, u32[]{:S(2)}) %collective-permute-start.3) | collective-permute-done | bytes 524320 | tf_op jit(solution)/shard_map/ppermute | solution.py:43
  133.2 0.2 add_add_fusion
  133.4 1.2 multiply_add_fusion.2
  (64 shorter events, 1.8 us)
Async XLA Ops:
  1.7 26.2 %copy-start = (f32[512,512]{1,0:T(8,128)S(1)}, f32[512,512]{1,0:T(8,128)}, u32[]{:S(2)}) copy-start(f32[512,512]{1,0:T(8,128)} %constant.62.clone) | copy-start | bytes 3145732
  28.7 26.5 %copy-start.8 = (f32[2]{0:T(128)S(1)}, f32[2]{0:T(128)}, u32[]{:S(2)}) copy-start(f32[2]{0:T(128)} %param.13) | copy-start | bytes 28
  29.7 17.6 %all-to-all-start.1 = ((f32[16,40,128]{2,1,0:T(8,128)}), f32[16,40,128]{2,1,0:T(8,128)S(1)}, u32[]{:S(2)}, u32[]{:S(2)}) async-start(f32[16,40,128]{2,1,0:T(8,128)} %pad_maximum_fusion.4), calls=%async_computation.1 | async-start | bytes 655360 | tf_op jit(solution)/shard_map/all_to_all | solution.py:153
  47.5 9.4 %collective-permute-start = (f32[32,7,160]{2,0,1:T(8,128)S(1)}, f32[32,7,160]{2,0,1:T(8,128)S(1)}, u32[]{:S(2)}, u32[]{:S(2)}) collective-permute-start(f32[32,7,160]{2,0,1:T(8,128)S(1)} %get-tuple-element.31), channel_id=1, source_target_pairs={{0,16},{16,32},{32,48},{48,64},{64,80},{80,96},{96,112},{112,128},... | collective-permute-start | bytes 430088 | tf_op jit(solution)/shard_map/ppermute | solution.py:32
  49.4 9.3 %collective-permute-start.1 = (f32[32,7,160]{2,0,1:T(8,128)S(1)}, f32[32,7,160]{2,0,1:T(8,128)S(1)}, u32[]{:S(2)}, u32[]{:S(2)}) collective-permute-start(f32[32,7,160]{2,0,1:T(8,128)S(1)} %get-tuple-element.32), channel_id=1, source_target_pairs={{16,0},{32,16},{48,32},{64,48},{80,64},{96,80},{112,96},{128,112},... | collective-permute-start | bytes 430088 | tf_op jit(solution)/shard_map/ppermute | solution.py:35
  60.6 1.4 %copy-start.1 = (f32[32,30,128]{2,0,1:T(8,128)}, f32[32,30,128]{2,0,1:T(8,128)S(1)}, u32[]{:S(2)}) copy-start(f32[32,30,128]{2,0,1:T(8,128)S(1)} %select_divide_fusion.2) | copy-start | bytes 1474564
  62.0 1.0 slice-start
  86.1 5.2 %copy-start.7 = (s32[2,32,1]{1,2,0:T(1,128)S(1)}, s32[2,32,1]{1,2,0:T(1,128)}, u32[]{:S(2)}) copy-start(s32[2,32,1]{1,2,0:T(1,128)} %param.17) | copy-start | bytes 772
  86.1 5.2 %copy-start.9 = (s32[2,32,1]{1,2,0:T(1,128)S(1)}, s32[2,32,1]{1,2,0:T(1,128)}, u32[]{:S(2)}) copy-start(s32[2,32,1]{1,2,0:T(1,128)} %param.16) | copy-start | bytes 772
  87.5 19.8 %all-to-all-start.3 = ((f32[16,53,128]{2,1,0:T(8,128)}), f32[16,53,128]{2,1,0:T(8,128)S(1)}, u32[]{:S(2)}, u32[]{:S(2)}) async-start(f32[16,53,128]{2,1,0:T(8,128)} %pad_maximum_fusion.2), calls=%async_computation.3 | async-start | bytes 917504 | tf_op jit(solution)/shard_map/all_to_all | solution.py:153
  107.3 0.8 copy-start.3
  108.1 1.4 %copy-start.6 = (f32[32,1344]{1,0:T(8,128)}, f32[32,1344]{1,0:T(8,128)S(1)}, u32[]{:S(2)}) copy-start(f32[32,1344]{1,0:T(8,128)S(1)} %reshape.176) | copy-start | bytes 516100
  109.4 3.2 %slice-start.1 = ((f32[32,1344]{1,0:T(8,128)}), f32[32,132]{1,0:T(8,128)S(1)}, s32[]{:S(2)}) async-start(f32[32,1344]{1,0:T(8,128)} %copy-done.6), calls=%async_computation.5 | async-start | bytes 65536 | tf_op jit(solution)/shard_map/slice | solution.py:241
  115.5 10.8 %copy-start.4 = (f32[32,16,128]{2,1,0:T(8,128)S(1)}, f32[32,16,128]{2,1,0:T(8,128)}, u32[]{:S(2)}) copy-start(f32[32,16,128]{2,1,0:T(8,128)} %param.19) | copy-start | bytes 786436
  115.5 10.8 %copy-start.5 = (f32[32,16,128]{2,1,0:T(8,128)S(1)}, f32[32,16,128]{2,1,0:T(8,128)}, u32[]{:S(2)}) copy-start(f32[32,16,128]{2,1,0:T(8,128)} %param.20) | copy-start | bytes 786436
  118.4 14.8 %copy-start.2 = (f32[2,32,16,128]{3,2,0,1:T(8,128)S(1)}, f32[2,32,16,128]{3,2,0,1:T(8,128)}, u32[]{:S(2)}) copy-start(f32[2,32,16,128]{3,2,0,1:T(8,128)} %get-tuple-element.64) | copy-start | bytes 1572868
  118.4 12.9 %collective-permute-start.2 = (f32[2,32,16,128]{3,2,0,1:T(8,128)}, f32[2,32,16,128]{3,2,0,1:T(8,128)S(1)}, u32[]{:S(2)}, u32[]{:S(2)}) collective-permute-start(f32[2,32,16,128]{3,2,0,1:T(8,128)} %get-tuple-element.27), channel_id=1, source_target_pairs={{0,16},{16,32},{32,48},{48,64},{64,80},{80,96},{96,112},{112,128},... | collective-permute-start | bytes 1572872 | tf_op jit(solution)/shard_map/ppermute | solution.py:43
  120.5 12.8 %collective-permute-start.3 = (f32[2,32,16,128]{3,2,0,1:T(8,128)}, f32[2,32,16,128]{3,2,0,1:T(8,128)S(1)}, u32[]{:S(2)}, u32[]{:S(2)}) collective-permute-start(f32[2,32,16,128]{3,2,0,1:T(8,128)} %get-tuple-element.28), channel_id=1, source_target_pairs={{16,0},{32,16},{48,32},{64,48},{80,64},{96,80},{112,96},{128,112},... | collective-permute-start | bytes 1572872 | tf_op jit(solution)/shard_map/ppermute | solution.py:43
